TPU v7x, 128 devices: a whole 4x4x4 slice. The times are simulated.
128 devices in a mesh: batch: 16 (over z_lo, x, core), patch: 8 (over z_hi, y).
Axes of the slice: x: 4, y: 4, z: 4 (z_hi: 2, z_lo: 2; z = z_hi * 2 + z_lo), core: 2. Of those that a mesh axis runs over, the one named last changes fastest.
Arguments:
- hidden_in: bfloat16 [49152, 1280], P(('batch', 'patch')), parts along dimension 0, may hold values from -45 to 45
- stale_keys: bfloat16 [49152, 1280], P(('batch', 'patch')), parts along dimension 0, may hold values from -150 to 150
- stale_values: bfloat16 [49152, 1280], P(('batch', 'patch')), parts along dimension 0, may hold values from -12 to 12
- stale_moments: float32 [768, 2, 2, 32], P(('batch', 'patch')), parts along dimension 0, may hold values from -5120 to 102400, as said below
- gain_attn: float32 [1280], replicated, may hold values from 0.1 to 1.9
- bias_attn: float32 [1280], replicated, may hold values from -3 to 3
- w_query: bfloat16 [1280, 1280], replicated, may hold values from -0.3125 to 0.3125
- w_key: bfloat16 [1280, 1280], replicated, may hold values from -0.625 to 0.625
- w_value: bfloat16 [1280, 1280], replicated, may hold values from -0.625 to 0.625
- gain_conv: float32 [1280], replicated, may hold values from 0.1 to 1.9
- bias_conv: float32 [1280], replicated, may hold values from -3 to 3
- conv_weight: bfloat16 [3, 3, 1280, 640], replicated, may hold values from -0.0546875 to 0.0546875
- conv_bias: float32 [640], replicated, may hold values from -3 to 3
- w_time: bfloat16 [320, 640], replicated, may hold values from -0.3125 to 0.3125
- timestep: int32 [1], replicated, may hold values from 0 to 999
Outputs:
- conv_out: bfloat16 [49152, 640], P(('batch', 'patch')), parts along dimension 0
There are 16 independent parts, one for each index of `batch`. A program takes and returns all parts, laid end to end along the dimension named above; an argument that names none is the same for every part. Nothing has to cross between parts.
Inputs may be any that keep to these rules, and one draw needn't show every extreme that they name: `stale_moments`: each row's entries are the sums and sums of squares of 2560 values: that count times the second is at least the square of the first.
All inputs are finite; a program needn't handle non-finite values.
Results may differ from a plain program's by a relative error of at most 0.008.
The roundings to bfloat16 on the way count: a program that leaves them out, or rounds other values in their place, can miss the bound.
Values may be sent and summed in bfloat16 or wider, within the bound.
No kernel may reach another device: no remote copies, remote signals or barrier semaphores. Data moves between devices by JAX's collectives and lax.ppermute only.
A program may use at most 320 MiB of HBM per device.

v0:
```python
import functools
import math

import jax
import jax.numpy as jnp
from jax import lax
from jax.sharding import PartitionSpec as P
from jax.experimental import pallas as pl
from jax.experimental.pallas import tpu as pltpu

HEADS = 20
GROUPS = 32
W = 64
YRING = 4


EPS = 1e-05


def padded_2(cells, sides, width):
    for axis, dim in sides:
        count = lax.axis_size(axis)
        ends = count - 1
        head = lax.slice_in_dim(cells, 0, width, axis=dim)
        tail = lax.slice_in_dim(cells, cells.shape[dim] - width, cells.shape[dim], axis=dim)
        cells = jnp.concatenate(
            [
                lax.ppermute(tail, axis, [(i, (i + 1) % count) for i in range(ends)]),
                cells,
                lax.ppermute(head, axis, [((i + 1) % count, i) for i in range(ends)]),
            ],
            axis=dim,
        )
    return cells


def group_moments(rows_in, groups):
    values = rows_in.astype(jnp.float32).reshape(
        rows_in.shape[0], groups, rows_in.shape[1] // groups
    )
    return jnp.stack([jnp.sum(values, axis=(0, 2)), jnp.sum(values * values, axis=(0, 2))])


def group_normalize(rows_in, totals, count, gain, offset, groups):
    average = totals[0] / count
    variance = totals[1] / count - average * average
    inverse = lax.rsqrt(variance + EPS)
    group_width = rows_in.shape[1] // groups
    factors = jnp.repeat(inverse, group_width) * gain
    shifts = offset - jnp.repeat(average * inverse, group_width) * gain
    return rows_in.astype(jnp.float32) * factors + shifts


def time_embedding(timestep, w_time):
    half_dim = w_time.shape[0] // 2
    frequency = jnp.exp(-math.log(10000.0) * jnp.arange(half_dim, dtype=jnp.float32) / half_dim)
    angles = timestep[0].astype(jnp.float32) * frequency
    embedded = jnp.concatenate([jnp.cos(angles), jnp.sin(angles)])
    return jnp.dot(embedded[None, :], w_time.astype(jnp.float32), precision=lax.Precision.HIGHEST)[
        0
    ]


def attn_kernel(*refs, n_pieces):
    q_ref = refs[0]
    piece_refs = refs[1 : 1 + 2 * n_pieces]
    m_ref, l_ref, acc_ref = refs[1 + 2 * n_pieces :]
    head_dim = q_ref.shape[1] // 2
    dims = (((1,), (1,)), ((), ()))
    for hh in range(2):
        lanes = slice(hh * head_dim, (hh + 1) * head_dim)
        qh = q_ref[:, lanes]
        scores = [
            lax.dot_general(
                qh, piece_refs[2 * i][:, lanes], dims, preferred_element_type=jnp.float32
            )
            for i in range(n_pieces)
        ]
        m = functools.reduce(jnp.maximum, [jnp.max(s, axis=1, keepdims=True) for s in scores])
        total = None
        acc = None
        for i in range(n_pieces):
            w = jnp.exp(scores[i] - m)
            part = jnp.sum(w, axis=1, keepdims=True)
            pv = jnp.dot(
                w.astype(jnp.bfloat16),
                piece_refs[2 * i + 1][:, lanes],
                preferred_element_type=jnp.float32,
            )
            total = part if total is None else total + part
            acc = pv if acc is None else acc + pv
        rows = q_ref.shape[0]
        m_ref[:, lanes] = jnp.broadcast_to(m, (rows, head_dim))
        l_ref[:, lanes] = jnp.broadcast_to(total, (rows, head_dim))
        acc_ref[:, lanes] = acc


def attention_partial(query, pieces):
    tok_rows, width = query.shape
    pairs = width // 128
    in_specs = [pl.BlockSpec((tok_rows, 128), lambda h: (0, h))]
    args = [query]
    for keys, kblk, values, vblk in pieces:
        in_specs.append(pl.BlockSpec((keys.shape[0], 128), lambda h, o=kblk: (0, h + o)))
        in_specs.append(pl.BlockSpec((values.shape[0], 128), lambda h, o=vblk: (0, h + o)))
        args += [keys, values]
    out_spec = pl.BlockSpec((tok_rows, 128), lambda h: (0, h))
    out_shape = jax.ShapeDtypeStruct((tok_rows, width), jnp.float32)
    return pl.pallas_call(
        functools.partial(attn_kernel, n_pieces=len(pieces)),
        grid=(pairs,),
        in_specs=in_specs,
        out_specs=[out_spec] * 3,
        out_shape=[out_shape] * 3,
        compiler_params=pltpu.CompilerParams(vmem_limit_bytes=48 * 1024 * 1024),
    )(*args)


def body(
    hidden_in,
    stale_keys,
    stale_values,
    stale_moments,
    gain_attn,
    bias_attn,
    w_query,
    w_key,
    w_value,
    gain_conv,
    bias_conv,
    conv_weight,
    conv_bias,
    w_time,
    timestep,
):
    devices = lax.axis_size("patch")
    tok_rows = hidden_in.shape[0]
    channels = hidden_in.shape[1]
    all_tokens = tok_rows * devices
    count = all_tokens * (channels // GROUPS)
    ring = YRING
    planes = devices // ring
    half = tok_rows // 2
    vblk = channels // 128

    def perm(dy, dz):
        return [
            (z * ring + y, ((z + dz) % planes) * ring + (y + dy) % ring)
            for z in range(planes)
            for y in range(ring)
        ]

    own_stale = jnp.sum(stale_moments, axis=0)
    stale_all = own_stale
    for flip in range(1, ring):
        if flip & (flip - 1) == 0:
            pairs = [
                (z * ring + y, z * ring + (y ^ flip)) for z in range(planes) for y in range(ring)
            ]
            stale_all = stale_all + lax.ppermute(stale_all, "patch", pairs)
    stale_all = stale_all + lax.ppermute(stale_all, "patch", perm(0, 1))
    kv = jnp.concatenate([stale_keys, stale_values], axis=1)
    kv, stale_all = lax.optimization_barrier((kv, stale_all))
    from_left = lax.ppermute(kv, "patch", perm(1, 0))
    from_right = lax.ppermute(kv, "patch", perm(-1, 0))
    partner = lax.ppermute(kv, "patch", perm(0, 1))
    far_a = lax.ppermute(from_left[:half], "patch", perm(1, 0))
    far_b = lax.ppermute(from_right[half:], "patch", perm(-1, 0))
    partner_left = lax.ppermute(partner, "patch", perm(1, 0))
    partner_right = lax.ppermute(partner, "patch", perm(-1, 0))
    partner_far_a = lax.ppermute(partner_left[:half], "patch", perm(1, 0))
    partner_far_b = lax.ppermute(partner_right[half:], "patch", perm(-1, 0))

    total_attn = stale_all[0]
    totals_attn = total_attn - own_stale[0] + group_moments(hidden_in, GROUPS)
    normed = group_normalize(hidden_in, totals_attn, count, gain_attn, bias_attn, GROUPS).astype(
        jnp.bfloat16
    )
    query = jnp.dot(normed, w_query, preferred_element_type=jnp.float32).astype(jnp.bfloat16)
    key_fresh = jnp.dot(normed, w_key, preferred_element_type=jnp.float32).astype(jnp.bfloat16)
    value_fresh = jnp.dot(normed, w_value, preferred_element_type=jnp.float32).astype(jnp.bfloat16)
    query = query * jnp.asarray((channels // HEADS) ** -0.5, jnp.bfloat16)

    sets = [
        [(key_fresh, 0, value_fresh, 0)]
        + [(a, 0, a, vblk) for a in (from_left, from_right, partner)],
        [(a, 0, a, vblk) for a in (far_a, far_b, partner_left, partner_right)],
        [(a, 0, a, vblk) for a in (partner_far_a, partner_far_b)],
    ]
    partials = []
    for pieces in sets:
        partials.append(attention_partial(query, pieces))
    m = functools.reduce(jnp.maximum, [p[0] for p in partials])
    scales = [jnp.exp(p[0] - m) for p in partials]
    acc = sum(p[2] * r for p, r in zip(partials, scales))
    total = sum(p[1] * r for p, r in zip(partials, scales))
    attended = acc / total
    updated = (hidden_in.astype(jnp.float32) + attended).astype(jnp.bfloat16)
    total_conv = stale_all[1]
    totals_conv = total_conv - own_stale[1] + group_moments(updated, GROUPS)
    normed_conv = group_normalize(updated, totals_conv, count, gain_conv, bias_conv, GROUPS)
    activated = jax.nn.silu(normed_conv).astype(jnp.bfloat16).reshape(tok_rows // W, W, channels)
    padded = padded_2(activated, (("patch", 0),), 1)
    convolved = lax.conv_general_dilated(
        padded[None],
        conv_weight,
        (1, 1),
        ((0, 0), (1, 1)),
        dimension_numbers=("NHWC", "HWIO", "NHWC"),
        preferred_element_type=jnp.float32,
    )[0]
    temb = time_embedding(timestep, w_time)
    conv_out = (convolved + conv_bias + temb).astype(jnp.bfloat16)
    return conv_out.reshape(tok_rows, conv_weight.shape[3])


def solution(mesh):
    return jax.shard_map(
        body,
        mesh=mesh,
        in_specs=(
            P(("batch", "patch"), None),
            P(("batch", "patch"), None),
            P(("batch", "patch"), None),
            P(("batch", "patch"), None, None, None),
            P(),
            P(),
            P(),
            P(),
            P(),
            P(),
            P(),
            P(),
            P(),
            P(),
            P(),
        ),
        out_specs=P(("batch", "patch"), None),
        check_vma=False,
    )
```

profile of v0, /device:TPU:24, one launch (start us, length us, event | category | flops | bytes accessed | tf_op | source)
XLA Modules:
  0.0 217.8 jit_solution(1262457884824829709)
XLA Ops:
  0.0 0.9 reduce_sum.54
  0.9 0.8 collective-permute-start
  1.7 2.8 %collective-permute-done = f32[2,2,32]{2,1,0:T(2,128)S(1)} collective-permute-done((f32[2,2,32]{2,1,0:T(2,128)S(1)}, f32[2,2,32]{2,1,0:T(2,128)S(1)}, u32[]{:S(2)}, u32[]{:S(2)}) %collective-permute-start) | collective-permute-done | bytes 544 | tf_op jit(solution)/shard_map/ppermute | solution.py:160
  4.5 1.2 collective-permute-start.1
  5.8 3.9 %collective-permute-done.1 = f32[2,2,32]{2,1,0:T(2,128)S(1)} collective-permute-done((f32[2,2,32]{2,1,0:T(2,128)S(1)}, f32[2,2,32]{2,1,0:T(2,128)S(1)}, u32[]{:S(2)}, u32[]{:S(2)}) %collective-permute-start.1) | collective-permute-done | bytes 544 | tf_op jit(solution)/shard_map/ppermute | solution.py:160
  9.7 4.0 %collective-permute-start.2 = (f32[2,2,32]{2,1,0:T(2,128)S(1)}, f32[2,2,32]{2,1,0:T(2,128)S(1)}, u32[]{:S(2)}, u32[]{:S(2)}) collective-permute-start(f32[2,2,32]{2,1,0:T(2,128)S(1)} %add.75), channel_id=1, source_target_pairs={{0,4},{1,5},{2,6},{3,7},{4,0},{5,1},{6,2},{7,3},{8,12},{9,13},{10,... | collective-permute-start | bytes 1544 | tf_op jit(solution)/shard_map/ppermute | solution.py:161
  13.6 2.9 %pad_maximum_fusion = bf16[384,2560]{1,0:T(8,128)(2,1)} fusion(bf16[384,1280]{1,0:T(8,128)(2,1)} %param.17, bf16[384,1280]{1,0:T(8,128)(2,1)} %param.16), kind=kLoop, calls=%fused_computation.25 | loop fusion | flops 3932160 | bytes 3932160 | tf_op jit(solution)/shard_map/concatenate | solution.py:162
  16.5 2.2 collective-permute-start.5
  18.7 0.7 collective-permute-start.4
  19.4 2.5 %collective-permute-start.3 = (bf16[384,2560]{1,0:T(8,128)(2,1)}, bf16[384,2560]{1,0:T(8,128)(2,1)}, u32[]{:S(2)}, u32[]{:S(2)}) collective-permute-start(bf16[384,2560]{1,0:T(8,128)(2,1)} %pad_maximum_fusion), channel_id=1, source_target_pairs={{0,1},{1,2},{2,3},{3,0},{4,5},{5,6},{6,7},{7,4},{8,9},{9,10},{10,1... | collective-permute-start | bytes 5898248 | tf_op jit(solution)/shard_map/ppermute | solution.py:164
  21.9 38.4 %collective-permute-done.5.refs_7_.refs_8_ = bf16[384,2560]{1,0:T(8,128)(2,1)} collective-permute-done((bf16[384,2560]{1,0:T(8,128)(2,1)}, bf16[384,2560]{1,0:T(8,128)(2,1)}, u32[]{:S(2)}, u32[]{:S(2)}) %collective-permute-start.5) | collective-permute-done | bytes 1966112 | tf_op jit(solution)/shard_map/ppermute | solution.py:166
  60.3 0.7 collective-permute-start.9
  61.1 2.5 %collective-permute-start.8 = (bf16[384,2560]{1,0:T(8,128)(2,1)}, bf16[384,2560]{1,0:T(8,128)(2,1)}, u32[]{:S(2)}, u32[]{:S(2)}) collective-permute-start(bf16[384,2560]{1,0:T(8,128)(2,1)} %collective-permute-done.5.refs_7_.refs_8_), channel_id=1, source_target_pairs={{0,1},{1,2},{2,3},{3,0},{4,5},{5,6},{6,7},{7,4},{8,9},{9,10},{10,1... | collective-permute-start | bytes 5898248 | tf_op jit(solution)/shard_map/ppermute | solution.py:169
  64.2 0.3 convert_reduce_fusion
  64.5 0.1 reduce_sum.59
  64.6 0.1 reduce_sum.60
  64.7 0.1 reduce_sum.62
  64.8 0.1 reduce_sum.66
  65.1 0.1 reshape.47
  65.3 0.1 reshape.46
  65.4 1.3 slice.68
  66.8 1.3 slice.67
  68.0 3.3 %collective-permute-start.6 = (bf16[192,2560]{1,0:T(8,128)(2,1)S(1)}, bf16[192,2560]{1,0:T(8,128)(2,1)S(1)}, u32[]{:S(2)}, u32[]{:S(2)}) collective-permute-start(bf16[192,2560]{1,0:T(8,128)(2,1)S(1)} %slice.67), channel_id=1, source_target_pairs={{0,1},{1,2},{2,3},{3,0},{4,5},{5,6},{6,7},{7,4},{8,9},{9,10},{10,1... | collective-permute-start | bytes 2949128 | tf_op jit(solution)/shard_map/ppermute | solution.py:167
  71.3 36.2 %collective-permute-done.9.refs_7_.refs_8_ = bf16[384,2560]{1,0:T(8,128)(2,1)} collective-permute-done((bf16[384,2560]{1,0:T(8,128)(2,1)}, bf16[384,2560]{1,0:T(8,128)(2,1)}, u32[]{:S(2)}, u32[]{:S(2)}) %collective-permute-start.9) | collective-permute-done | bytes 1966112 | tf_op jit(solution)/shard_map/ppermute | solution.py:170
  107.6 1.3 slice.70
  108.9 2.2 %slice.69 = bf16[192,2560]{1,0:T(8,128)(2,1)} slice(bf16[384,2560]{1,0:T(8,128)(2,1)} %collective-permute-done.8.refs_5_.refs_6_), slice={[0:192], [0:2560]} | slice | bytes 1966080 | tf_op jit(solution)/shard_map/slice | solution.py:171
  111.1 3.2 %collective-permute-start.10 = (bf16[192,2560]{1,0:T(8,128)(2,1)}, bf16[192,2560]{1,0:T(8,128)(2,1)S(1)}, u32[]{:S(2)}, u32[]{:S(2)}) collective-permute-start(bf16[192,2560]{1,0:T(8,128)(2,1)} %slice.69), channel_id=1, source_target_pairs={{0,1},{1,2},{2,3},{3,0},{4,5},{5,6},{6,7},{7,4},{8,9},{9,10},{10,1... | collective-permute-start | bytes 2949128 | tf_op jit(solution)/shard_map/ppermute | solution.py:171
  114.4 1.5 fusion.1.refs_0_
  115.8 0.5 copy-done.12
  116.3 1.5 convolution_convert_fusion.1.refs_1_
  117.8 0.4 copy-done.13
  118.2 1.4 convolution_convert_fusion.refs_2_
  119.7 23.6 %shard_map.145 = (f32[384,1280]{1,0:T(8,128)S(1)}, f32[384,1280]{1,0:T(8,128)}, f32[384,1280]{1,0:T(8,128)}) custom-call(bf16[384,1280]{1,0:T(8,128)(2,1)S(1)} %fusion.1.refs_0_, bf16[384,1280]{1,0:T(8,128)(2,1)S(1)} %convolution_convert_fusion.1.refs_1_, bf16[384,1280]{1,0:T(8,128)(2,1)S(1)} %convolution_convert_fusion.refs_2_, ...), custom_call_target="tpu_custom_call" | custom-call | tf_op jit(solution)/shard_map/pallas_call | solution.py:109
  143.3 21.3 %shard_map.146 = (f32[384,1280]{1,0:T(8,128)S(1)}, f32[384,1280]{1,0:T(8,128)}, f32[384,1280]{1,0:T(8,128)}) custom-call(bf16[384,1280]{1,0:T(8,128)(2,1)S(1)} %fusion.1.refs_0_, bf16[192,2560]{1,0:T(8,128)(2,1)S(1)} %collective-permute-done.6.refs_1_.refs_2_, bf16[192,2560]{1,0:T(8,128)(2,1)S(1)} %collective-permute-done.6.refs_1_.refs_2_, ...), custom_call_target="tpu_custom_call" | custom-call | tf_op jit(solution)/shard_map/pallas_call | solution.py:109
  164.6 13.8 %shard_map.147 = (f32[384,1280]{1,0:T(8,128)S(1)}, f32[384,1280]{1,0:T(8,128)}, f32[384,1280]{1,0:T(8,128)}) custom-call(bf16[384,1280]{1,0:T(8,128)(2,1)S(1)} %fusion.1.refs_0_, bf16[192,2560]{1,0:T(8,128)(2,1)S(1)} %collective-permute-done.10.refs_1_.refs_2_, bf16[192,2560]{1,0:T(8,128)(2,1)S(1)} %collective-permute-done.10.refs_1_.refs_2_, ...), custom_call_target="tpu_custom_call" | custom-call | tf_op jit(solution)/shard_map/pallas_call | solution.py:109
  178.4 4.3 %convert_reduce_fusion.1 = (f32[1280]{0:T(1024)S(1)}, f32[1280]{0:T(1024)S(1)}, bf16[384,1280]{1,0:T(8,128)(2,1)S(1)}) fusion(f32[384,1280]{1,0:T(8,128)} %get-tuple-element.26, f32[384,1280]{1,0:T(8,128)} %get-tuple-element.25, f32[384,1280]{1,0:T(8,128)S(1)} %copy-done.4, f32[384,1280]{1,0:T(8,128)} %get-tuple-element.23, ...), kind=kLoop, calls=%fused_computation.8 | loop fusion | flops 11302400 | bytes 19671040 | tf_op jit(solution)/shard_map/reduce_sum | solution.py:41
  182.7 0.1 reduce_sum.81
  182.8 0.1 reduce_sum.82
  182.9 0.1 reduce_sum.84
  183.0 0.1 reduce_sum.85
  183.2 0.1 reshape.49
  183.4 0.1 reshape.48
  183.5 0.6 fusion.9
  184.1 2.7 %collective-permute-start.12 = (bf16[1,64,1280]{2,1,0:T(8,128)(2,1)S(1)}, bf16[1,64,1280]{2,1,0:T(8,128)(2,1)S(1)}, u32[]{:S(2)}, u32[]{:S(2)}) collective-permute-start(bf16[1,64,1280]{2,1,0:T(8,128)(2,1)S(1)} %get-tuple-element.36), channel_id=1, source_target_pairs={{0,1},{1,2},{2,3},{3,4},{4,5},{5,6},{6,7},{8,9},{9,10},{10,11},{11... | collective-permute-start | bytes 491528 | tf_op jit(solution)/shard_map/ppermute | solution.py:28
  186.8 3.4 %collective-permute-start.13 = (bf16[1,64,1280]{2,1,0:T(8,128)(2,1)S(1)}, bf16[1,64,1280]{2,1,0:T(8,128)(2,1)S(1)}, u32[]{:S(2)}, u32[]{:S(2)}) collective-permute-start(bf16[1,64,1280]{2,1,0:T(8,128)(2,1)S(1)} %get-tuple-element.37), channel_id=1, source_target_pairs={{1,0},{2,1},{3,2},{4,3},{5,4},{6,5},{7,6},{9,8},{10,9},{11,10},{12... | collective-permute-start | bytes 491528 | tf_op jit(solution)/shard_map/ppermute | solution.py:30
  190.2 0.1 pad_maximum_fusion.1
  190.3 0.3 convolution_reduce_fusion
  190.6 0.6 copy.30
  191.1 0.2 collective-permute-done.12
  191.3 0.3 copy.29
  191.6 6.0 %collective-permute-done.13 = bf16[1,64,1280]{2,1,0:T(8,128)(2,1)S(1)} collective-permute-done((bf16[1,64,1280]{2,1,0:T(8,128)(2,1)S(1)}, bf16[1,64,1280]{2,1,0:T(8,128)(2,1)S(1)}, u32[]{:S(2)}, u32[]{:S(2)}) %collective-permute-start.13) | collective-permute-done | bytes 163872 | tf_op jit(solution)/shard_map/ppermute | solution.py:30
  197.6 0.3 copy.31
  197.9 1.1 maximum_bitcast_fusion
  198.9 0.1 pad
  199.1 0.2 copy.33
  199.3 0.1 slice.74
  199.4 0.3 copy-done.14
  199.7 15.7 %fusion.21 = f32[6,8,9,640]{3,1,2,0:T(8,128)S(1)} fusion(bf16[3,3,1280,640]{3,2,1,0:T(8,128)(2,1)} %param.26, bf16[8,1,7,2,1280]{4,2,3,0,1:T(8,128)(2,1)S(1)} %slice.74, bf16[8,1,8,9,1280]{4,2,3,0,1:T(8,128)(2,1)S(1)} %copy.33, pred[8,9]{0,1:T(8,128)(4,1)S(1)} %copy-done.14), kind=kOutput, calls=%fused_computation.32 | convolution fusion | flops 6375782400 | bytes 17612872 | tf_op jit(solution)/shard_map/conv_general_dilated | solution.py:204
  215.4 0.3 copy.34
  215.7 0.1 slice.75
  215.8 0.2 copy.35
  216.0 0.4 copy-done.11
  216.4 0.9 fusion.25
  217.2 0.6 copy-done.1
  (51 shorter events, 0.7 us)
Async XLA Ops:
  0.0 114.4 %copy-start = (bf16[1280,1280]{1,0:T(8,128)(2,1)S(1)}, bf16[1280,1280]{1,0:T(8,128)(2,1)}, u32[]{:S(2)}) copy-start(bf16[1280,1280]{1,0:T(8,128)(2,1)} %param.21) | copy-start | bytes 9830404
  0.9 3.7 %collective-permute-start = (f32[2,2,32]{2,1,0:T(2,128)S(1)}, f32[2,2,32]{2,1,0:T(2,128)S(1)}, u32[]{:S(2)}, u32[]{:S(2)}) collective-permute-start(f32[2,2,32]{2,1,0:T(2,128)S(1)} %reduce_sum.54), channel_id=1, source_target_pairs={{0,1},{1,0},{2,3},{3,2},{4,5},{5,4},{6,7},{7,6},{8,9},{9,8},{10,11... | collective-permute-start | bytes 1544 | tf_op jit(solution)/shard_map/ppermute | solution.py:160
  4.5 5.1 %collective-permute-start.1 = (f32[2,2,32]{2,1,0:T(2,128)S(1)}, f32[2,2,32]{2,1,0:T(2,128)S(1)}, u32[]{:S(2)}, u32[]{:S(2)}) collective-permute-start(f32[2,2,32]{2,1,0:T(2,128)S(1)} %add.74), channel_id=1, source_target_pairs={{0,2},{1,3},{2,0},{3,1},{4,6},{5,7},{6,4},{7,5},{8,10},{9,11},{10,... | collective-permute-start | bytes 1544 | tf_op jit(solution)/shard_map/ppermute | solution.py:160
  9.6 54.6 %copy-start.2 = (bf16[384,1280]{1,0:T(8,128)(2,1)S(1)}, bf16[384,1280]{1,0:T(8,128)(2,1)}, u32[]{:S(2)}) copy-start(bf16[384,1280]{1,0:T(8,128)(2,1)} %param.15) | copy-start | bytes 2949124
  9.6 55.7 %copy-start.7 = (f32[1280]{0:T(1024)S(1)}, f32[1280]{0:T(1024)}, u32[]{:S(2)}) copy-start(f32[1280]{0:T(1024)} %param.19) | copy-start | bytes 15364
  9.6 55.7 %copy-start.8 = (f32[1280]{0:T(1024)S(1)}, f32[1280]{0:T(1024)}, u32[]{:S(2)}) copy-start(f32[1280]{0:T(1024)} %param.20) | copy-start | bytes 15364
  9.7 6.9 %collective-permute-start.2 = (f32[2,2,32]{2,1,0:T(2,128)S(1)}, f32[2,2,32]{2,1,0:T(2,128)S(1)}, u32[]{:S(2)}, u32[]{:S(2)}) collective-permute-start(f32[2,2,32]{2,1,0:T(2,128)S(1)} %add.75), channel_id=1, source_target_pairs={{0,4},{1,5},{2,6},{3,7},{4,0},{5,1},{6,2},{7,3},{8,12},{9,13},{10,... | collective-permute-start | bytes 1544 | tf_op jit(solution)/shard_map/ppermute | solution.py:161
  16.5 43.8 %collective-permute-start.5 = (bf16[384,2560]{1,0:T(8,128)(2,1)}, bf16[384,2560]{1,0:T(8,128)(2,1)}, u32[]{:S(2)}, u32[]{:S(2)}) collective-permute-start(bf16[384,2560]{1,0:T(8,128)(2,1)} %pad_maximum_fusion), channel_id=1, source_target_pairs={{0,4},{1,5},{2,6},{3,7},{4,0},{5,1},{6,2},{7,3},{8,12},{9,13},{10,... | collective-permute-start | bytes 5898248 | tf_op jit(solution)/shard_map/ppermute | solution.py:166
  18.7 46.7 %collective-permute-start.4 = (bf16[384,2560]{1,0:T(8,128)(2,1)}, bf16[384,2560]{1,0:T(8,128)(2,1)}, u32[]{:S(2)}, u32[]{:S(2)}) collective-permute-start(bf16[384,2560]{1,0:T(8,128)(2,1)} %pad_maximum_fusion), channel_id=1, source_target_pairs={{0,3},{1,0},{2,1},{3,2},{4,7},{5,4},{6,5},{7,6},{8,11},{9,8},{10,9... | collective-permute-start | bytes 5898248 | tf_op jit(solution)/shard_map/ppermute | solution.py:165
  19.4 47.3 %collective-permute-start.3 = (bf16[384,2560]{1,0:T(8,128)(2,1)}, bf16[384,2560]{1,0:T(8,128)(2,1)}, u32[]{:S(2)}, u32[]{:S(2)}) collective-permute-start(bf16[384,2560]{1,0:T(8,128)(2,1)} %pad_maximum_fusion), channel_id=1, source_target_pairs={{0,1},{1,2},{2,3},{3,0},{4,5},{5,6},{6,7},{7,4},{8,9},{9,10},{10,1... | collective-permute-start | bytes 5898248 | tf_op jit(solution)/shard_map/ppermute | solution.py:164
  60.3 47.2 %collective-permute-start.9 = (bf16[384,2560]{1,0:T(8,128)(2,1)}, bf16[384,2560]{1,0:T(8,128)(2,1)}, u32[]{:S(2)}, u32[]{:S(2)}) collective-permute-start(bf16[384,2560]{1,0:T(8,128)(2,1)} %collective-permute-done.5.refs_7_.refs_8_), channel_id=1, source_target_pairs={{0,3},{1,0},{2,1},{3,2},{4,7},{5,4},{6,5},{7,6},{8,11},{9,8},{10,9... | collective-permute-start | bytes 5898248 | tf_op jit(solution)/shard_map/ppermute | solution.py:170
  61.1 47.8 %collective-permute-start.8 = (bf16[384,2560]{1,0:T(8,128)(2,1)}, bf16[384,2560]{1,0:T(8,128)(2,1)}, u32[]{:S(2)}, u32[]{:S(2)}) collective-permute-start(bf16[384,2560]{1,0:T(8,128)(2,1)} %collective-permute-done.5.refs_7_.refs_8_), channel_id=1, source_target_pairs={{0,1},{1,2},{2,3},{3,0},{4,5},{5,6},{6,7},{7,4},{8,9},{9,10},{10,1... | collective-permute-start | bytes 5898248 | tf_op jit(solution)/shard_map/ppermute | solution.py:169
  66.7 76.6 %collective-permute-start.7 = (bf16[192,2560]{1,0:T(8,128)(2,1)S(1)}, bf16[192,2560]{1,0:T(8,128)(2,1)S(1)}, u32[]{:S(2)}, u32[]{:S(2)}) collective-permute-start(bf16[192,2560]{1,0:T(8,128)(2,1)S(1)} %slice.68), channel_id=1, source_target_pairs={{0,3},{1,0},{2,1},{3,2},{4,7},{5,4},{6,5},{7,6},{8,11},{9,8},{10,9... | collective-permute-start | bytes 2949128 | tf_op jit(solution)/shard_map/ppermute | solution.py:168
  68.0 46.3 %copy-start.3 = (bf16[384,1280]{1,0:T(8,128)(2,1)S(1)}, bf16[384,1280]{1,0:T(8,128)(2,1)}, u32[]{:S(2)}) copy-start(bf16[384,1280]{1,0:T(8,128)(2,1)} %param.15) | copy-start | bytes 2949124
  68.0 75.2 %collective-permute-start.6 = (bf16[192,2560]{1,0:T(8,128)(2,1)S(1)}, bf16[192,2560]{1,0:T(8,128)(2,1)S(1)}, u32[]{:S(2)}, u32[]{:S(2)}) collective-permute-start(bf16[192,2560]{1,0:T(8,128)(2,1)S(1)} %slice.67), channel_id=1, source_target_pairs={{0,1},{1,2},{2,3},{3,0},{4,5},{5,6},{6,7},{7,4},{8,9},{9,10},{10,1... | collective-permute-start | bytes 2949128 | tf_op jit(solution)/shard_map/ppermute | solution.py:167
  108.8 55.7 %collective-permute-start.11 = (bf16[192,2560]{1,0:T(8,128)(2,1)S(1)}, bf16[192,2560]{1,0:T(8,128)(2,1)S(1)}, u32[]{:S(2)}, u32[]{:S(2)}) collective-permute-start(bf16[192,2560]{1,0:T(8,128)(2,1)S(1)} %slice.70), channel_id=1, source_target_pairs={{0,3},{1,0},{2,1},{3,2},{4,7},{5,4},{6,5},{7,6},{8,11},{9,8},{10,9... | collective-permute-start | bytes 2949128 | tf_op jit(solution)/shard_map/ppermute | solution.py:172
  111.1 53.4 %collective-permute-start.10 = (bf16[192,2560]{1,0:T(8,128)(2,1)}, bf16[192,2560]{1,0:T(8,128)(2,1)S(1)}, u32[]{:S(2)}, u32[]{:S(2)}) collective-permute-start(bf16[192,2560]{1,0:T(8,128)(2,1)} %slice.69), channel_id=1, source_target_pairs={{0,1},{1,2},{2,3},{3,0},{4,5},{5,6},{6,7},{7,4},{8,9},{9,10},{10,1... | collective-permute-start | bytes 2949128 | tf_op jit(solution)/shard_map/ppermute | solution.py:171
  114.4 1.9 copy-start.12
  116.3 1.9 copy-start.13
  164.6 13.8 %copy-start.4 = (f32[384,1280]{1,0:T(8,128)S(1)}, f32[384,1280]{1,0:T(8,128)}, u32[]{:S(2)}) copy-start(f32[384,1280]{1,0:T(8,128)} %get-tuple-element.24) | copy-start | bytes 5898244
  164.6 13.8 %copy-start.5 = (f32[384,1280]{1,0:T(8,128)S(1)}, f32[384,1280]{1,0:T(8,128)}, u32[]{:S(2)}) copy-start(f32[384,1280]{1,0:T(8,128)} %get-tuple-element.18) | copy-start | bytes 5898244
  178.4 5.1 %copy-start.9 = (f32[1280]{0:T(1024)S(1)}, f32[1280]{0:T(1024)}, u32[]{:S(2)}) copy-start(f32[1280]{0:T(1024)} %param.24) | copy-start | bytes 15364
  178.4 5.1 %copy-start.10 = (f32[1280]{0:T(1024)S(1)}, f32[1280]{0:T(1024)}, u32[]{:S(2)}) copy-start(f32[1280]{0:T(1024)} %param.25) | copy-start | bytes 15364
  182.7 7.6 %copy-start.6 = (bf16[320,640]{1,0:T(8,128)(2,1)S(1)}, bf16[320,640]{1,0:T(8,128)(2,1)}, u32[]{:S(2)}) copy-start(bf16[320,640]{1,0:T(8,128)(2,1)} %param.28) | copy-start | bytes 1228804
  184.1 7.2 %collective-permute-start.12 = (bf16[1,64,1280]{2,1,0:T(8,128)(2,1)S(1)}, bf16[1,64,1280]{2,1,0:T(8,128)(2,1)S(1)}, u32[]{:S(2)}, u32[]{:S(2)}) collective-permute-start(bf16[1,64,1280]{2,1,0:T(8,128)(2,1)S(1)} %get-tuple-element.36), channel_id=1, source_target_pairs={{0,1},{1,2},{2,3},{3,4},{4,5},{5,6},{6,7},{8,9},{9,10},{10,11},{11... | collective-permute-start | bytes 491528 | tf_op jit(solution)/shard_map/ppermute | solution.py:28
  186.8 10.8 %collective-permute-start.13 = (bf16[1,64,1280]{2,1,0:T(8,128)(2,1)S(1)}, bf16[1,64,1280]{2,1,0:T(8,128)(2,1)S(1)}, u32[]{:S(2)}, u32[]{:S(2)}) collective-permute-start(bf16[1,64,1280]{2,1,0:T(8,128)(2,1)S(1)} %get-tuple-element.37), channel_id=1, source_target_pairs={{1,0},{2,1},{3,2},{4,3},{5,4},{6,5},{7,6},{9,8},{10,9},{11,10},{12... | collective-permute-start | bytes 491528 | tf_op jit(solution)/shard_map/ppermute | solution.py:30
  199.0 0.7 copy-start.14
  215.7 0.7 copy-start.11
  215.7 2.1 copy-start.1
where the time goes:
time: 218 us
  waiting for transfers between devices  87.6 us (40%)
  Pallas kernels  58.6 us (27%)
  starting transfers between devices  27.4 us (13%)
  matrix products  20.3 us (9%)
  other arithmetic  11.6 us (5%)
  local copies, waits for them, and re-layouts  11.3 us (5%)
    pallas_call x3, Pallas kernels, attention_partial(): pl.pallas_call(functools.partial(attn_kernel, n_pieces=len(pieces)), grid...  58.6 us
    ppermute x1, waiting for transfers between devices, body(): partner = lax.ppermute(kv, 'patch', perm(0, 1))  38.4 us
    ppermute x1, waiting for transfers between devices, body(): partner_right = lax.ppermute(partner, 'patch', perm(-1, 0))  36.2 us
    conv_general_dilated x1, matrix products, body(): lax.conv_general_dilated(padded[None], conv_weight, (1, 1), ((0, 0), (1,...  15.7 us
    ppermute x2, waiting for transfers between devices, body(): stale_all = stale_all + lax.ppermute(stale_all, 'patch', pairs)  6.7 us
    ppermute x1, waiting for transfers between devices, padded_2(): lax.ppermute(head, axis, [((i + 1) % count, i) for i in range(ends)])  6.02 us
    reduce_sum x4, other arithmetic, group_moments(): jnp.sum(values, axis=(0, 2))  4.84 us
  transfers between devices with their start and end apart: 14, of which 6 were waited for; matrix products, arithmetic and copies ran while one was open for 7% of the time, Pallas kernels for 21%

commit v1 on v0

--- a/solution.py
+++ b/solution.py
@@ -160,13 +160,12 @@
             stale_all = stale_all + lax.ppermute(stale_all, "patch", pairs)
     stale_all = stale_all + lax.ppermute(stale_all, "patch", perm(0, 1))
     kv = jnp.concatenate([stale_keys, stale_values], axis=1)
-    kv, stale_all = lax.optimization_barrier((kv, stale_all))
     from_left = lax.ppermute(kv, "patch", perm(1, 0))
     from_right = lax.ppermute(kv, "patch", perm(-1, 0))
     partner = lax.ppermute(kv, "patch", perm(0, 1))
     far_a = lax.ppermute(from_left[:half], "patch", perm(1, 0))
     far_b = lax.ppermute(from_right[half:], "patch", perm(-1, 0))
-    partner_left = lax.ppermute(partner, "patch", perm(1, 0))
+    partner_left = lax.ppermute(from_left, "patch", perm(0, 1))
     partner_right = lax.ppermute(partner, "patch", perm(-1, 0))
     partner_far_a = lax.ppermute(partner_left[:half], "patch", perm(1, 0))
     partner_far_b = lax.ppermute(partner_right[half:], "patch", perm(-1, 0))
@@ -181,11 +180,13 @@
     value_fresh = jnp.dot(normed, w_value, preferred_element_type=jnp.float32).astype(jnp.bfloat16)
     query = query * jnp.asarray((channels // HEADS) ** -0.5, jnp.bfloat16)
 
+    far = jnp.concatenate([far_a, far_b], axis=0)
+    partner_far = jnp.concatenate([partner_far_a, partner_far_b], axis=0)
     sets = [
         [(key_fresh, 0, value_fresh, 0)]
         + [(a, 0, a, vblk) for a in (from_left, from_right, partner)],
-        [(a, 0, a, vblk) for a in (far_a, far_b, partner_left, partner_right)],
-        [(a, 0, a, vblk) for a in (partner_far_a, partner_far_b)],
+        [(a, 0, a, vblk) for a in (far, partner_left, partner_right)],
+        [(partner_far, 0, partner_far, vblk)],
     ]
     partials = []
     for pieces in sets:

time: 218 us -> 220 us (level)
  the two profiles are of different devices: /device:TPU:24 before, /device:TPU:28 now
where the time goes in v1:
time: 220 us; the launch traced here: 219 us
  waiting for transfers between devices  91.3 us (42%)
  Pallas kernels  55.4 us (25%)
  starting transfers between devices  26.9 us (12%)
  matrix products  20.3 us (9%)
  local copies, waits for them, and re-layouts  13.2 us (6%)
  other arithmetic  11.3 us (5%)
    pallas_call x3, Pallas kernels, attention_partial(): pl.pallas_call(functools.partial(attn_kernel, n_pieces=len(pieces)), grid...  55.4 us
    ppermute x1, waiting for transfers between devices, body(): partner = lax.ppermute(kv, 'patch', perm(0, 1))  41.1 us
    ppermute x2, waiting for transfers between devices, body(): stale_all = stale_all + lax.ppermute(stale_all, 'patch', pairs)  40.1 us
    conv_general_dilated x1, matrix products, body(): lax.conv_general_dilated(padded[None], conv_weight, (1, 1), ((0, 0), (1,...  15.6 us
    ppermute x1, waiting for transfers between devices, padded_2(): lax.ppermute(head, axis, [((i + 1) % count, i) for i in range(ends)])  7.46 us
    reduce_sum x4, other arithmetic, group_moments(): jnp.sum(values, axis=(0, 2))  5.53 us
  transfers between devices with their start and end apart: 14, of which 6 were waited for; matrix products, arithmetic and copies ran while one was open for 7% of the time, Pallas kernels for 20%

profile of v1, /device:TPU:28, one launch (start us, length us, event | category | flops | bytes accessed | tf_op | source)
XLA Modules:
  0.0 219.4 jit_solution(1739400323421768055)
XLA Ops:
  0.0 2.4 %constant_dynamic-update-slice_fusion.1 = bf16[384,2560]{1,0:T(8,128)(2,1)} fusion(bf16[384,1280]{1,0:T(8,128)(2,1)} %param.16), kind=kLoop, calls=%fused_computation.45 | loop fusion | bytes 1966080
  2.4 1.1 constant_dynamic-update-slice_fusion
  3.5 3.9 %collective-permute-start.5 = (bf16[384,2560]{1,0:T(8,128)(2,1)}, bf16[384,2560]{1,0:T(8,128)(2,1)}, u32[]{:S(2)}, u32[]{:S(2)}) collective-permute-start(bf16[384,2560]{1,0:T(8,128)(2,1)} %constant_dynamic-update-slice_fusion), channel_id=1, source_target_pairs={{0,4},{1,5},{2,6},{3,7},{4,0},{5,1},{6,2},{7,3},{8,12},{9,13},{10,... | collective-permute-start | bytes 5898248 | tf_op jit(solution)/shard_map/ppermute | solution.py:165
  7.4 0.2 collective-permute-start.3
  7.6 1.8 collective-permute-start.4
  9.4 41.1 %collective-permute-done.5.refs_7_.refs_8_ = bf16[384,2560]{1,0:T(8,128)(2,1)} collective-permute-done((bf16[384,2560]{1,0:T(8,128)(2,1)}, bf16[384,2560]{1,0:T(8,128)(2,1)}, u32[]{:S(2)}, u32[]{:S(2)}) %collective-permute-start.5) | collective-permute-done | bytes 1966112 | tf_op jit(solution)/shard_map/ppermute | solution.py:165
  50.5 0.7 collective-permute-start.9
  51.3 0.7 collective-permute-done.3.refs_3_.refs_4_
  52.0 2.5 %collective-permute-start.8 = (bf16[384,2560]{1,0:T(8,128)(2,1)}, bf16[384,2560]{1,0:T(8,128)(2,1)}, u32[]{:S(2)}, u32[]{:S(2)}) collective-permute-start(bf16[384,2560]{1,0:T(8,128)(2,1)} %collective-permute-done.3.refs_3_.refs_4_), channel_id=1, source_target_pairs={{0,4},{1,5},{2,6},{3,7},{4,0},{5,1},{6,2},{7,3},{8,12},{9,13},{10,... | collective-permute-start | bytes 5898248 | tf_op jit(solution)/shard_map/ppermute | solution.py:168
  54.5 0.5 collective-permute-start
  55.1 38.3 %collective-permute-done = f32[2,2,32]{2,1,0:T(2,128)S(1)} collective-permute-done((f32[2,2,32]{2,1,0:T(2,128)S(1)}, f32[2,2,32]{2,1,0:T(2,128)S(1)}, u32[]{:S(2)}, u32[]{:S(2)}) %collective-permute-start) | collective-permute-done | bytes 544 | tf_op jit(solution)/shard_map/ppermute | solution.py:160
  93.4 1.2 collective-permute-start.1
  94.6 1.5 convert_reduce_fusion
  96.8 1.7 collective-permute-done.1
  98.5 2.7 %collective-permute-start.2 = (f32[2,2,32]{2,1,0:T(2,128)S(1)}, f32[2,2,32]{2,1,0:T(2,128)S(1)}, u32[]{:S(2)}, u32[]{:S(2)}) collective-permute-start(f32[2,2,32]{2,1,0:T(2,128)S(1)} %add.75), channel_id=1, source_target_pairs={{0,4},{1,5},{2,6},{3,7},{4,0},{5,1},{6,2},{7,3},{8,12},{9,13},{10,... | collective-permute-start | bytes 1544 | tf_op jit(solution)/shard_map/ppermute | solution.py:161
  101.2 0.1 reduce_sum.59
  101.3 0.1 reduce_sum.60
  101.4 0.1 reduce_sum.62
  101.5 0.1 reduce_sum.66
  101.7 1.9 collective-permute-done.2
  103.7 0.1 reshape.47
  103.9 0.1 reshape.46
  104.0 1.3 slice.69
  105.4 2.5 %collective-permute-start.7 = (bf16[192,2560]{1,0:T(8,128)(2,1)S(1)}, bf16[192,2560]{1,0:T(8,128)(2,1)S(1)}, u32[]{:S(2)}, u32[]{:S(2)}) collective-permute-start(bf16[192,2560]{1,0:T(8,128)(2,1)S(1)} %slice.69), channel_id=1, source_target_pairs={{0,3},{1,0},{2,1},{3,2},{4,7},{5,4},{6,5},{7,6},{8,11},{9,8},{10,9... | collective-permute-start | bytes 2949128 | tf_op jit(solution)/shard_map/ppermute | solution.py:167
  107.9 1.3 slice.68
  109.2 0.8 collective-permute-start.6
  110.0 1.4 fusion.1.refs_0_
  111.5 1.4 slice.71
  112.9 1.3 collective-permute-start.11
  114.2 1.3 slice.70
  115.5 2.2 %collective-permute-start.10 = (bf16[192,2560]{1,0:T(8,128)(2,1)S(1)}, bf16[192,2560]{1,0:T(8,128)(2,1)S(1)}, u32[]{:S(2)}, u32[]{:S(2)}) collective-permute-start(bf16[192,2560]{1,0:T(8,128)(2,1)S(1)} %slice.70), channel_id=1, source_target_pairs={{0,1},{1,2},{2,3},{3,0},{4,5},{5,6},{6,7},{7,4},{8,9},{9,10},{10,1... | collective-permute-start | bytes 2949128 | tf_op jit(solution)/shard_map/ppermute | solution.py:170
  117.7 1.5 convolution_convert_fusion.1.refs_1_
  119.2 1.5 convolution_convert_fusion.refs_2_
  120.7 23.6 %shard_map.145 = (f32[384,1280]{1,0:T(8,128)S(1)}, f32[384,1280]{1,0:T(8,128)}, f32[384,1280]{1,0:T(8,128)}) custom-call(bf16[384,1280]{1,0:T(8,128)(2,1)S(1)} %fusion.1.refs_0_, bf16[384,1280]{1,0:T(8,128)(2,1)S(1)} %convolution_convert_fusion.1.refs_1_, bf16[384,1280]{1,0:T(8,128)(2,1)S(1)} %convolution_convert_fusion.refs_2_, ...), custom_call_target="tpu_custom_call" | custom-call | tf_op jit(solution)/shard_map/pallas_call | solution.py:109
  144.4 1.4 pad_maximum_fusion.refs_1_.refs_2_
  145.8 19.6 %shard_map.146 = (f32[384,1280]{1,0:T(8,128)S(1)}, f32[384,1280]{1,0:T(8,128)S(1)}, f32[384,1280]{1,0:T(8,128)}) custom-call(bf16[384,1280]{1,0:T(8,128)(2,1)S(1)} %fusion.1.refs_0_, bf16[384,2560]{1,0:T(8,128)(2,1)} %pad_maximum_fusion.refs_1_.refs_2_, bf16[384,2560]{1,0:T(8,128)(2,1)} %pad_maximum_fusion.refs_1_.refs_2_, ...), custom_call_target="tpu_custom_call" | custom-call | tf_op jit(solution)/shard_map/pallas_call | solution.py:109
  165.4 1.4 pad_maximum_fusion.1.refs_1_.refs_2_
  166.8 12.2 %shard_map.147 = (f32[384,1280]{1,0:T(8,128)S(1)}, f32[384,1280]{1,0:T(8,128)S(1)}, f32[384,1280]{1,0:T(8,128)}) custom-call(bf16[384,1280]{1,0:T(8,128)(2,1)S(1)} %fusion.1.refs_0_, bf16[384,2560]{1,0:T(8,128)(2,1)} %pad_maximum_fusion.1.refs_1_.refs_2_, bf16[384,2560]{1,0:T(8,128)(2,1)} %pad_maximum_fusion.1.refs_1_.refs_2_), custom_call_target="tpu_custom_call" | custom-call | tf_op jit(solution)/shard_map/pallas_call | solution.py:109
  179.0 3.8 %convert_reduce_fusion.1 = (f32[1280]{0:T(1024)S(1)}, f32[1280]{0:T(1024)S(1)}, bf16[384,1280]{1,0:T(8,128)(2,1)S(1)}) fusion(f32[384,1280]{1,0:T(8,128)S(1)} %get-tuple-element.22, f32[384,1280]{1,0:T(8,128)S(1)} %get-tuple-element.21, f32[384,1280]{1,0:T(8,128)S(1)} %copy-done.3, f32[384,1280]{1,0:T(8,128)} %get-tuple-element.19, ...), kind=kLoop, calls=%fused_computation.8 | loop fusion | flops 11302400 | bytes 19671040 | tf_op jit(solution)/shard_map/reduce_sum | solution.py:41
  182.8 0.1 reduce_sum.81
  182.9 0.1 reduce_sum.82
  183.0 0.1 reduce_sum.84
  183.1 0.1 reduce_sum.85
  183.3 0.1 reshape.49
  183.5 0.1 reshape.48
  183.6 0.6 fusion.9
  184.2 4.2 %collective-permute-start.12 = (bf16[1,64,1280]{2,1,0:T(8,128)(2,1)S(1)}, bf16[1,64,1280]{2,1,0:T(8,128)(2,1)S(1)}, u32[]{:S(2)}, u32[]{:S(2)}) collective-permute-start(bf16[1,64,1280]{2,1,0:T(8,128)(2,1)S(1)} %get-tuple-element.32), channel_id=1, source_target_pairs={{0,1},{1,2},{2,3},{3,4},{4,5},{5,6},{6,7},{8,9},{9,10},{10,11},{11... | collective-permute-start | bytes 491528 | tf_op jit(solution)/shard_map/ppermute | solution.py:28
  188.4 2.1 collective-permute-start.13
  190.7 0.3 convolution_reduce_fusion
  191.0 0.6 copy.30
  191.5 0.3 copy.29
  191.8 7.5 %collective-permute-done.13 = bf16[1,64,1280]{2,1,0:T(8,128)(2,1)S(1)} collective-permute-done((bf16[1,64,1280]{2,1,0:T(8,128)(2,1)S(1)}, bf16[1,64,1280]{2,1,0:T(8,128)(2,1)S(1)}, u32[]{:S(2)}, u32[]{:S(2)}) %collective-permute-start.13) | collective-permute-done | bytes 163872 | tf_op jit(solution)/shard_map/ppermute | solution.py:30
  199.3 0.3 copy.31
  199.5 1.1 maximum_bitcast_fusion
  200.6 0.1 pad
  200.7 0.2 copy.33
  201.0 0.3 copy-done.14
  201.4 15.6 %fusion.21 = f32[6,8,9,640]{3,1,2,0:T(8,128)S(1)} fusion(bf16[3,3,1280,640]{3,2,1,0:T(8,128)(2,1)} %param.26, bf16[8,1,7,2,1280]{4,2,3,0,1:T(8,128)(2,1)S(1)} %slice.76, bf16[8,1,8,9,1280]{4,2,3,0,1:T(8,128)(2,1)S(1)} %copy.33, pred[8,9]{0,1:T(8,128)(4,1)S(1)} %copy-done.14), kind=kOutput, calls=%fused_computation.33 | convolution fusion | flops 6375782400 | bytes 17612872 | tf_op jit(solution)/shard_map/conv_general_dilated | solution.py:205
  217.0 0.3 copy.34
  217.3 0.1 slice.77
  217.4 0.2 copy.35
  217.6 0.4 copy-done.11
  218.0 0.9 fusion.25
  218.8 0.6 copy-done.1
  (54 shorter events, 0.7 us)
Async XLA Ops:
  0.0 110.0 %copy-start = (bf16[1280,1280]{1,0:T(8,128)(2,1)S(1)}, bf16[1280,1280]{1,0:T(8,128)(2,1)}, u32[]{:S(2)}) copy-start(bf16[1280,1280]{1,0:T(8,128)(2,1)} %param.21) | copy-start | bytes 9830404
  0.0 2.4 %copy-start.4 = (bf16[384,1280]{1,0:T(8,128)(2,1)S(1)}, bf16[384,1280]{1,0:T(8,128)(2,1)}, u32[]{:S(2)}) copy-start(bf16[384,1280]{1,0:T(8,128)(2,1)} %param.17) | copy-start | bytes 2949124
  0.0 54.5 %copy-start.6 = (f32[6,2,2,32]{3,2,1,0:T(2,128)S(1)}, f32[6,2,2,32]{3,2,1,0:T(2,128)}, u32[]{:S(2)}) copy-start(f32[6,2,2,32]{3,2,1,0:T(2,128)} %param.18) | copy-start | bytes 9220
  2.4 101.5 %copy-start.7 = (f32[1280]{0:T(1024)S(1)}, f32[1280]{0:T(1024)}, u32[]{:S(2)}) copy-start(f32[1280]{0:T(1024)} %param.19) | copy-start | bytes 15364
  2.4 101.5 %copy-start.8 = (f32[1280]{0:T(1024)S(1)}, f32[1280]{0:T(1024)}, u32[]{:S(2)}) copy-start(f32[1280]{0:T(1024)} %param.20) | copy-start | bytes 15364
  3.5 47.0 %collective-permute-start.5 = (bf16[384,2560]{1,0:T(8,128)(2,1)}, bf16[384,2560]{1,0:T(8,128)(2,1)}, u32[]{:S(2)}, u32[]{:S(2)}) collective-permute-start(bf16[384,2560]{1,0:T(8,128)(2,1)} %constant_dynamic-update-slice_fusion), channel_id=1, source_target_pairs={{0,4},{1,5},{2,6},{3,7},{4,0},{5,1},{6,2},{7,3},{8,12},{9,13},{10,... | collective-permute-start | bytes 5898248 | tf_op jit(solution)/shard_map/ppermute | solution.py:165
  7.4 44.6 %collective-permute-start.3 = (bf16[384,2560]{1,0:T(8,128)(2,1)}, bf16[384,2560]{1,0:T(8,128)(2,1)}, u32[]{:S(2)}, u32[]{:S(2)}) collective-permute-start(bf16[384,2560]{1,0:T(8,128)(2,1)} %constant_dynamic-update-slice_fusion), channel_id=1, source_target_pairs={{0,1},{1,2},{2,3},{3,0},{4,5},{5,6},{6,7},{7,4},{8,9},{9,10},{10,1... | collective-permute-start | bytes 5898248 | tf_op jit(solution)/shard_map/ppermute | solution.py:163
  7.6 96.4 %collective-permute-start.4 = (bf16[384,2560]{1,0:T(8,128)(2,1)}, bf16[384,2560]{1,0:T(8,128)(2,1)}, u32[]{:S(2)}, u32[]{:S(2)}) collective-permute-start(bf16[384,2560]{1,0:T(8,128)(2,1)} %constant_dynamic-update-slice_fusion), channel_id=1, source_target_pairs={{0,3},{1,0},{2,1},{3,2},{4,7},{5,4},{6,5},{7,6},{8,11},{9,8},{10,9... | collective-permute-start | bytes 5898248 | tf_op jit(solution)/shard_map/ppermute | solution.py:164
  50.5 61.0 %collective-permute-start.9 = (bf16[384,2560]{1,0:T(8,128)(2,1)}, bf16[384,2560]{1,0:T(8,128)(2,1)}, u32[]{:S(2)}, u32[]{:S(2)}) collective-permute-start(bf16[384,2560]{1,0:T(8,128)(2,1)} %collective-permute-done.5.refs_7_.refs_8_), channel_id=1, source_target_pairs={{0,3},{1,0},{2,1},{3,2},{4,7},{5,4},{6,5},{7,6},{8,11},{9,8},{10,9... | collective-permute-start | bytes 5898248 | tf_op jit(solution)/shard_map/ppermute | solution.py:169
  52.0 62.3 %collective-permute-start.8 = (bf16[384,2560]{1,0:T(8,128)(2,1)}, bf16[384,2560]{1,0:T(8,128)(2,1)}, u32[]{:S(2)}, u32[]{:S(2)}) collective-permute-start(bf16[384,2560]{1,0:T(8,128)(2,1)} %collective-permute-done.3.refs_3_.refs_4_), channel_id=1, source_target_pairs={{0,4},{1,5},{2,6},{3,7},{4,0},{5,1},{6,2},{7,3},{8,12},{9,13},{10,... | collective-permute-start | bytes 5898248 | tf_op jit(solution)/shard_map/ppermute | solution.py:168
  54.5 38.9 %collective-permute-start = (f32[2,2,32]{2,1,0:T(2,128)S(1)}, f32[2,2,32]{2,1,0:T(2,128)S(1)}, u32[]{:S(2)}, u32[]{:S(2)}) collective-permute-start(f32[2,2,32]{2,1,0:T(2,128)S(1)} %reduce_sum.54), channel_id=1, source_target_pairs={{0,1},{1,0},{2,3},{3,2},{4,5},{5,4},{6,7},{7,6},{8,9},{9,8},{10,11... | collective-permute-start | bytes 1544 | tf_op jit(solution)/shard_map/ppermute | solution.py:160
  93.4 5.1 %collective-permute-start.1 = (f32[2,2,32]{2,1,0:T(2,128)S(1)}, f32[2,2,32]{2,1,0:T(2,128)S(1)}, u32[]{:S(2)}, u32[]{:S(2)}) collective-permute-start(f32[2,2,32]{2,1,0:T(2,128)S(1)} %add.74), channel_id=1, source_target_pairs={{0,2},{1,3},{2,0},{3,1},{4,6},{5,7},{6,4},{7,5},{8,10},{9,11},{10,... | collective-permute-start | bytes 1544 | tf_op jit(solution)/shard_map/ppermute | solution.py:160
  98.5 5.1 %collective-permute-start.2 = (f32[2,2,32]{2,1,0:T(2,128)S(1)}, f32[2,2,32]{2,1,0:T(2,128)S(1)}, u32[]{:S(2)}, u32[]{:S(2)}) collective-permute-start(f32[2,2,32]{2,1,0:T(2,128)S(1)} %add.75), channel_id=1, source_target_pairs={{0,4},{1,5},{2,6},{3,7},{4,0},{5,1},{6,2},{7,3},{8,12},{9,13},{10,... | collective-permute-start | bytes 1544 | tf_op jit(solution)/shard_map/ppermute | solution.py:161
  104.0 6.0 %copy-start.2 = (bf16[384,1280]{1,0:T(8,128)(2,1)S(1)}, bf16[384,1280]{1,0:T(8,128)(2,1)}, u32[]{:S(2)}) copy-start(bf16[384,1280]{1,0:T(8,128)(2,1)} %param.15) | copy-start | bytes 2949124
  105.4 39.0 %collective-permute-start.7 = (bf16[192,2560]{1,0:T(8,128)(2,1)S(1)}, bf16[192,2560]{1,0:T(8,128)(2,1)S(1)}, u32[]{:S(2)}, u32[]{:S(2)}) collective-permute-start(bf16[192,2560]{1,0:T(8,128)(2,1)S(1)} %slice.69), channel_id=1, source_target_pairs={{0,3},{1,0},{2,1},{3,2},{4,7},{5,4},{6,5},{7,6},{8,11},{9,8},{10,9... | collective-permute-start | bytes 2949128 | tf_op jit(solution)/shard_map/ppermute | solution.py:167
  109.2 35.2 %collective-permute-start.6 = (bf16[192,2560]{1,0:T(8,128)(2,1)S(1)}, bf16[192,2560]{1,0:T(8,128)(2,1)S(1)}, u32[]{:S(2)}, u32[]{:S(2)}) collective-permute-start(bf16[192,2560]{1,0:T(8,128)(2,1)S(1)} %slice.68), channel_id=1, source_target_pairs={{0,1},{1,2},{2,3},{3,0},{4,5},{5,6},{6,7},{7,4},{8,9},{9,10},{10,1... | collective-permute-start | bytes 2949128 | tf_op jit(solution)/shard_map/ppermute | solution.py:166
  111.5 6.3 %copy-start.12 = (bf16[1280,1280]{1,0:T(8,128)(2,1)S(1)}, bf16[1280,1280]{1,0:T(8,128)(2,1)}, u32[]{:S(2)}) copy-start(bf16[1280,1280]{1,0:T(8,128)(2,1)} %param.22) | copy-start | bytes 9830404
  112.9 52.5 %collective-permute-start.11 = (bf16[192,2560]{1,0:T(8,128)(2,1)S(1)}, bf16[192,2560]{1,0:T(8,128)(2,1)S(1)}, u32[]{:S(2)}, u32[]{:S(2)}) collective-permute-start(bf16[192,2560]{1,0:T(8,128)(2,1)S(1)} %slice.71), channel_id=1, source_target_pairs={{0,3},{1,0},{2,1},{3,2},{4,7},{5,4},{6,5},{7,6},{8,11},{9,8},{10,9... | collective-permute-start | bytes 2949128 | tf_op jit(solution)/shard_map/ppermute | solution.py:171
  115.5 3.7 %copy-start.13 = (bf16[1280,1280]{1,0:T(8,128)(2,1)S(1)}, bf16[1280,1280]{1,0:T(8,128)(2,1)}, u32[]{:S(2)}) copy-start(bf16[1280,1280]{1,0:T(8,128)(2,1)} %param.23) | copy-start | bytes 9830404
  115.5 49.8 %collective-permute-start.10 = (bf16[192,2560]{1,0:T(8,128)(2,1)S(1)}, bf16[192,2560]{1,0:T(8,128)(2,1)S(1)}, u32[]{:S(2)}, u32[]{:S(2)}) collective-permute-start(bf16[192,2560]{1,0:T(8,128)(2,1)S(1)} %slice.70), channel_id=1, source_target_pairs={{0,1},{1,2},{2,3},{3,0},{4,5},{5,6},{6,7},{7,4},{8,9},{9,10},{10,1... | collective-permute-start | bytes 2949128 | tf_op jit(solution)/shard_map/ppermute | solution.py:170
  166.8 12.2 %copy-start.3 = (f32[384,1280]{1,0:T(8,128)S(1)}, f32[384,1280]{1,0:T(8,128)}, u32[]{:S(2)}) copy-start(f32[384,1280]{1,0:T(8,128)} %get-tuple-element.20) | copy-start | bytes 5898244
  179.0 4.6 %copy-start.9 = (f32[1280]{0:T(1024)S(1)}, f32[1280]{0:T(1024)}, u32[]{:S(2)}) copy-start(f32[1280]{0:T(1024)} %param.24) | copy-start | bytes 15364
  179.0 4.6 %copy-start.10 = (f32[1280]{0:T(1024)S(1)}, f32[1280]{0:T(1024)}, u32[]{:S(2)}) copy-start(f32[1280]{0:T(1024)} %param.25) | copy-start | bytes 15364
  182.8 7.9 %copy-start.5 = (bf16[320,640]{1,0:T(8,128)(2,1)S(1)}, bf16[320,640]{1,0:T(8,128)(2,1)}, u32[]{:S(2)}) copy-start(bf16[320,640]{1,0:T(8,128)(2,1)} %param.28) | copy-start | bytes 1228804
  184.2 7.3 %collective-permute-start.12 = (bf16[1,64,1280]{2,1,0:T(8,128)(2,1)S(1)}, bf16[1,64,1280]{2,1,0:T(8,128)(2,1)S(1)}, u32[]{:S(2)}, u32[]{:S(2)}) collective-permute-start(bf16[1,64,1280]{2,1,0:T(8,128)(2,1)S(1)} %get-tuple-element.32), channel_id=1, source_target_pairs={{0,1},{1,2},{2,3},{3,4},{4,5},{5,6},{6,7},{8,9},{9,10},{10,11},{11... | collective-permute-start | bytes 491528 | tf_op jit(solution)/shard_map/ppermute | solution.py:28
  188.4 10.8 %collective-permute-start.13 = (bf16[1,64,1280]{2,1,0:T(8,128)(2,1)S(1)}, bf16[1,64,1280]{2,1,0:T(8,128)(2,1)S(1)}, u32[]{:S(2)}, u32[]{:S(2)}) collective-permute-start(bf16[1,64,1280]{2,1,0:T(8,128)(2,1)S(1)} %get-tuple-element.33), channel_id=1, source_target_pairs={{1,0},{2,1},{3,2},{4,3},{5,4},{6,5},{7,6},{9,8},{10,9},{11,10},{12... | collective-permute-start | bytes 491528 | tf_op jit(solution)/shard_map/ppermute | solution.py:30
  200.7 0.7 copy-start.14
  217.3 0.7 copy-start.11
  217.3 2.1 copy-start.1

commit v2 on v1

--- a/solution.py
+++ b/solution.py
@@ -12,6 +12,7 @@
 GROUPS = 32
 W = 64
 YRING = 4
+SC_PAIRS = 4
 
 
 EPS = 1e-05
@@ -141,7 +142,7 @@
     ring = YRING
     planes = devices // ring
     half = tok_rows // 2
-    vblk = channels // 128
+    vblk = channels // 128 - SC_PAIRS
 
     def perm(dy, dz):
         return [
@@ -159,7 +160,10 @@
             ]
             stale_all = stale_all + lax.ppermute(stale_all, "patch", pairs)
     stale_all = stale_all + lax.ppermute(stale_all, "patch", perm(0, 1))
-    kv = jnp.concatenate([stale_keys, stale_values], axis=1)
+    split = SC_PAIRS * 128
+    kv_sc = jnp.concatenate([stale_keys[:, :split], stale_values[:, :split]], axis=1)
+    gathered = lax.all_gather(kv_sc, "patch", axis=0, tiled=True)
+    kv = jnp.concatenate([stale_keys[:, split:], stale_values[:, split:]], axis=1)
     from_left = lax.ppermute(kv, "patch", perm(1, 0))
     from_right = lax.ppermute(kv, "patch", perm(-1, 0))
     partner = lax.ppermute(kv, "patch", perm(0, 1))
@@ -182,20 +186,25 @@
 
     far = jnp.concatenate([far_a, far_b], axis=0)
     partner_far = jnp.concatenate([partner_far_a, partner_far_b], axis=0)
+    query_tc = query[:, split:]
     sets = [
-        [(key_fresh, 0, value_fresh, 0)]
+        [(key_fresh[:, split:], 0, value_fresh[:, split:], 0)]
         + [(a, 0, a, vblk) for a in (from_left, from_right, partner)],
         [(a, 0, a, vblk) for a in (far, partner_left, partner_right)],
         [(partner_far, 0, partner_far, vblk)],
     ]
     partials = []
     for pieces in sets:
-        partials.append(attention_partial(query, pieces))
+        partials.append(attention_partial(query_tc, pieces))
     m = functools.reduce(jnp.maximum, [p[0] for p in partials])
     scales = [jnp.exp(p[0] - m) for p in partials]
     acc = sum(p[2] * r for p, r in zip(partials, scales))
     total = sum(p[1] * r for p, r in zip(partials, scales))
-    attended = acc / total
+    own_first = lax.axis_index("patch") * tok_rows
+    fresh_sc = jnp.concatenate([key_fresh[:, :split], value_fresh[:, :split]], axis=1)
+    keys_sc = lax.dynamic_update_slice_in_dim(gathered, fresh_sc, own_first, 0)
+    _, l_sc, acc_sc = attention_partial(query[:, :split], [(keys_sc, 0, keys_sc, SC_PAIRS)])
+    attended = jnp.concatenate([acc_sc / l_sc, acc / total], axis=1)
     updated = (hidden_in.astype(jnp.float32) + attended).astype(jnp.bfloat16)
     total_conv = stale_all[1]
     totals_conv = total_conv - own_stale[1] + group_moments(updated, GROUPS)

time: 220 us -> 227 us (1.032)
  the two profiles are of different devices: /device:TPU:28 before, /device:TPU:30 now
where the time goes in v2:
time: 227 us
  waiting for transfers between devices  88.8 us (39%)
  Pallas kernels  52.6 us (23%)
  starting transfers between devices  23.1 us (10%)
  matrix products  21.6 us (10%)
  local copies, waits for them, and re-layouts  14.6 us (6%)
  between operations  14.6 us (6%)
  other arithmetic  11.3 us (5%)
    pallas_call x4, Pallas kernels, attention_partial(): pl.pallas_call(functools.partial(attn_kernel, n_pieces=len(pieces)), grid...  52.6 us
    ppermute x2, waiting for transfers between devices, body(): stale_all = stale_all + lax.ppermute(stale_all, 'patch', pairs)  39.2 us
    ppermute x1, waiting for transfers between devices, body(): partner_right = lax.ppermute(partner, 'patch', perm(-1, 0))  22.7 us
    ppermute x1, waiting for transfers between devices, body(): partner_left = lax.ppermute(from_left, 'patch', perm(0, 1))  17 us
    conv_general_dilated x1, matrix products, body(): lax.conv_general_dilated(padded[None], conv_weight, (1, 1), ((0, 0), (1,...  15.6 us
    ppermute x1, waiting for transfers between devices, padded_2(): lax.ppermute(head, axis, [((i + 1) % count, i) for i in range(ends)])  5.3 us
  transfers between devices with their start and end apart: 15, of which 7 were waited for; matrix products, arithmetic and copies ran while one was open for 8% of the time, Pallas kernels for 15%

profile of v2, /device:TPU:30, one launch (start us, length us, event | category | flops | bytes accessed | tf_op | source)
XLA Modules:
  0.0 226.6 jit_solution(197636327720134429)
XLA Ops:
  6.5 2.0 slice-done
  8.5 0.1 slice-done.2
  8.6 1.0 pad_maximum_fusion.3
  9.7 1.0 slice-done.1
  10.7 0.2 slice-done.3
  10.9 1.1 pad_maximum_fusion
  12.0 3.9 %collective-permute-start.5 = (bf16[384,1536]{1,0:T(8,128)(2,1)}, bf16[384,1536]{1,0:T(8,128)(2,1)}, u32[]{:S(2)}, u32[]{:S(2)}) collective-permute-start(bf16[384,1536]{1,0:T(8,128)(2,1)} %pad_maximum_fusion), channel_id=1, source_target_pairs={{0,4},{1,5},{2,6},{3,7},{4,0},{5,1},{6,2},{7,3},{8,12},{9,13},{10,... | collective-permute-start | bytes 3538952 | tf_op jit(solution)/shard_map/ppermute | solution.py:169
  15.9 0.2 collective-permute-start.3
  16.1 1.8 collective-permute-start.4
  17.9 0.8 collective-permute-start
  18.8 1.5 convert_reduce_fusion
  20.9 35.4 %collective-permute-done = f32[2,2,32]{2,1,0:T(2,128)S(1)} collective-permute-done((f32[2,2,32]{2,1,0:T(2,128)S(1)}, f32[2,2,32]{2,1,0:T(2,128)S(1)}, u32[]{:S(2)}, u32[]{:S(2)}) %collective-permute-start) | collective-permute-done | bytes 544 | tf_op jit(solution)/shard_map/ppermute | solution.py:161
  56.3 1.2 collective-permute-start.1
  57.6 3.8 %collective-permute-done.1 = f32[2,2,32]{2,1,0:T(2,128)S(1)} collective-permute-done((f32[2,2,32]{2,1,0:T(2,128)S(1)}, f32[2,2,32]{2,1,0:T(2,128)S(1)}, u32[]{:S(2)}, u32[]{:S(2)}) %collective-permute-start.1) | collective-permute-done | bytes 544 | tf_op jit(solution)/shard_map/ppermute | solution.py:161
  61.4 0.3 collective-permute-start.2
  61.8 0.1 reduce_sum.60
  62.0 0.1 reduce_sum.66
  62.1 4.4 %collective-permute-done.2 = f32[2,2,32]{2,1,0:T(2,128)S(1)} collective-permute-done((f32[2,2,32]{2,1,0:T(2,128)S(1)}, f32[2,2,32]{2,1,0:T(2,128)S(1)}, u32[]{:S(2)}, u32[]{:S(2)}) %collective-permute-start.2) | collective-permute-done | bytes 544 | tf_op jit(solution)/shard_map/ppermute | solution.py:162
  66.5 1.8 collective-permute-start.9
  68.3 0.3 collective-permute-start.8
  69.0 2.8 %convolution_convert_fusion.1 = bf16[384,1280]{1,0:T(8,128)(2,1)S(1)} fusion(bf16[1280,1280]{1,0:T(8,128)(2,1)S(1)} %copy-done, bf16[384,1280]{1,0:T(8,128)(2,1)} %param.15, f32[1280]{0:T(1024)S(1)} %get-tuple-element.41, f32[1280]{0:T(1024)S(1)} %get-tuple-element.40), kind=kOutput, calls=%fused_computation.10 | convolution fusion | flops 1260748800 | bytes 5253120 | tf_op jit(solution)/shard_map/dot_general | solution.py:183
  71.9 1.5 slice.115
  73.3 0.2 collective-permute-start.7
  73.5 1.1 slice.114
  74.6 3.2 %collective-permute-start.6 = (bf16[192,1536]{1,0:T(8,128)(2,1)S(1)}, bf16[192,1536]{1,0:T(8,128)(2,1)S(1)}, u32[]{:S(2)}, u32[]{:S(2)}) collective-permute-start(bf16[192,1536]{1,0:T(8,128)(2,1)S(1)} %slice.114), channel_id=1, source_target_pairs={{0,1},{1,2},{2,3},{3,0},{4,5},{5,6},{6,7},{7,4},{8,9},{9,10},{10,1... | collective-permute-start | bytes 1769480 | tf_op jit(solution)/shard_map/ppermute | solution.py:170
  77.8 1.4 convolution_convert_fusion
  79.3 0.8 slice.110
  80.2 22.7 %collective-permute-done.9.refs_5_.refs_6_ = bf16[384,1536]{1,0:T(8,128)(2,1)} collective-permute-done((bf16[384,1536]{1,0:T(8,128)(2,1)}, bf16[384,1536]{1,0:T(8,128)(2,1)}, u32[]{:S(2)}, u32[]{:S(2)}) %collective-permute-start.9) | collective-permute-done | bytes 1179680 | tf_op jit(solution)/shard_map/ppermute | solution.py:173
  102.9 1.1 slice.117
  104.0 1.7 collective-permute-start.11
  105.7 17.0 %collective-permute-done.8.refs_3_.refs_4_ = bf16[384,1536]{1,0:T(8,128)(2,1)} collective-permute-done((bf16[384,1536]{1,0:T(8,128)(2,1)}, bf16[384,1536]{1,0:T(8,128)(2,1)}, u32[]{:S(2)}, u32[]{:S(2)}) %collective-permute-start.8) | collective-permute-done | bytes 1179680 | tf_op jit(solution)/shard_map/ppermute | solution.py:172
  122.6 1.1 slice.116
  123.7 1.6 collective-permute-start.10
  125.4 1.5 fusion.1
  126.9 14.5 %shard_map.146 = (f32[384,768]{1,0:T(8,128)S(1)}, f32[384,768]{1,0:T(8,128)S(1)}, f32[384,768]{1,0:T(8,128)S(1)}) custom-call(bf16[384,768]{1,0:T(8,128)(2,1)S(1)} %slice.111.refs_0_, bf16[384,768]{1,0:T(8,128)(2,1)S(1)} %slice.112.refs_1_, bf16[384,768]{1,0:T(8,128)(2,1)S(1)} %slice.113.refs_2_, bf16[384,1536]{1,0:T(8,128)(2,1)} %collective-permute-done.3.refs_3_.refs_4_, ...), custom_call_target="tpu_custom_call" | custom-call | tf_op jit(solution)/shard_map/pallas_call | solution.py:110
  141.5 12.0 %shard_map.147 = (f32[384,768]{1,0:T(8,128)S(1)}, f32[384,768]{1,0:T(8,128)S(1)}, f32[384,768]{1,0:T(8,128)S(1)}) custom-call(bf16[384,768]{1,0:T(8,128)(2,1)S(1)} %slice.111.refs_0_, bf16[384,1536]{1,0:T(8,128)(2,1)S(1)} %pad_maximum_fusion.1.refs_1_.refs_2_, bf16[384,1536]{1,0:T(8,128)(2,1)S(1)} %pad_maximum_fusion.1.refs_1_.refs_2_, ...), custom_call_target="tpu_custom_call" | custom-call | tf_op jit(solution)/shard_map/pallas_call | solution.py:110
  153.6 6.5 %shard_map.148 = (f32[384,768]{1,0:T(8,128)S(1)}, f32[384,768]{1,0:T(8,128)S(1)}, f32[384,768]{1,0:T(8,128)S(1)}) custom-call(bf16[384,768]{1,0:T(8,128)(2,1)S(1)} %slice.111.refs_0_, bf16[384,1536]{1,0:T(8,128)(2,1)S(1)} %pad_maximum_fusion.2.refs_1_.refs_2_, bf16[384,1536]{1,0:T(8,128)(2,1)S(1)} %pad_maximum_fusion.2.refs_1_.refs_2_), custom_call_target="tpu_custom_call" | custom-call | tf_op jit(solution)/shard_map/pallas_call | solution.py:110
  160.1 1.9 add_divide_fusion
  162.0 2.0 maximum_dynamic-update-slice_fusion.refs_1_.refs_2_
  164.0 19.7 %shard_map.145 = (f32[384,512]{1,0:T(8,128)}, f32[384,512]{1,0:T(8,128)S(1)}, f32[384,512]{1,0:T(8,128)S(1)}) custom-call(bf16[384,512]{1,0:T(8,128)(2,1)S(1)} %slice.108.refs_0_, bf16[3072,1024]{1,0:T(8,128)(2,1)} %maximum_dynamic-update-slice_fusion.refs_1_.refs_2_, bf16[3072,1024]{1,0:T(8,128)(2,1)} %maximum_dynamic-update-slice_fusion.refs_1_.refs_2_), custom_call_target="tpu_custom_call" | custom-call | tf_op jit(solution)/shard_map/pallas_call | solution.py:110
  183.7 0.2 div.40
  183.9 1.1 copy-done.2
  185.0 0.3 copy-done.4
  185.2 0.4 convert_reduce_fusion.1
  185.7 0.1 reduce_sum.82
  186.0 0.1 reduce_sum.85
  186.5 0.6 fusion.9
  187.1 1.9 collective-permute-start.12
  189.0 4.1 %collective-permute-start.13 = (bf16[1,64,1280]{2,1,0:T(8,128)(2,1)S(1)}, bf16[1,64,1280]{2,1,0:T(8,128)(2,1)S(1)}, u32[]{:S(2)}, u32[]{:S(2)}) collective-permute-start(bf16[1,64,1280]{2,1,0:T(8,128)(2,1)S(1)} %get-tuple-element.37), channel_id=1, source_target_pairs={{1,0},{2,1},{3,2},{4,3},{5,4},{6,5},{7,6},{9,8},{10,9},{11,10},{12... | collective-permute-start | bytes 491528 | tf_op jit(solution)/shard_map/ppermute | solution.py:31
  193.2 0.3 convolution_reduce_fusion
  193.5 0.6 copy.30
  194.1 0.2 collective-permute-done.12
  194.3 0.3 copy.29
  194.5 5.3 %collective-permute-done.13 = bf16[1,64,1280]{2,1,0:T(8,128)(2,1)S(1)} collective-permute-done((bf16[1,64,1280]{2,1,0:T(8,128)(2,1)S(1)}, bf16[1,64,1280]{2,1,0:T(8,128)(2,1)S(1)}, u32[]{:S(2)}, u32[]{:S(2)}) %collective-permute-start.13) | collective-permute-done | bytes 163872 | tf_op jit(solution)/shard_map/ppermute | solution.py:31
  199.8 0.3 copy.31
  200.1 1.1 maximum_bitcast_fusion
  201.3 0.2 copy.33
  201.6 0.3 copy-done.15
  201.9 15.6 %fusion.21 = f32[6,8,9,640]{3,1,2,0:T(8,128)S(1)} fusion(bf16[3,3,1280,640]{3,2,1,0:T(8,128)(2,1)} %param.26, bf16[8,1,7,2,1280]{4,2,3,0,1:T(8,128)(2,1)S(1)} %slice.122, bf16[8,1,8,9,1280]{4,2,3,0,1:T(8,128)(2,1)S(1)} %copy.33, pred[8,9]{0,1:T(8,128)(4,1)S(1)} %copy-done.15), kind=kOutput, calls=%fused_computation.31 | convolution fusion | flops 6375782400 | bytes 17612872 | tf_op jit(solution)/shard_map/conv_general_dilated | solution.py:214
  217.5 0.3 copy.34
  218.0 0.2 copy.35
  218.2 0.6 copy-done.12
  218.8 0.9 fusion.25
  219.7 0.1 copy-done.1
  (78 shorter events, 1.9 us)
Async XLA Ops:
  6.5 62.5 %copy-start = (bf16[1280,1280]{1,0:T(8,128)(2,1)S(1)}, bf16[1280,1280]{1,0:T(8,128)(2,1)}, u32[]{:S(2)}) copy-start(bf16[1280,1280]{1,0:T(8,128)(2,1)} %param.22) | copy-start | bytes 9830404
  6.5 155.4 %all-gather.2.cloned.1.call-start = ((), (), s32[]{:S(2)}) async-start(), calls=%async_computation | async-start | bytes 7077888 | tf_op jit(solution)/shard_map/all_gather | solution.py:165
  6.5 2.0 slice-start
  6.5 2.1 slice-start.2
  9.7 1.1 slice-start.1
  9.7 1.3 slice-start.3
  9.7 8.2 %copy-start.7 = (f32[6,2,2,32]{3,2,1,0:T(2,128)S(1)}, f32[6,2,2,32]{3,2,1,0:T(2,128)}, u32[]{:S(2)}) copy-start(f32[6,2,2,32]{3,2,1,0:T(2,128)} %param.18) | copy-start | bytes 9220
  10.9 58.0 %copy-start.8 = (f32[1280]{0:T(1024)S(1)}, f32[1280]{0:T(1024)}, u32[]{:S(2)}) copy-start(f32[1280]{0:T(1024)} %param.19) | copy-start | bytes 15364
  10.9 58.0 %copy-start.9 = (f32[1280]{0:T(1024)S(1)}, f32[1280]{0:T(1024)}, u32[]{:S(2)}) copy-start(f32[1280]{0:T(1024)} %param.20) | copy-start | bytes 15364
  12.0 54.5 %collective-permute-start.5 = (bf16[384,1536]{1,0:T(8,128)(2,1)}, bf16[384,1536]{1,0:T(8,128)(2,1)}, u32[]{:S(2)}, u32[]{:S(2)}) collective-permute-start(bf16[384,1536]{1,0:T(8,128)(2,1)} %pad_maximum_fusion), channel_id=1, source_target_pairs={{0,4},{1,5},{2,6},{3,7},{4,0},{5,1},{6,2},{7,3},{8,12},{9,13},{10,... | collective-permute-start | bytes 3538952 | tf_op jit(solution)/shard_map/ppermute | solution.py:169
  15.9 52.5 %collective-permute-start.3 = (bf16[384,1536]{1,0:T(8,128)(2,1)}, bf16[384,1536]{1,0:T(8,128)(2,1)}, u32[]{:S(2)}, u32[]{:S(2)}) collective-permute-start(bf16[384,1536]{1,0:T(8,128)(2,1)} %pad_maximum_fusion), channel_id=1, source_target_pairs={{0,1},{1,2},{2,3},{3,0},{4,5},{5,6},{6,7},{7,4},{8,9},{9,10},{10,1... | collective-permute-start | bytes 3538952 | tf_op jit(solution)/shard_map/ppermute | solution.py:167
  16.1 55.7 %collective-permute-start.4 = (bf16[384,1536]{1,0:T(8,128)(2,1)}, bf16[384,1536]{1,0:T(8,128)(2,1)}, u32[]{:S(2)}, u32[]{:S(2)}) collective-permute-start(bf16[384,1536]{1,0:T(8,128)(2,1)} %pad_maximum_fusion), channel_id=1, source_target_pairs={{0,3},{1,0},{2,1},{3,2},{4,7},{5,4},{6,5},{7,6},{8,11},{9,8},{10,9... | collective-permute-start | bytes 3538952 | tf_op jit(solution)/shard_map/ppermute | solution.py:168
  17.9 38.4 %collective-permute-start = (f32[2,2,32]{2,1,0:T(2,128)S(1)}, f32[2,2,32]{2,1,0:T(2,128)S(1)}, u32[]{:S(2)}, u32[]{:S(2)}) collective-permute-start(f32[2,2,32]{2,1,0:T(2,128)S(1)} %reduce_sum.54), channel_id=1, source_target_pairs={{0,1},{1,0},{2,3},{3,2},{4,5},{5,4},{6,7},{7,6},{8,9},{9,8},{10,11... | collective-permute-start | bytes 1544 | tf_op jit(solution)/shard_map/ppermute | solution.py:161
  56.3 5.1 %collective-permute-start.1 = (f32[2,2,32]{2,1,0:T(2,128)S(1)}, f32[2,2,32]{2,1,0:T(2,128)S(1)}, u32[]{:S(2)}, u32[]{:S(2)}) collective-permute-start(f32[2,2,32]{2,1,0:T(2,128)S(1)} %add.77), channel_id=1, source_target_pairs={{0,2},{1,3},{2,0},{3,1},{4,6},{5,7},{6,4},{7,5},{8,10},{9,11},{10,... | collective-permute-start | bytes 1544 | tf_op jit(solution)/shard_map/ppermute | solution.py:161
  61.4 5.1 %collective-permute-start.2 = (f32[2,2,32]{2,1,0:T(2,128)S(1)}, f32[2,2,32]{2,1,0:T(2,128)S(1)}, u32[]{:S(2)}, u32[]{:S(2)}) collective-permute-start(f32[2,2,32]{2,1,0:T(2,128)S(1)} %add.78), channel_id=1, source_target_pairs={{0,4},{1,5},{2,6},{3,7},{4,0},{5,1},{6,2},{7,3},{8,12},{9,13},{10,... | collective-permute-start | bytes 1544 | tf_op jit(solution)/shard_map/ppermute | solution.py:162
  66.5 36.3 %collective-permute-start.9 = (bf16[384,1536]{1,0:T(8,128)(2,1)}, bf16[384,1536]{1,0:T(8,128)(2,1)}, u32[]{:S(2)}, u32[]{:S(2)}) collective-permute-start(bf16[384,1536]{1,0:T(8,128)(2,1)} %collective-permute-done.5.refs_7_.refs_8_), channel_id=1, source_target_pairs={{0,3},{1,0},{2,1},{3,2},{4,7},{5,4},{6,5},{7,6},{8,11},{9,8},{10,9... | collective-permute-start | bytes 3538952 | tf_op jit(solution)/shard_map/ppermute | solution.py:173
  68.3 54.3 %collective-permute-start.8 = (bf16[384,1536]{1,0:T(8,128)(2,1)}, bf16[384,1536]{1,0:T(8,128)(2,1)}, u32[]{:S(2)}, u32[]{:S(2)}) collective-permute-start(bf16[384,1536]{1,0:T(8,128)(2,1)} %collective-permute-done.3.refs_3_.refs_4_), channel_id=1, source_target_pairs={{0,4},{1,5},{2,6},{3,7},{4,0},{5,1},{6,2},{7,3},{8,12},{9,13},{10,... | collective-permute-start | bytes 3538952 | tf_op jit(solution)/shard_map/ppermute | solution.py:172
  69.0 8.8 %copy-start.13 = (bf16[1280,1280]{1,0:T(8,128)(2,1)S(1)}, bf16[1280,1280]{1,0:T(8,128)(2,1)}, u32[]{:S(2)}) copy-start(bf16[1280,1280]{1,0:T(8,128)(2,1)} %param.23) | copy-start | bytes 9830404
  71.8 7.5 %copy-start.5 = (bf16[384,1280]{1,0:T(8,128)(2,1)}, bf16[384,1280]{1,0:T(8,128)(2,1)S(1)}, u32[]{:S(2)}) copy-start(bf16[384,1280]{1,0:T(8,128)(2,1)S(1)} %convolution_convert_fusion.1) | copy-start | bytes 2949124
  71.8 6.0 %copy-start.3 = (bf16[384,1280]{1,0:T(8,128)(2,1)S(1)}, bf16[384,1280]{1,0:T(8,128)(2,1)}, u32[]{:S(2)}) copy-start(bf16[384,1280]{1,0:T(8,128)(2,1)} %param.15) | copy-start | bytes 2949124
  73.3 68.1 %collective-permute-start.7 = (bf16[192,1536]{1,0:T(8,128)(2,1)S(1)}, bf16[192,1536]{1,0:T(8,128)(2,1)S(1)}, u32[]{:S(2)}, u32[]{:S(2)}) collective-permute-start(bf16[192,1536]{1,0:T(8,128)(2,1)S(1)} %slice.115), channel_id=1, source_target_pairs={{0,3},{1,0},{2,1},{3,2},{4,7},{5,4},{6,5},{7,6},{8,11},{9,8},{10,9... | collective-permute-start | bytes 1769480 | tf_op jit(solution)/shard_map/ppermute | solution.py:171
  74.6 66.8 %collective-permute-start.6 = (bf16[192,1536]{1,0:T(8,128)(2,1)S(1)}, bf16[192,1536]{1,0:T(8,128)(2,1)S(1)}, u32[]{:S(2)}, u32[]{:S(2)}) collective-permute-start(bf16[192,1536]{1,0:T(8,128)(2,1)S(1)} %slice.114), channel_id=1, source_target_pairs={{0,1},{1,2},{2,3},{3,0},{4,5},{5,6},{6,7},{7,4},{8,9},{9,10},{10,1... | collective-permute-start | bytes 1769480 | tf_op jit(solution)/shard_map/ppermute | solution.py:170
  80.1 45.3 %copy-start.14 = (bf16[1280,1280]{1,0:T(8,128)(2,1)S(1)}, bf16[1280,1280]{1,0:T(8,128)(2,1)}, u32[]{:S(2)}) copy-start(bf16[1280,1280]{1,0:T(8,128)(2,1)} %param.21) | copy-start | bytes 9830404
  104.0 49.5 %collective-permute-start.11 = (bf16[192,1536]{1,0:T(8,128)(2,1)S(1)}, bf16[192,1536]{1,0:T(8,128)(2,1)S(1)}, u32[]{:S(2)}, u32[]{:S(2)}) collective-permute-start(bf16[192,1536]{1,0:T(8,128)(2,1)S(1)} %slice.117), channel_id=1, source_target_pairs={{0,3},{1,0},{2,1},{3,2},{4,7},{5,4},{6,5},{7,6},{8,11},{9,8},{10,9... | collective-permute-start | bytes 1769480 | tf_op jit(solution)/shard_map/ppermute | solution.py:175
  123.7 29.8 %collective-permute-start.10 = (bf16[192,1536]{1,0:T(8,128)(2,1)S(1)}, bf16[192,1536]{1,0:T(8,128)(2,1)S(1)}, u32[]{:S(2)}, u32[]{:S(2)}) collective-permute-start(bf16[192,1536]{1,0:T(8,128)(2,1)S(1)} %slice.116), channel_id=1, source_target_pairs={{0,1},{1,2},{2,3},{3,0},{4,5},{5,6},{6,7},{7,4},{8,9},{9,10},{10,1... | collective-permute-start | bytes 1769480 | tf_op jit(solution)/shard_map/ppermute | solution.py:174
  160.0 1.9 slice-start.4
  183.7 1.3 copy-start.2
  183.7 1.5 copy-start.4
  185.2 1.2 copy-start.10
  185.2 1.2 copy-start.11
  185.7 7.6 %copy-start.6 = (bf16[320,640]{1,0:T(8,128)(2,1)S(1)}, bf16[320,640]{1,0:T(8,128)(2,1)}, u32[]{:S(2)}) copy-start(bf16[320,640]{1,0:T(8,128)(2,1)} %param.28) | copy-start | bytes 1228804
  187.1 7.2 %collective-permute-start.12 = (bf16[1,64,1280]{2,1,0:T(8,128)(2,1)S(1)}, bf16[1,64,1280]{2,1,0:T(8,128)(2,1)S(1)}, u32[]{:S(2)}, u32[]{:S(2)}) collective-permute-start(bf16[1,64,1280]{2,1,0:T(8,128)(2,1)S(1)} %get-tuple-element.36), channel_id=1, source_target_pairs={{0,1},{1,2},{2,3},{3,4},{4,5},{5,6},{6,7},{8,9},{9,10},{10,11},{11... | collective-permute-start | bytes 491528 | tf_op jit(solution)/shard_map/ppermute | solution.py:29
  189.0 10.8 %collective-permute-start.13 = (bf16[1,64,1280]{2,1,0:T(8,128)(2,1)S(1)}, bf16[1,64,1280]{2,1,0:T(8,128)(2,1)S(1)}, u32[]{:S(2)}, u32[]{:S(2)}) collective-permute-start(bf16[1,64,1280]{2,1,0:T(8,128)(2,1)S(1)} %get-tuple-element.37), channel_id=1, source_target_pairs={{1,0},{2,1},{3,2},{4,3},{5,4},{6,5},{7,6},{9,8},{10,9},{11,10},{12... | collective-permute-start | bytes 491528 | tf_op jit(solution)/shard_map/ppermute | solution.py:31
  201.3 0.7 copy-start.15
  217.8 1.9 copy-start.1
  217.9 0.8 copy-start.12
Sparse Core Ops, SparseCore 0:
  9.8 134.4 all-gather.1

commit v3 on v1

--- a/solution.py
+++ b/solution.py
@@ -15,23 +15,6 @@
 
 
 EPS = 1e-05
-
-
-def padded_2(cells, sides, width):
-    for axis, dim in sides:
-        count = lax.axis_size(axis)
-        ends = count - 1
-        head = lax.slice_in_dim(cells, 0, width, axis=dim)
-        tail = lax.slice_in_dim(cells, cells.shape[dim] - width, cells.shape[dim], axis=dim)
-        cells = jnp.concatenate(
-            [
-                lax.ppermute(tail, axis, [(i, (i + 1) % count) for i in range(ends)]),
-                cells,
-                lax.ppermute(head, axis, [((i + 1) % count, i) for i in range(ends)]),
-            ],
-            axis=dim,
-        )
-    return cells
 
 
 def group_moments(rows_in, groups):
@@ -201,15 +184,27 @@
     totals_conv = total_conv - own_stale[1] + group_moments(updated, GROUPS)
     normed_conv = group_normalize(updated, totals_conv, count, gain_conv, bias_conv, GROUPS)
     activated = jax.nn.silu(normed_conv).astype(jnp.bfloat16).reshape(tok_rows // W, W, channels)
-    padded = padded_2(activated, (("patch", 0),), 1)
-    convolved = lax.conv_general_dilated(
-        padded[None],
-        conv_weight,
-        (1, 1),
-        ((0, 0), (1, 1)),
-        dimension_numbers=("NHWC", "HWIO", "NHWC"),
-        preferred_element_type=jnp.float32,
-    )[0]
+    rows = activated.shape[0]
+    count_p = lax.axis_size("patch")
+    top = lax.ppermute(
+        activated[rows - 1 :], "patch", [(i, i + 1) for i in range(count_p - 1)]
+    )
+    bottom = lax.ppermute(activated[:1], "patch", [(i + 1, i) for i in range(count_p - 1)])
+
+    def conv_rows(cells):
+        return lax.conv_general_dilated(
+            cells[None],
+            conv_weight,
+            (1, 1),
+            ((0, 0), (1, 1)),
+            dimension_numbers=("NHWC", "HWIO", "NHWC"),
+            preferred_element_type=jnp.float32,
+        )[0]
+
+    inner = conv_rows(activated)
+    first_row = conv_rows(jnp.concatenate([top, activated[:2]], axis=0))
+    last_row = conv_rows(jnp.concatenate([activated[rows - 2 :], bottom], axis=0))
+    convolved = jnp.concatenate([first_row, inner, last_row], axis=0)
     temb = time_embedding(timestep, w_time)
     conv_out = (convolved + conv_bias + temb).astype(jnp.bfloat16)
     return conv_out.reshape(tok_rows, conv_weight.shape[3])

time: 220 us -> 215 us (0.977)
  the two profiles are of different devices: /device:TPU:28 before, /device:TPU:64 now
where the time goes in v3:
time: 215 us
  waiting for transfers between devices  85.6 us (40%)
  Pallas kernels  55.4 us (26%)
  starting transfers between devices  25.5 us (12%)
  matrix products  20 us (9%)
  local copies, waits for them, and re-layouts  14.9 us (7%)
  other arithmetic  12 us (6%)
    pallas_call x3, Pallas kernels, attention_partial(): pl.pallas_call(functools.partial(attn_kernel, n_pieces=len(pieces)), grid...  55.4 us
    ppermute x1, waiting for transfers between devices, body(): partner = lax.ppermute(kv, 'patch', perm(0, 1))  43.1 us
    ppermute x2, waiting for transfers between devices, body(): stale_all = stale_all + lax.ppermute(stale_all, 'patch', pairs)  40.2 us
    conv_general_dilated x3, matrix products, conv_rows(): lax.conv_general_dilated(cells[None], conv_weight, (1, 1), ((0, 0), (1, 1...  14.3 us
    ppermute x1, starting transfers between devices, body(): lax.ppermute(activated[:1], 'patch', [(i + 1, i) for i in range(count_p -...  7.02 us
    reduce_sum x4, other arithmetic, group_moments(): jnp.sum(values, axis=(0, 2))  5.53 us
  transfers between devices with their start and end apart: 14, of which 4 were waited for; matrix products, arithmetic and copies ran while one was open for 13% of the time, Pallas kernels for 20%

profile of v3, /device:TPU:64, one launch (start us, length us, event | category | flops | bytes accessed | tf_op | source)
XLA Modules:
  0.0 214.6 jit_solution(9107451900393513440)
XLA Ops:
  0.0 2.4 %constant_dynamic-update-slice_fusion.1 = bf16[384,2560]{1,0:T(8,128)(2,1)} fusion(bf16[384,1280]{1,0:T(8,128)(2,1)} %param.16), kind=kLoop, calls=%fused_computation.67 | loop fusion | bytes 1966080
  2.4 1.1 constant_dynamic-update-slice_fusion
  3.5 1.6 collective-permute-start.3
  5.1 1.7 collective-permute-start.4
  6.8 43.1 %collective-permute-done.5.refs_7_.refs_8_ = bf16[384,2560]{1,0:T(8,128)(2,1)} collective-permute-done((bf16[384,2560]{1,0:T(8,128)(2,1)}, bf16[384,2560]{1,0:T(8,128)(2,1)}, u32[]{:S(2)}, u32[]{:S(2)}) %collective-permute-start.5) | collective-permute-done | bytes 1966112 | tf_op jit(solution)/shard_map/ppermute | solution.py:148
  49.9 3.0 %collective-permute-start.9 = (bf16[384,2560]{1,0:T(8,128)(2,1)}, bf16[384,2560]{1,0:T(8,128)(2,1)}, u32[]{:S(2)}, u32[]{:S(2)}) collective-permute-start(bf16[384,2560]{1,0:T(8,128)(2,1)} %collective-permute-done.5.refs_7_.refs_8_), channel_id=1, source_target_pairs={{0,3},{1,0},{2,1},{3,2},{4,7},{5,4},{6,5},{7,6},{8,11},{9,8},{10,9... | collective-permute-start | bytes 5898248 | tf_op jit(solution)/shard_map/ppermute | solution.py:152
  52.9 0.3 collective-permute-start.8
  53.2 0.1 collective-permute-start
  54.0 1.5 convert_reduce_fusion
  55.5 38.4 %collective-permute-done = f32[2,2,32]{2,1,0:T(2,128)S(1)} collective-permute-done((f32[2,2,32]{2,1,0:T(2,128)S(1)}, f32[2,2,32]{2,1,0:T(2,128)S(1)}, u32[]{:S(2)}, u32[]{:S(2)}) %collective-permute-start) | collective-permute-done | bytes 544 | tf_op jit(solution)/shard_map/ppermute | solution.py:143
  93.9 3.2 %collective-permute-start.1 = (f32[2,2,32]{2,1,0:T(2,128)S(1)}, f32[2,2,32]{2,1,0:T(2,128)S(1)}, u32[]{:S(2)}, u32[]{:S(2)}) collective-permute-start(f32[2,2,32]{2,1,0:T(2,128)S(1)} %add.74), channel_id=1, source_target_pairs={{0,2},{1,3},{2,0},{3,1},{4,6},{5,7},{6,4},{7,5},{8,10},{9,11},{10,... | collective-permute-start | bytes 1544 | tf_op jit(solution)/shard_map/ppermute | solution.py:143
  97.2 1.8 collective-permute-done.1
  99.0 1.2 collective-permute-start.2
  100.2 1.3 convolution_reduce_fusion
  101.6 0.1 reduce_sum.60
  101.8 0.1 reduce_sum.66
  101.9 2.2 %collective-permute-done.2 = f32[2,2,32]{2,1,0:T(2,128)S(1)} collective-permute-done((f32[2,2,32]{2,1,0:T(2,128)S(1)}, f32[2,2,32]{2,1,0:T(2,128)S(1)}, u32[]{:S(2)}, u32[]{:S(2)}) %collective-permute-start.2) | collective-permute-done | bytes 544 | tf_op jit(solution)/shard_map/ppermute | solution.py:144
  104.5 1.3 slice.89
  105.9 1.4 collective-permute-start.7
  107.3 1.3 slice.88
  108.5 0.8 collective-permute-start.6
  109.3 1.5 fusion.1.refs_0_
  110.8 1.4 slice.91
  112.2 2.6 %collective-permute-start.11 = (bf16[192,2560]{1,0:T(8,128)(2,1)S(1)}, bf16[192,2560]{1,0:T(8,128)(2,1)S(1)}, u32[]{:S(2)}, u32[]{:S(2)}) collective-permute-start(bf16[192,2560]{1,0:T(8,128)(2,1)S(1)} %slice.91), channel_id=1, source_target_pairs={{0,3},{1,0},{2,1},{3,2},{4,7},{5,4},{6,5},{7,6},{8,11},{9,8},{10,9... | collective-permute-start | bytes 2949128 | tf_op jit(solution)/shard_map/ppermute | solution.py:154
  114.8 1.3 slice.90
  116.1 0.3 collective-permute-start.10
  116.4 1.5 convolution_convert_fusion.1.refs_1_
  117.9 0.2 copy-done.13
  118.0 1.5 convolution_convert_fusion.refs_2_
  119.5 23.6 %shard_map.145 = (f32[384,1280]{1,0:T(8,128)S(1)}, f32[384,1280]{1,0:T(8,128)}, f32[384,1280]{1,0:T(8,128)}) custom-call(bf16[384,1280]{1,0:T(8,128)(2,1)S(1)} %fusion.1.refs_0_, bf16[384,1280]{1,0:T(8,128)(2,1)S(1)} %convolution_convert_fusion.1.refs_1_, bf16[384,1280]{1,0:T(8,128)(2,1)S(1)} %convolution_convert_fusion.refs_2_, ...), custom_call_target="tpu_custom_call" | custom-call | tf_op jit(solution)/shard_map/pallas_call | solution.py:92
  143.1 1.4 pad_maximum_fusion.refs_1_.refs_2_
  144.5 19.6 %shard_map.146 = (f32[384,1280]{1,0:T(8,128)S(1)}, f32[384,1280]{1,0:T(8,128)S(1)}, f32[384,1280]{1,0:T(8,128)}) custom-call(bf16[384,1280]{1,0:T(8,128)(2,1)S(1)} %fusion.1.refs_0_, bf16[384,2560]{1,0:T(8,128)(2,1)} %pad_maximum_fusion.refs_1_.refs_2_, bf16[384,2560]{1,0:T(8,128)(2,1)} %pad_maximum_fusion.refs_1_.refs_2_, ...), custom_call_target="tpu_custom_call" | custom-call | tf_op jit(solution)/shard_map/pallas_call | solution.py:92
  164.1 1.4 pad_maximum_fusion.1.refs_1_.refs_2_
  165.5 12.2 %shard_map.147 = (f32[384,1280]{1,0:T(8,128)S(1)}, f32[384,1280]{1,0:T(8,128)S(1)}, f32[384,1280]{1,0:T(8,128)}) custom-call(bf16[384,1280]{1,0:T(8,128)(2,1)S(1)} %fusion.1.refs_0_, bf16[384,2560]{1,0:T(8,128)(2,1)} %pad_maximum_fusion.1.refs_1_.refs_2_, bf16[384,2560]{1,0:T(8,128)(2,1)} %pad_maximum_fusion.1.refs_1_.refs_2_), custom_call_target="tpu_custom_call" | custom-call | tf_op jit(solution)/shard_map/pallas_call | solution.py:92
  177.8 3.8 %convert_reduce_fusion.1 = (f32[1280]{0:T(1024)S(1)}, f32[1280]{0:T(1024)S(1)}, bf16[384,1280]{1,0:T(8,128)(2,1)S(1)}) fusion(f32[384,1280]{1,0:T(8,128)S(1)} %get-tuple-element.22, f32[384,1280]{1,0:T(8,128)S(1)} %get-tuple-element.21, f32[384,1280]{1,0:T(8,128)S(1)} %copy-done.3, f32[384,1280]{1,0:T(8,128)} %get-tuple-element.19, ...), kind=kLoop, calls=%fused_computation.6 | loop fusion | flops 11302400 | bytes 19671040 | tf_op jit(solution)/shard_map/reduce_sum | solution.py:24
  181.7 0.1 reduce_sum.82
  181.9 0.1 reduce_sum.85
  182.1 0.1 reshape.49
  182.4 0.6 fusion.9
  183.0 2.4 %collective-permute-start.12 = (bf16[1,64,1280]{2,1,0:T(8,128)(2,1)S(1)}, bf16[1,64,1280]{2,1,0:T(8,128)(2,1)S(1)}, u32[]{:S(2)}, u32[]{:S(2)}) collective-permute-start(bf16[1,64,1280]{2,1,0:T(8,128)(2,1)S(1)} %get-tuple-element.32), channel_id=1, source_target_pairs={{0,1},{1,2},{2,3},{3,4},{4,5},{5,6},{6,7},{8,9},{9,10},{10,11},{11... | collective-permute-start | bytes 491528 | tf_op jit(solution)/shard_map/ppermute | solution.py:189
  185.5 7.0 %collective-permute-start.13 = (bf16[1,64,1280]{2,1,0:T(8,128)(2,1)S(1)}, bf16[1,64,1280]{2,1,0:T(8,128)(2,1)S(1)}, u32[]{:S(2)}, u32[]{:S(2)}) collective-permute-start(bf16[1,64,1280]{2,1,0:T(8,128)(2,1)S(1)} %get-tuple-element.33), channel_id=1, source_target_pairs={{1,0},{2,1},{3,2},{4,3},{5,4},{6,5},{7,6},{9,8},{10,9},{11,10},{12... | collective-permute-start | bytes 491528 | tf_op jit(solution)/shard_map/ppermute | solution.py:192
  192.5 0.3 copy.46
  192.9 0.3 copy.54
  193.2 0.6 copy.50
  193.8 0.2 pad.2
  194.0 0.2 copy.52
  194.3 0.4 copy-done.10
  194.7 9.0 %fusion.23 = f32[4,8,9,640]{3,1,2,0:T(8,128)S(1)} fusion(bf16[3,3,1280,640]{3,2,1,0:T(8,128)(2,1)} %param.26, bf16[6,1,7,2,1280]{4,2,3,0,1:T(8,128)(2,1)S(1)} %slice.98, bf16[6,1,8,9,1280]{4,2,3,0,1:T(8,128)(2,1)S(1)} %copy.52, pred[8,9]{0,1:T(8,128)(4,1)S(1)} %copy-done.10), kind=kOutput, calls=%fused_computation.37 | convolution fusion | flops 4250972160 | bytes 16803912 | tf_op jit(solution)/shard_map/conv_general_dilated | solution.py:195
  203.8 0.2 copy.53
  204.0 0.3 copy.55
  204.3 0.7 maximum_bitcast_fusion.1
  205.0 0.3 pad.4
  205.3 0.3 copy.45
  205.6 0.7 maximum_bitcast_fusion
  206.3 0.3 pad
  206.7 2.6 %convolution_select_fusion.1 = f32[1,8,9,640]{3,1,2,0:T(8,128)S(1)} fusion(bf16[3,3,1280,640]{3,2,1,0:T(8,128)(2,1)S(1)} %bitcast.92, bf16[3,1,7,2,1280]{4,2,3,0,1:T(8,128)(2,1)S(1)} %slice.96, bf16[3,1,8,9,1280]{4,2,3,0,1:T(8,128)(2,1)S(1)} %copy.48, pred[8,9]{0,1:T(8,128)(4,1)S(1)} %copy-done.10), kind=kOutput, calls=%fused_computation.39 | convolution fusion | flops 1063756800 | bytes 15590472 | tf_op jit(solution)/shard_map/conv_general_dilated | solution.py:195
  209.3 0.2 copy.49
  209.6 2.6 %convolution_select_fusion = f32[1,8,9,640]{3,1,2,0:T(8,128)S(1)} fusion(bf16[3,3,1280,640]{3,2,1,0:T(8,128)(2,1)S(1)} %bitcast.92, bf16[3,1,7,2,1280]{4,2,3,0,1:T(8,128)(2,1)S(1)} %slice.102, bf16[3,1,8,9,1280]{4,2,3,0,1:T(8,128)(2,1)S(1)} %copy.57, pred[8,9]{0,1:T(8,128)(4,1)S(1)} %copy-done.10), kind=kOutput, calls=%fused_computation.38 | convolution fusion | flops 1063756800 | bytes 15590472 | tf_op jit(solution)/shard_map/conv_general_dilated | solution.py:195
  212.2 0.2 copy.58
  212.4 0.1 slice_bitcast_fusion.1
  212.5 0.4 pad_maximum_fusion.2
  213.0 0.2 copy.59
  213.2 0.9 fusion.27
  214.1 0.6 copy-done.1
  (77 shorter events, 1.6 us)
Async XLA Ops:
  0.0 109.3 %copy-start = (bf16[1280,1280]{1,0:T(8,128)(2,1)S(1)}, bf16[1280,1280]{1,0:T(8,128)(2,1)}, u32[]{:S(2)}) copy-start(bf16[1280,1280]{1,0:T(8,128)(2,1)} %param.21) | copy-start | bytes 9830404
  0.0 2.4 %copy-start.4 = (bf16[384,1280]{1,0:T(8,128)(2,1)S(1)}, bf16[384,1280]{1,0:T(8,128)(2,1)}, u32[]{:S(2)}) copy-start(bf16[384,1280]{1,0:T(8,128)(2,1)} %param.17) | copy-start | bytes 2949124
  0.0 53.2 %copy-start.5 = (f32[6,2,2,32]{3,2,1,0:T(2,128)S(1)}, f32[6,2,2,32]{3,2,1,0:T(2,128)}, u32[]{:S(2)}) copy-start(f32[6,2,2,32]{3,2,1,0:T(2,128)} %param.18) | copy-start | bytes 9220
  2.4 102.0 %copy-start.6 = (f32[1280]{0:T(1024)S(1)}, f32[1280]{0:T(1024)}, u32[]{:S(2)}) copy-start(f32[1280]{0:T(1024)} %param.19) | copy-start | bytes 15364
  2.4 102.1 %copy-start.7 = (f32[1280]{0:T(1024)S(1)}, f32[1280]{0:T(1024)}, u32[]{:S(2)}) copy-start(f32[1280]{0:T(1024)} %param.20) | copy-start | bytes 15364
  3.5 46.4 %collective-permute-start.5 = (bf16[384,2560]{1,0:T(8,128)(2,1)}, bf16[384,2560]{1,0:T(8,128)(2,1)}, u32[]{:S(2)}, u32[]{:S(2)}) collective-permute-start(bf16[384,2560]{1,0:T(8,128)(2,1)} %constant_dynamic-update-slice_fusion), channel_id=1, source_target_pairs={{0,4},{1,5},{2,6},{3,7},{4,0},{5,1},{6,2},{7,3},{8,12},{9,13},{10,... | collective-permute-start | bytes 5898248 | tf_op jit(solution)/shard_map/ppermute | solution.py:148
  3.5 49.4 %collective-permute-start.3 = (bf16[384,2560]{1,0:T(8,128)(2,1)}, bf16[384,2560]{1,0:T(8,128)(2,1)}, u32[]{:S(2)}, u32[]{:S(2)}) collective-permute-start(bf16[384,2560]{1,0:T(8,128)(2,1)} %constant_dynamic-update-slice_fusion), channel_id=1, source_target_pairs={{0,1},{1,2},{2,3},{3,0},{4,5},{5,6},{6,7},{7,4},{8,9},{9,10},{10,1... | collective-permute-start | bytes 5898248 | tf_op jit(solution)/shard_map/ppermute | solution.py:146
  5.1 99.4 %collective-permute-start.4 = (bf16[384,2560]{1,0:T(8,128)(2,1)}, bf16[384,2560]{1,0:T(8,128)(2,1)}, u32[]{:S(2)}, u32[]{:S(2)}) collective-permute-start(bf16[384,2560]{1,0:T(8,128)(2,1)} %constant_dynamic-update-slice_fusion), channel_id=1, source_target_pairs={{0,3},{1,0},{2,1},{3,2},{4,7},{5,4},{6,5},{7,6},{8,11},{9,8},{10,9... | collective-permute-start | bytes 5898248 | tf_op jit(solution)/shard_map/ppermute | solution.py:147
  49.9 60.9 %collective-permute-start.9 = (bf16[384,2560]{1,0:T(8,128)(2,1)}, bf16[384,2560]{1,0:T(8,128)(2,1)}, u32[]{:S(2)}, u32[]{:S(2)}) collective-permute-start(bf16[384,2560]{1,0:T(8,128)(2,1)} %collective-permute-done.5.refs_7_.refs_8_), channel_id=1, source_target_pairs={{0,3},{1,0},{2,1},{3,2},{4,7},{5,4},{6,5},{7,6},{8,11},{9,8},{10,9... | collective-permute-start | bytes 5898248 | tf_op jit(solution)/shard_map/ppermute | solution.py:152
  52.9 61.9 %collective-permute-start.8 = (bf16[384,2560]{1,0:T(8,128)(2,1)}, bf16[384,2560]{1,0:T(8,128)(2,1)}, u32[]{:S(2)}, u32[]{:S(2)}) collective-permute-start(bf16[384,2560]{1,0:T(8,128)(2,1)} %collective-permute-done.3.refs_3_.refs_4_), channel_id=1, source_target_pairs={{0,4},{1,5},{2,6},{3,7},{4,0},{5,1},{6,2},{7,3},{8,12},{9,13},{10,... | collective-permute-start | bytes 5898248 | tf_op jit(solution)/shard_map/ppermute | solution.py:151
  53.2 40.7 %collective-permute-start = (f32[2,2,32]{2,1,0:T(2,128)S(1)}, f32[2,2,32]{2,1,0:T(2,128)S(1)}, u32[]{:S(2)}, u32[]{:S(2)}) collective-permute-start(f32[2,2,32]{2,1,0:T(2,128)S(1)} %reduce_sum.54), channel_id=1, source_target_pairs={{0,1},{1,0},{2,3},{3,2},{4,5},{5,4},{6,7},{7,6},{8,9},{9,8},{10,11... | collective-permute-start | bytes 1544 | tf_op jit(solution)/shard_map/ppermute | solution.py:143
  93.9 5.1 %collective-permute-start.1 = (f32[2,2,32]{2,1,0:T(2,128)S(1)}, f32[2,2,32]{2,1,0:T(2,128)S(1)}, u32[]{:S(2)}, u32[]{:S(2)}) collective-permute-start(f32[2,2,32]{2,1,0:T(2,128)S(1)} %add.74), channel_id=1, source_target_pairs={{0,2},{1,3},{2,0},{3,1},{4,6},{5,7},{6,4},{7,5},{8,10},{9,11},{10,... | collective-permute-start | bytes 1544 | tf_op jit(solution)/shard_map/ppermute | solution.py:143
  99.0 5.1 %collective-permute-start.2 = (f32[2,2,32]{2,1,0:T(2,128)S(1)}, f32[2,2,32]{2,1,0:T(2,128)S(1)}, u32[]{:S(2)}, u32[]{:S(2)}) collective-permute-start(f32[2,2,32]{2,1,0:T(2,128)S(1)} %add.75), channel_id=1, source_target_pairs={{0,4},{1,5},{2,6},{3,7},{4,0},{5,1},{6,2},{7,3},{8,12},{9,13},{10,... | collective-permute-start | bytes 1544 | tf_op jit(solution)/shard_map/ppermute | solution.py:144
  104.5 4.8 %copy-start.2 = (bf16[384,1280]{1,0:T(8,128)(2,1)S(1)}, bf16[384,1280]{1,0:T(8,128)(2,1)}, u32[]{:S(2)}) copy-start(bf16[384,1280]{1,0:T(8,128)(2,1)} %param.15) | copy-start | bytes 2949124
  105.9 37.2 %collective-permute-start.7 = (bf16[192,2560]{1,0:T(8,128)(2,1)S(1)}, bf16[192,2560]{1,0:T(8,128)(2,1)S(1)}, u32[]{:S(2)}, u32[]{:S(2)}) collective-permute-start(bf16[192,2560]{1,0:T(8,128)(2,1)S(1)} %slice.89), channel_id=1, source_target_pairs={{0,3},{1,0},{2,1},{3,2},{4,7},{5,4},{6,5},{7,6},{8,11},{9,8},{10,9... | collective-permute-start | bytes 2949128 | tf_op jit(solution)/shard_map/ppermute | solution.py:150
  108.5 34.6 %collective-permute-start.6 = (bf16[192,2560]{1,0:T(8,128)(2,1)S(1)}, bf16[192,2560]{1,0:T(8,128)(2,1)S(1)}, u32[]{:S(2)}, u32[]{:S(2)}) collective-permute-start(bf16[192,2560]{1,0:T(8,128)(2,1)S(1)} %slice.88), channel_id=1, source_target_pairs={{0,1},{1,2},{2,3},{3,0},{4,5},{5,6},{6,7},{7,4},{8,9},{9,10},{10,1... | collective-permute-start | bytes 2949128 | tf_op jit(solution)/shard_map/ppermute | solution.py:149
  110.8 5.6 %copy-start.12 = (bf16[1280,1280]{1,0:T(8,128)(2,1)S(1)}, bf16[1280,1280]{1,0:T(8,128)(2,1)}, u32[]{:S(2)}) copy-start(bf16[1280,1280]{1,0:T(8,128)(2,1)} %param.22) | copy-start | bytes 9830404
  112.2 51.9 %collective-permute-start.11 = (bf16[192,2560]{1,0:T(8,128)(2,1)S(1)}, bf16[192,2560]{1,0:T(8,128)(2,1)S(1)}, u32[]{:S(2)}, u32[]{:S(2)}) collective-permute-start(bf16[192,2560]{1,0:T(8,128)(2,1)S(1)} %slice.91), channel_id=1, source_target_pairs={{0,3},{1,0},{2,1},{3,2},{4,7},{5,4},{6,5},{7,6},{8,11},{9,8},{10,9... | collective-permute-start | bytes 2949128 | tf_op jit(solution)/shard_map/ppermute | solution.py:154
  116.1 1.9 copy-start.13
  116.1 48.0 %collective-permute-start.10 = (bf16[192,2560]{1,0:T(8,128)(2,1)S(1)}, bf16[192,2560]{1,0:T(8,128)(2,1)S(1)}, u32[]{:S(2)}, u32[]{:S(2)}) collective-permute-start(bf16[192,2560]{1,0:T(8,128)(2,1)S(1)} %slice.90), channel_id=1, source_target_pairs={{0,1},{1,2},{2,3},{3,0},{4,5},{5,6},{6,7},{7,4},{8,9},{9,10},{10,1... | collective-permute-start | bytes 2949128 | tf_op jit(solution)/shard_map/ppermute | solution.py:153
  165.5 12.2 %copy-start.3 = (f32[384,1280]{1,0:T(8,128)S(1)}, f32[384,1280]{1,0:T(8,128)}, u32[]{:S(2)}) copy-start(f32[384,1280]{1,0:T(8,128)} %get-tuple-element.20) | copy-start | bytes 5898244
  177.8 4.6 %copy-start.8 = (f32[1280]{0:T(1024)S(1)}, f32[1280]{0:T(1024)}, u32[]{:S(2)}) copy-start(f32[1280]{0:T(1024)} %param.24) | copy-start | bytes 15364
  177.8 4.6 %copy-start.9 = (f32[1280]{0:T(1024)S(1)}, f32[1280]{0:T(1024)}, u32[]{:S(2)}) copy-start(f32[1280]{0:T(1024)} %param.25) | copy-start | bytes 15364
  183.0 22.3 %collective-permute-start.12 = (bf16[1,64,1280]{2,1,0:T(8,128)(2,1)S(1)}, bf16[1,64,1280]{2,1,0:T(8,128)(2,1)S(1)}, u32[]{:S(2)}, u32[]{:S(2)}) collective-permute-start(bf16[1,64,1280]{2,1,0:T(8,128)(2,1)S(1)} %get-tuple-element.32), channel_id=1, source_target_pairs={{0,1},{1,2},{2,3},{3,4},{4,5},{5,6},{6,7},{8,9},{9,10},{10,11},{11... | collective-permute-start | bytes 491528 | tf_op jit(solution)/shard_map/ppermute | solution.py:189
  185.5 18.5 %collective-permute-start.13 = (bf16[1,64,1280]{2,1,0:T(8,128)(2,1)S(1)}, bf16[1,64,1280]{2,1,0:T(8,128)(2,1)S(1)}, u32[]{:S(2)}, u32[]{:S(2)}) collective-permute-start(bf16[1,64,1280]{2,1,0:T(8,128)(2,1)S(1)} %get-tuple-element.33), channel_id=1, source_target_pairs={{1,0},{2,1},{3,2},{4,3},{5,4},{6,5},{7,6},{9,8},{10,9},{11,10},{12... | collective-permute-start | bytes 491528 | tf_op jit(solution)/shard_map/ppermute | solution.py:192
  194.0 0.7 copy-start.10
  194.7 12.0 %slice-start = ((s8[14745600]{0:T(1024)(128)(4,1)}), s8[4194304]{0:T(1024)(128)(4,1)S(1)}, s32[]{:S(2)}) async-start(s8[14745600]{0:T(1024)(128)(4,1)} %bitcast.91), calls=%async_computation | async-start | bytes 8388608
  194.7 12.0 %slice-start.1 = ((s8[14745600]{0:T(1024)(128)(4,1)}), s8[4194304]{0:T(1024)(128)(4,1)S(1)}, s32[]{:S(2)}) async-start(s8[14745600]{0:T(1024)(128)(4,1)} %bitcast.91), calls=%async_computation.1 | async-start | bytes 8388608
  194.7 12.0 %slice-start.2 = ((s8[14745600]{0:T(1024)(128)(4,1)}), s8[2162688]{0:T(1024)(128)(4,1)S(1)}, s32[]{:S(2)}) async-start(s8[14745600]{0:T(1024)(128)(4,1)} %bitcast.91), calls=%async_computation.2 | async-start | bytes 4325376
  203.8 3.0 %slice-start.3 = ((s8[14745600]{0:T(1024)(128)(4,1)}), s8[4194304]{0:T(1024)(128)(4,1)S(1)}, s32[]{:S(2)}) async-start(s8[14745600]{0:T(1024)(128)(4,1)} %bitcast.91), calls=%async_computation.3 | async-start | bytes 8388608
  212.5 0.7 copy-start.11
  212.5 2.1 copy-start.1

commit v4 on v3

--- a/solution.py
+++ b/solution.py
@@ -11,6 +11,7 @@
 HEADS = 20
 GROUPS = 32
 W = 64
+HEAD_DIM = 64
 YRING = 4
 
 
@@ -44,13 +45,21 @@
     ]
 
 
-def attn_kernel(*refs, n_pieces):
+def attn_kernel(*refs, n_pieces, carry, final):
     q_ref = refs[0]
-    piece_refs = refs[1 : 1 + 2 * n_pieces]
-    m_ref, l_ref, acc_ref = refs[1 + 2 * n_pieces :]
-    head_dim = q_ref.shape[1] // 2
+    pos = 1
+    if carry:
+        mp_ref, lp_ref, accp_ref = refs[pos : pos + 3]
+        pos += 3
+    if final:
+        h_ref = refs[pos]
+        pos += 1
+    piece_refs = refs[pos : pos + 2 * n_pieces]
+    out_refs = refs[pos + 2 * n_pieces :]
+    head_dim = HEAD_DIM
+    rows = q_ref.shape[0]
     dims = (((1,), (1,)), ((), ()))
-    for hh in range(2):
+    for hh in range(q_ref.shape[1] // head_dim):
         lanes = slice(hh * head_dim, (hh + 1) * head_dim)
         qh = q_ref[:, lanes]
         scores = [
@@ -60,8 +69,15 @@
             for i in range(n_pieces)
         ]
         m = functools.reduce(jnp.maximum, [jnp.max(s, axis=1, keepdims=True) for s in scores])
-        total = None
-        acc = None
+        if carry:
+            m_prev = jnp.max(mp_ref[:, lanes], axis=1, keepdims=True)
+            m = jnp.maximum(m, m_prev)
+            rescale = jnp.exp(m_prev - m)
+            total = jnp.max(lp_ref[:, lanes], axis=1, keepdims=True) * rescale
+            acc = accp_ref[:, lanes] * rescale
+        else:
+            total = None
+            acc = None
         for i in range(n_pieces):
             w = jnp.exp(scores[i] - m)
             part = jnp.sum(w, axis=1, keepdims=True)
@@ -72,29 +88,53 @@
             )
             total = part if total is None else total + part
             acc = pv if acc is None else acc + pv
-        rows = q_ref.shape[0]
-        m_ref[:, lanes] = jnp.broadcast_to(m, (rows, head_dim))
-        l_ref[:, lanes] = jnp.broadcast_to(total, (rows, head_dim))
-        acc_ref[:, lanes] = acc
-
-
-def attention_partial(query, pieces):
+        if final:
+            (o_ref,) = out_refs
+            o_ref[:, lanes] = (h_ref[:, lanes].astype(jnp.float32) + acc / total).astype(
+                jnp.bfloat16
+            )
+        else:
+            m_ref, l_ref, acc_ref = out_refs
+            m_ref[:, lanes] = jnp.broadcast_to(m, (rows, head_dim))
+            l_ref[:, lanes] = jnp.broadcast_to(total, (rows, head_dim))
+            acc_ref[:, lanes] = acc
+
+
+def attention_partial(query, pieces, carry=None, hidden=None, block=128):
     tok_rows, width = query.shape
-    pairs = width // 128
-    in_specs = [pl.BlockSpec((tok_rows, 128), lambda h: (0, h))]
+    steps = width // block
+    in_specs = [pl.BlockSpec((tok_rows, block), lambda h: (0, h))]
     args = [query]
+    if carry is not None:
+        in_specs += [pl.BlockSpec((tok_rows, block), lambda h: (0, h))] * 3
+        args += list(carry)
+    if hidden is not None:
+        in_specs.append(pl.BlockSpec((tok_rows, block), lambda h: (0, h)))
+        args.append(hidden)
     for keys, kblk, values, vblk in pieces:
-        in_specs.append(pl.BlockSpec((keys.shape[0], 128), lambda h, o=kblk: (0, h + o)))
-        in_specs.append(pl.BlockSpec((values.shape[0], 128), lambda h, o=vblk: (0, h + o)))
+        ko = kblk * 128 // block
+        vo = vblk * 128 // block
+        in_specs.append(pl.BlockSpec((keys.shape[0], block), lambda h, o=ko: (0, h + o)))
+        in_specs.append(pl.BlockSpec((values.shape[0], block), lambda h, o=vo: (0, h + o)))
         args += [keys, values]
-    out_spec = pl.BlockSpec((tok_rows, 128), lambda h: (0, h))
-    out_shape = jax.ShapeDtypeStruct((tok_rows, width), jnp.float32)
+    out_spec = pl.BlockSpec((tok_rows, block), lambda h: (0, h))
+    if hidden is not None:
+        out_specs = out_spec
+        out_shape = jax.ShapeDtypeStruct((tok_rows, width), jnp.bfloat16)
+    else:
+        out_specs = [out_spec] * 3
+        out_shape = [jax.ShapeDtypeStruct((tok_rows, width), jnp.float32)] * 3
     return pl.pallas_call(
-        functools.partial(attn_kernel, n_pieces=len(pieces)),
-        grid=(pairs,),
+        functools.partial(
+            attn_kernel,
+            n_pieces=len(pieces),
+            carry=carry is not None,
+            final=hidden is not None,
+        ),
+        grid=(steps,),
         in_specs=in_specs,
-        out_specs=[out_spec] * 3,
-        out_shape=[out_shape] * 3,
+        out_specs=out_specs,
+        out_shape=out_shape,
         compiler_params=pltpu.CompilerParams(vmem_limit_bytes=48 * 1024 * 1024),
     )(*args)
 
@@ -171,15 +211,9 @@
         [(a, 0, a, vblk) for a in (far, partner_left, partner_right)],
         [(partner_far, 0, partner_far, vblk)],
     ]
-    partials = []
-    for pieces in sets:
-        partials.append(attention_partial(query, pieces))
-    m = functools.reduce(jnp.maximum, [p[0] for p in partials])
-    scales = [jnp.exp(p[0] - m) for p in partials]
-    acc = sum(p[2] * r for p, r in zip(partials, scales))
-    total = sum(p[1] * r for p, r in zip(partials, scales))
-    attended = acc / total
-    updated = (hidden_in.astype(jnp.float32) + attended).astype(jnp.bfloat16)
+    state = attention_partial(query, sets[0])
+    state = attention_partial(query, sets[1], carry=state)
+    updated = attention_partial(query, sets[2], carry=state, hidden=hidden_in, block=256)
     total_conv = stale_all[1]
     totals_conv = total_conv - own_stale[1] + group_moments(updated, GROUPS)
     normed_conv = group_normalize(updated, totals_conv, count, gain_conv, bias_conv, GROUPS)

time: 215 us -> 226 us (1.051)
  Pallas kernels: 55.4 us -> 63.5 us
  other arithmetic: 12 us -> 8.81 us
  waiting for transfers between devices: 85.6 us -> 88.2 us
    ppermute x1, waiting for transfers between devices: 0.01 us -> 42.9 us  [body(): from_left = lax.ppermute(kv, 'patch', perm(1, 0))]
    ppermute x1, waiting for transfers between devices: 43.1 us -> 1.53 us  [body(): partner = lax.ppermute(kv, 'patch', perm(0, 1))]
    pallas_call x3, Pallas kernels: 55.4 us -> 63.5 us  [attention_partial(): pl.pallas_call(functools.partial(attn_kernel, n_pieces=len(pieces), carry...]
    reduce_sum x4, other arithmetic: 5.53 us -> 2 us  [group_moments(): jnp.sum(values, axis=(0, 2))]
  transfers between devices with their start and end apart: 14 -> 14, of which waited for: 4 -> 6; matrix products, arithmetic and copies ran while one was open for 13% -> 9% of each run, Pallas kernels for 20% -> 23%
where the time goes in v4:
time: 226 us; the launch traced here: 224 us
  waiting for transfers between devices  88.2 us (39%)
  Pallas kernels  63.5 us (28%)
  starting transfers between devices  26.5 us (12%)
  matrix products  20.1 us (9%)
  local copies, waits for them, and re-layouts  15.4 us (7%)
  other arithmetic  8.81 us (4%)
    pallas_call x3, Pallas kernels, attention_partial(): pl.pallas_call(functools.partial(attn_kernel, n_pieces=len(pieces), carry...  63.5 us
    ppermute x1, waiting for transfers between devices, body(): from_left = lax.ppermute(kv, 'patch', perm(1, 0))  42.9 us
    ppermute x2, waiting for transfers between devices, body(): stale_all = stale_all + lax.ppermute(stale_all, 'patch', pairs)  41.5 us
    conv_general_dilated x3, matrix products, conv_rows(): lax.conv_general_dilated(cells[None], conv_weight, (1, 1), ((0, 0), (1, 1...  14.5 us
    ppermute x1, starting transfers between devices, body(): lax.ppermute(activated[:1], 'patch', [(i + 1, i) for i in range(count_p -...  7.54 us
  transfers between devices with their start and end apart: 14, of which 6 were waited for; matrix products, arithmetic and copies ran while one was open for 9% of the time, Pallas kernels for 23%

profile of v4, /device:TPU:64, one launch (start us, length us, event | category | flops | bytes accessed | tf_op | source)
XLA Modules:
  0.0 223.9 jit_solution(2524702605924957003)
XLA Ops:
  0.0 2.4 %constant_dynamic-update-slice_fusion.1 = bf16[384,2560]{1,0:T(8,128)(2,1)} fusion(bf16[384,1280]{1,0:T(8,128)(2,1)} %param.16), kind=kLoop, calls=%fused_computation.65 | loop fusion | bytes 1966080
  2.4 1.0 constant_dynamic-update-slice_fusion
  3.5 1.6 collective-permute-start.3
  5.0 1.7 collective-permute-start.4
  6.7 42.9 %collective-permute-done.3.refs_3_.refs_4_ = bf16[384,2560]{1,0:T(8,128)(2,1)} collective-permute-done((bf16[384,2560]{1,0:T(8,128)(2,1)}, bf16[384,2560]{1,0:T(8,128)(2,1)}, u32[]{:S(2)}, u32[]{:S(2)}) %collective-permute-start.3) | collective-permute-done | bytes 1966112 | tf_op jit(solution)/shard_map/ppermute | solution.py:186
  49.6 1.5 collective-permute-done.5.refs_7_.refs_8_
  51.1 1.7 collective-permute-start.9
  52.9 0.4 collective-permute-start
  53.9 1.5 convert_reduce_fusion.1
  55.5 39.4 %collective-permute-done = f32[2,2,32]{2,1,0:T(2,128)S(1)} collective-permute-done((f32[2,2,32]{2,1,0:T(2,128)S(1)}, f32[2,2,32]{2,1,0:T(2,128)S(1)}, u32[]{:S(2)}, u32[]{:S(2)}) %collective-permute-start) | collective-permute-done | bytes 544 | tf_op jit(solution)/shard_map/ppermute | solution.py:183
  94.9 2.9 %collective-permute-start.1 = (f32[2,2,32]{2,1,0:T(2,128)S(1)}, f32[2,2,32]{2,1,0:T(2,128)S(1)}, u32[]{:S(2)}, u32[]{:S(2)}) collective-permute-start(f32[2,2,32]{2,1,0:T(2,128)S(1)} %add.59), channel_id=1, source_target_pairs={{0,2},{1,3},{2,0},{3,1},{4,6},{5,7},{6,4},{7,5},{8,10},{9,11},{10,... | collective-permute-start | bytes 1544 | tf_op jit(solution)/shard_map/ppermute | solution.py:183
  97.9 2.1 collective-permute-done.1
  100.0 2.1 collective-permute-start.2
  102.1 1.3 convolution_reduce_fusion
  103.5 0.1 reduce_sum.60
  103.7 0.1 reduce_sum.66
  103.8 1.3 collective-permute-done.2
  105.5 1.4 slice.88
  106.9 1.3 slice.89
  108.2 3.3 %collective-permute-start.7 = (bf16[192,2560]{1,0:T(8,128)(2,1)S(1)}, bf16[192,2560]{1,0:T(8,128)(2,1)S(1)}, u32[]{:S(2)}, u32[]{:S(2)}) collective-permute-start(bf16[192,2560]{1,0:T(8,128)(2,1)S(1)} %slice.89), channel_id=1, source_target_pairs={{0,3},{1,0},{2,1},{3,2},{4,7},{5,4},{6,5},{7,6},{8,11},{9,8},{10,9... | collective-permute-start | bytes 2949128 | tf_op jit(solution)/shard_map/ppermute | solution.py:190
  111.5 1.5 fusion.1.refs_0_
  113.0 1.4 slice.90
  114.5 1.3 slice.91
  115.8 3.3 %collective-permute-start.11 = (bf16[192,2560]{1,0:T(8,128)(2,1)S(1)}, bf16[192,2560]{1,0:T(8,128)(2,1)S(1)}, u32[]{:S(2)}, u32[]{:S(2)}) collective-permute-start(bf16[192,2560]{1,0:T(8,128)(2,1)S(1)} %slice.91), channel_id=1, source_target_pairs={{0,3},{1,0},{2,1},{3,2},{4,7},{5,4},{6,5},{7,6},{8,11},{9,8},{10,9... | collective-permute-start | bytes 2949128 | tf_op jit(solution)/shard_map/ppermute | solution.py:194
  119.1 1.4 convolution_convert_fusion.refs_2_
  120.5 1.5 convolution_convert_fusion.1.refs_1_
  122.0 23.8 %shard_map.145 = (f32[384,1280]{1,0:T(8,128)S(1)}, f32[384,1280]{1,0:T(8,128)}, f32[384,1280]{1,0:T(8,128)}) custom-call(bf16[384,1280]{1,0:T(8,128)(2,1)S(1)} %fusion.1.refs_0_, bf16[384,1280]{1,0:T(8,128)(2,1)S(1)} %convolution_convert_fusion.1.refs_1_, bf16[384,1280]{1,0:T(8,128)(2,1)S(1)} %convolution_convert_fusion.refs_2_, ...), custom_call_target="tpu_custom_call" | custom-call | tf_op jit(solution)/shard_map/pallas_call | solution.py:127
  145.8 1.6 pad_maximum_fusion.refs_4_.refs_5_
  147.4 0.4 copy-done.4
  147.8 28.4 %shard_map.146 = (f32[384,1280]{1,0:T(8,128)S(1)}, f32[384,1280]{1,0:T(8,128)S(1)}, f32[384,1280]{1,0:T(8,128)}) custom-call(bf16[384,1280]{1,0:T(8,128)(2,1)S(1)} %fusion.1.refs_0_, f32[384,1280]{1,0:T(8,128)} %copy-done.4, f32[384,1280]{1,0:T(8,128)} %get-tuple-element.12.refs_2_, f32[384,1280]{1,0:T(8,128)} %get-tuple-element.13.refs_3_, ...), custom_call_target="tpu_custom_call" | custom-call | tf_op jit(solution)/shard_map/pallas_call | solution.py:127
  176.2 1.5 pad_maximum_fusion.1.refs_5_.refs_6_
  177.7 0.4 copy-done.3
  178.1 11.4 %shard_map.147 = bf16[384,1280]{1,0:T(8,128)(2,1)S(1)} custom-call(bf16[384,1280]{1,0:T(8,128)(2,1)S(1)} %fusion.1.refs_0_, f32[384,1280]{1,0:T(8,128)S(1)} %get-tuple-element.14.refs_1_, f32[384,1280]{1,0:T(8,128)} %copy-done.3, f32[384,1280]{1,0:T(8,128)} %get-tuple-element.16.refs_3_, bf16[384,1280]{1,0:T(8,128)(2,1)S(1)} %copy-done.2, ...), custom_call_target="tpu_custom_call" | custom-call | tf_op jit(solution)/shard_map/pallas_call | solution.py:127
  189.4 0.3 convert_reduce_fusion
  189.8 0.1 reduce_sum.82
  190.0 0.1 reduce_sum.85
  190.2 0.1 reshape.48
  190.5 0.6 fusion.12
  191.2 0.6 copy.50
  191.7 0.2 pad.2
  192.0 0.2 copy.52
  192.3 0.4 copy-done.11
  192.7 9.3 %fusion.22 = f32[4,8,9,640]{3,1,2,0:T(8,128)S(1)} fusion(bf16[3,3,1280,640]{3,2,1,0:T(8,128)(2,1)} %param.26, bf16[6,1,7,2,1280]{4,2,3,0,1:T(8,128)(2,1)S(1)} %slice.98, bf16[6,1,8,9,1280]{4,2,3,0,1:T(8,128)(2,1)S(1)} %copy.52, pred[8,9]{0,1:T(8,128)(4,1)S(1)} %copy-done.11), kind=kOutput, calls=%fused_computation.35 | convolution fusion | flops 4250972160 | bytes 16803912 | tf_op jit(solution)/shard_map/conv_general_dilated | solution.py:229
  202.0 0.2 copy.53
  202.2 0.3 copy.46
  202.6 1.9 collective-permute-start.12
  204.5 0.3 copy.54
  204.8 7.5 %collective-permute-start.13 = (bf16[1,64,1280]{2,1,0:T(8,128)(2,1)S(1)}, bf16[1,64,1280]{2,1,0:T(8,128)(2,1)S(1)}, u32[]{:S(2)}, u32[]{:S(2)}) collective-permute-start(bf16[1,64,1280]{2,1,0:T(8,128)(2,1)S(1)} %get-tuple-element.26), channel_id=1, source_target_pairs={{1,0},{2,1},{3,2},{4,3},{5,4},{6,5},{7,6},{9,8},{10,9},{11,10},{12... | collective-permute-start | bytes 491528 | tf_op jit(solution)/shard_map/ppermute | solution.py:226
  212.5 0.9 collective-permute-done.12
  213.4 0.3 copy.45
  213.7 0.7 maximum_bitcast_fusion
  214.3 0.3 pad
  214.8 2.6 %convolution_select_fusion.1 = f32[1,8,9,640]{3,1,2,0:T(8,128)S(1)} fusion(bf16[3,3,1280,640]{3,2,1,0:T(8,128)(2,1)S(1)} %bitcast.92, bf16[3,1,7,2,1280]{4,2,3,0,1:T(8,128)(2,1)S(1)} %slice.96, bf16[3,1,8,9,1280]{4,2,3,0,1:T(8,128)(2,1)S(1)} %copy.48, pred[8,9]{0,1:T(8,128)(4,1)S(1)} %copy-done.11), kind=kOutput, calls=%fused_computation.37 | convolution fusion | flops 1063756800 | bytes 15590472 | tf_op jit(solution)/shard_map/conv_general_dilated | solution.py:229
  217.3 0.2 copy.49
  217.6 0.3 copy.55
  217.8 0.7 maximum_bitcast_fusion.1
  218.5 0.3 pad.4
  218.9 2.6 %convolution_select_fusion = f32[1,8,9,640]{3,1,2,0:T(8,128)S(1)} fusion(bf16[3,3,1280,640]{3,2,1,0:T(8,128)(2,1)S(1)} %bitcast.92, bf16[3,1,7,2,1280]{4,2,3,0,1:T(8,128)(2,1)S(1)} %slice.102, bf16[3,1,8,9,1280]{4,2,3,0,1:T(8,128)(2,1)S(1)} %copy.57, pred[8,9]{0,1:T(8,128)(4,1)S(1)} %copy-done.11), kind=kOutput, calls=%fused_computation.36 | convolution fusion | flops 1063756800 | bytes 15590472 | tf_op jit(solution)/shard_map/conv_general_dilated | solution.py:229
  221.4 0.2 copy.58
  221.6 0.1 slice_bitcast_fusion.1
  221.8 0.4 pad_maximum_fusion.2
  222.2 0.2 copy.59
  222.4 0.9 fusion.26
  223.3 0.6 copy-done.1
  (79 shorter events, 1.7 us)
Async XLA Ops:
  0.0 111.5 %copy-start = (bf16[1280,1280]{1,0:T(8,128)(2,1)S(1)}, bf16[1280,1280]{1,0:T(8,128)(2,1)}, u32[]{:S(2)}) copy-start(bf16[1280,1280]{1,0:T(8,128)(2,1)} %param.21) | copy-start | bytes 9830404
  0.0 2.4 %copy-start.5 = (bf16[384,1280]{1,0:T(8,128)(2,1)S(1)}, bf16[384,1280]{1,0:T(8,128)(2,1)}, u32[]{:S(2)}) copy-start(bf16[384,1280]{1,0:T(8,128)(2,1)} %param.17) | copy-start | bytes 2949124
  0.0 52.9 %copy-start.6 = (f32[6,2,2,32]{3,2,1,0:T(2,128)S(1)}, f32[6,2,2,32]{3,2,1,0:T(2,128)}, u32[]{:S(2)}) copy-start(f32[6,2,2,32]{3,2,1,0:T(2,128)} %param.18) | copy-start | bytes 9220
  2.4 103.0 %copy-start.7 = (f32[1280]{0:T(1024)S(1)}, f32[1280]{0:T(1024)}, u32[]{:S(2)}) copy-start(f32[1280]{0:T(1024)} %param.19) | copy-start | bytes 15364
  2.4 103.0 %copy-start.8 = (f32[1280]{0:T(1024)S(1)}, f32[1280]{0:T(1024)}, u32[]{:S(2)}) copy-start(f32[1280]{0:T(1024)} %param.20) | copy-start | bytes 15364
  3.5 46.1 %collective-permute-start.3 = (bf16[384,2560]{1,0:T(8,128)(2,1)}, bf16[384,2560]{1,0:T(8,128)(2,1)}, u32[]{:S(2)}, u32[]{:S(2)}) collective-permute-start(bf16[384,2560]{1,0:T(8,128)(2,1)} %constant_dynamic-update-slice_fusion), channel_id=1, source_target_pairs={{0,1},{1,2},{2,3},{3,0},{4,5},{5,6},{6,7},{7,4},{8,9},{9,10},{10,1... | collective-permute-start | bytes 5898248 | tf_op jit(solution)/shard_map/ppermute | solution.py:186
  5.0 46.1 %collective-permute-start.5 = (bf16[384,2560]{1,0:T(8,128)(2,1)}, bf16[384,2560]{1,0:T(8,128)(2,1)}, u32[]{:S(2)}, u32[]{:S(2)}) collective-permute-start(bf16[384,2560]{1,0:T(8,128)(2,1)} %constant_dynamic-update-slice_fusion), channel_id=1, source_target_pairs={{0,4},{1,5},{2,6},{3,7},{4,0},{5,1},{6,2},{7,3},{8,12},{9,13},{10,... | collective-permute-start | bytes 5898248 | tf_op jit(solution)/shard_map/ppermute | solution.py:188
  5.0 101.9 %collective-permute-start.4 = (bf16[384,2560]{1,0:T(8,128)(2,1)}, bf16[384,2560]{1,0:T(8,128)(2,1)}, u32[]{:S(2)}, u32[]{:S(2)}) collective-permute-start(bf16[384,2560]{1,0:T(8,128)(2,1)} %constant_dynamic-update-slice_fusion), channel_id=1, source_target_pairs={{0,3},{1,0},{2,1},{3,2},{4,7},{5,4},{6,5},{7,6},{8,11},{9,8},{10,9... | collective-permute-start | bytes 5898248 | tf_op jit(solution)/shard_map/ppermute | solution.py:187
  49.6 63.4 %collective-permute-start.8 = (bf16[384,2560]{1,0:T(8,128)(2,1)}, bf16[384,2560]{1,0:T(8,128)(2,1)}, u32[]{:S(2)}, u32[]{:S(2)}) collective-permute-start(bf16[384,2560]{1,0:T(8,128)(2,1)} %collective-permute-done.3.refs_3_.refs_4_), channel_id=1, source_target_pairs={{0,4},{1,5},{2,6},{3,7},{4,0},{5,1},{6,2},{7,3},{8,12},{9,13},{10,... | collective-permute-start | bytes 5898248 | tf_op jit(solution)/shard_map/ppermute | solution.py:191
  51.1 63.3 %collective-permute-start.9 = (bf16[384,2560]{1,0:T(8,128)(2,1)}, bf16[384,2560]{1,0:T(8,128)(2,1)}, u32[]{:S(2)}, u32[]{:S(2)}) collective-permute-start(bf16[384,2560]{1,0:T(8,128)(2,1)} %collective-permute-done.5.refs_7_.refs_8_), channel_id=1, source_target_pairs={{0,3},{1,0},{2,1},{3,2},{4,7},{5,4},{6,5},{7,6},{8,11},{9,8},{10,9... | collective-permute-start | bytes 5898248 | tf_op jit(solution)/shard_map/ppermute | solution.py:192
  52.9 42.0 %collective-permute-start = (f32[2,2,32]{2,1,0:T(2,128)S(1)}, f32[2,2,32]{2,1,0:T(2,128)S(1)}, u32[]{:S(2)}, u32[]{:S(2)}) collective-permute-start(f32[2,2,32]{2,1,0:T(2,128)S(1)} %reduce_sum.54), channel_id=1, source_target_pairs={{0,1},{1,0},{2,3},{3,2},{4,5},{5,4},{6,7},{7,6},{8,9},{9,8},{10,11... | collective-permute-start | bytes 1544 | tf_op jit(solution)/shard_map/ppermute | solution.py:183
  94.9 5.1 %collective-permute-start.1 = (f32[2,2,32]{2,1,0:T(2,128)S(1)}, f32[2,2,32]{2,1,0:T(2,128)S(1)}, u32[]{:S(2)}, u32[]{:S(2)}) collective-permute-start(f32[2,2,32]{2,1,0:T(2,128)S(1)} %add.59), channel_id=1, source_target_pairs={{0,2},{1,3},{2,0},{3,1},{4,6},{5,7},{6,4},{7,5},{8,10},{9,11},{10,... | collective-permute-start | bytes 1544 | tf_op jit(solution)/shard_map/ppermute | solution.py:183
  100.0 5.1 %collective-permute-start.2 = (f32[2,2,32]{2,1,0:T(2,128)S(1)}, f32[2,2,32]{2,1,0:T(2,128)S(1)}, u32[]{:S(2)}, u32[]{:S(2)}) collective-permute-start(f32[2,2,32]{2,1,0:T(2,128)S(1)} %add.60), channel_id=1, source_target_pairs={{0,4},{1,5},{2,6},{3,7},{4,0},{5,1},{6,2},{7,3},{8,12},{9,13},{10,... | collective-permute-start | bytes 1544 | tf_op jit(solution)/shard_map/ppermute | solution.py:184
  105.5 6.0 %copy-start.2 = (bf16[384,1280]{1,0:T(8,128)(2,1)S(1)}, bf16[384,1280]{1,0:T(8,128)(2,1)}, u32[]{:S(2)}) copy-start(bf16[384,1280]{1,0:T(8,128)(2,1)} %refs_4_.1) | copy-start | bytes 2949124
  106.8 38.9 %collective-permute-start.6 = (bf16[192,2560]{1,0:T(8,128)(2,1)S(1)}, bf16[192,2560]{1,0:T(8,128)(2,1)S(1)}, u32[]{:S(2)}, u32[]{:S(2)}) collective-permute-start(bf16[192,2560]{1,0:T(8,128)(2,1)S(1)} %slice.88), channel_id=1, source_target_pairs={{0,1},{1,2},{2,3},{3,0},{4,5},{5,6},{6,7},{7,4},{8,9},{9,10},{10,1... | collective-permute-start | bytes 2949128 | tf_op jit(solution)/shard_map/ppermute | solution.py:189
  108.2 37.6 %collective-permute-start.7 = (bf16[192,2560]{1,0:T(8,128)(2,1)S(1)}, bf16[192,2560]{1,0:T(8,128)(2,1)S(1)}, u32[]{:S(2)}, u32[]{:S(2)}) collective-permute-start(bf16[192,2560]{1,0:T(8,128)(2,1)S(1)} %slice.89), channel_id=1, source_target_pairs={{0,3},{1,0},{2,1},{3,2},{4,7},{5,4},{6,5},{7,6},{8,11},{9,8},{10,9... | collective-permute-start | bytes 2949128 | tf_op jit(solution)/shard_map/ppermute | solution.py:190
  113.0 6.1 %copy-start.13 = (bf16[1280,1280]{1,0:T(8,128)(2,1)S(1)}, bf16[1280,1280]{1,0:T(8,128)(2,1)}, u32[]{:S(2)}) copy-start(bf16[1280,1280]{1,0:T(8,128)(2,1)} %param.23) | copy-start | bytes 9830404
  114.4 61.8 %collective-permute-start.10 = (bf16[192,2560]{1,0:T(8,128)(2,1)S(1)}, bf16[192,2560]{1,0:T(8,128)(2,1)S(1)}, u32[]{:S(2)}, u32[]{:S(2)}) collective-permute-start(bf16[192,2560]{1,0:T(8,128)(2,1)S(1)} %slice.90), channel_id=1, source_target_pairs={{0,1},{1,2},{2,3},{3,0},{4,5},{5,6},{6,7},{7,4},{8,9},{9,10},{10,1... | collective-permute-start | bytes 2949128 | tf_op jit(solution)/shard_map/ppermute | solution.py:193
  115.8 4.8 %copy-start.14 = (bf16[1280,1280]{1,0:T(8,128)(2,1)S(1)}, bf16[1280,1280]{1,0:T(8,128)(2,1)}, u32[]{:S(2)}) copy-start(bf16[1280,1280]{1,0:T(8,128)(2,1)} %param.22) | copy-start | bytes 9830404
  115.8 60.4 %collective-permute-start.11 = (bf16[192,2560]{1,0:T(8,128)(2,1)S(1)}, bf16[192,2560]{1,0:T(8,128)(2,1)S(1)}, u32[]{:S(2)}, u32[]{:S(2)}) collective-permute-start(bf16[192,2560]{1,0:T(8,128)(2,1)S(1)} %slice.91), channel_id=1, source_target_pairs={{0,3},{1,0},{2,1},{3,2},{4,7},{5,4},{6,5},{7,6},{8,11},{9,8},{10,9... | collective-permute-start | bytes 2949128 | tf_op jit(solution)/shard_map/ppermute | solution.py:194
  145.8 2.0 copy-start.4
  176.2 1.9 copy-start.3
  178.1 12.5 %copy-start.9 = (f32[1280]{0:T(1024)S(1)}, f32[1280]{0:T(1024)}, u32[]{:S(2)}) copy-start(f32[1280]{0:T(1024)} %param.24) | copy-start | bytes 15364
  178.1 12.5 %copy-start.10 = (f32[1280]{0:T(1024)S(1)}, f32[1280]{0:T(1024)}, u32[]{:S(2)}) copy-start(f32[1280]{0:T(1024)} %param.25) | copy-start | bytes 15364
  192.0 0.7 copy-start.11
  192.0 22.7 %slice-start = ((s8[14745600]{0:T(1024)(128)(4,1)}), s8[4194304]{0:T(1024)(128)(4,1)S(1)}, s32[]{:S(2)}) async-start(s8[14745600]{0:T(1024)(128)(4,1)} %bitcast.91), calls=%async_computation | async-start | bytes 8388608
  192.7 22.1 %slice-start.1 = ((s8[14745600]{0:T(1024)(128)(4,1)}), s8[4194304]{0:T(1024)(128)(4,1)S(1)}, s32[]{:S(2)}) async-start(s8[14745600]{0:T(1024)(128)(4,1)} %bitcast.91), calls=%async_computation.1 | async-start | bytes 8388608
  192.7 22.1 %slice-start.2 = ((s8[14745600]{0:T(1024)(128)(4,1)}), s8[4194304]{0:T(1024)(128)(4,1)S(1)}, s32[]{:S(2)}) async-start(s8[14745600]{0:T(1024)(128)(4,1)} %bitcast.91), calls=%async_computation.2 | async-start | bytes 8388608
  192.7 22.1 %slice-start.3 = ((s8[14745600]{0:T(1024)(128)(4,1)}), s8[2162688]{0:T(1024)(128)(4,1)S(1)}, s32[]{:S(2)}) async-start(s8[14745600]{0:T(1024)(128)(4,1)} %bitcast.91), calls=%async_computation.3 | async-start | bytes 4325376
  202.6 10.8 %collective-permute-start.12 = (bf16[1,64,1280]{2,1,0:T(8,128)(2,1)S(1)}, bf16[1,64,1280]{2,1,0:T(8,128)(2,1)S(1)}, u32[]{:S(2)}, u32[]{:S(2)}) collective-permute-start(bf16[1,64,1280]{2,1,0:T(8,128)(2,1)S(1)} %get-tuple-element.25), channel_id=1, source_target_pairs={{0,1},{1,2},{2,3},{3,4},{4,5},{5,6},{6,7},{8,9},{9,10},{10,11},{11... | collective-permute-start | bytes 491528 | tf_op jit(solution)/shard_map/ppermute | solution.py:223
  204.8 12.7 %collective-permute-start.13 = (bf16[1,64,1280]{2,1,0:T(8,128)(2,1)S(1)}, bf16[1,64,1280]{2,1,0:T(8,128)(2,1)S(1)}, u32[]{:S(2)}, u32[]{:S(2)}) collective-permute-start(bf16[1,64,1280]{2,1,0:T(8,128)(2,1)S(1)} %get-tuple-element.26), channel_id=1, source_target_pairs={{1,0},{2,1},{3,2},{4,3},{5,4},{6,5},{7,6},{9,8},{10,9},{11,10},{12... | collective-permute-start | bytes 491528 | tf_op jit(solution)/shard_map/ppermute | solution.py:226
  221.7 0.7 copy-start.12
  221.8 2.1 copy-start.1

commit v5 on v3

--- a/solution.py
+++ b/solution.py
@@ -11,6 +11,7 @@
 HEADS = 20
 GROUPS = 32
 W = 64
+HEAD_DIM = 64
 YRING = 4
 
 
@@ -48,9 +49,9 @@
     q_ref = refs[0]
     piece_refs = refs[1 : 1 + 2 * n_pieces]
     m_ref, l_ref, acc_ref = refs[1 + 2 * n_pieces :]
-    head_dim = q_ref.shape[1] // 2
+    head_dim = HEAD_DIM
     dims = (((1,), (1,)), ((), ()))
-    for hh in range(2):
+    for hh in range(q_ref.shape[1] // head_dim):
         lanes = slice(hh * head_dim, (hh + 1) * head_dim)
         qh = q_ref[:, lanes]
         scores = [
@@ -78,16 +79,18 @@
         acc_ref[:, lanes] = acc
 
 
-def attention_partial(query, pieces):
+def attention_partial(query, pieces, block=128):
     tok_rows, width = query.shape
-    pairs = width // 128
-    in_specs = [pl.BlockSpec((tok_rows, 128), lambda h: (0, h))]
+    pairs = width // block
+    in_specs = [pl.BlockSpec((tok_rows, block), lambda h: (0, h))]
     args = [query]
     for keys, kblk, values, vblk in pieces:
-        in_specs.append(pl.BlockSpec((keys.shape[0], 128), lambda h, o=kblk: (0, h + o)))
-        in_specs.append(pl.BlockSpec((values.shape[0], 128), lambda h, o=vblk: (0, h + o)))
+        ko = kblk * 128 // block
+        vo = vblk * 128 // block
+        in_specs.append(pl.BlockSpec((keys.shape[0], block), lambda h, o=ko: (0, h + o)))
+        in_specs.append(pl.BlockSpec((values.shape[0], block), lambda h, o=vo: (0, h + o)))
         args += [keys, values]
-    out_spec = pl.BlockSpec((tok_rows, 128), lambda h: (0, h))
+    out_spec = pl.BlockSpec((tok_rows, block), lambda h: (0, h))
     out_shape = jax.ShapeDtypeStruct((tok_rows, width), jnp.float32)
     return pl.pallas_call(
         functools.partial(attn_kernel, n_pieces=len(pieces)),
@@ -146,8 +149,7 @@
     from_left = lax.ppermute(kv, "patch", perm(1, 0))
     from_right = lax.ppermute(kv, "patch", perm(-1, 0))
     partner = lax.ppermute(kv, "patch", perm(0, 1))
-    far_a = lax.ppermute(from_left[:half], "patch", perm(1, 0))
-    far_b = lax.ppermute(from_right[half:], "patch", perm(-1, 0))
+    far = lax.ppermute(from_left, "patch", perm(1, 0))
     partner_left = lax.ppermute(from_left, "patch", perm(0, 1))
     partner_right = lax.ppermute(partner, "patch", perm(-1, 0))
     partner_far_a = lax.ppermute(partner_left[:half], "patch", perm(1, 0))
@@ -163,7 +165,6 @@
     value_fresh = jnp.dot(normed, w_value, preferred_element_type=jnp.float32).astype(jnp.bfloat16)
     query = query * jnp.asarray((channels // HEADS) ** -0.5, jnp.bfloat16)
 
-    far = jnp.concatenate([far_a, far_b], axis=0)
     partner_far = jnp.concatenate([partner_far_a, partner_far_b], axis=0)
     sets = [
         [(key_fresh, 0, value_fresh, 0)]
@@ -172,8 +173,8 @@
         [(partner_far, 0, partner_far, vblk)],
     ]
     partials = []
-    for pieces in sets:
-        partials.append(attention_partial(query, pieces))
+    for i, pieces in enumerate(sets):
+        partials.append(attention_partial(query, pieces, block=256 if i == 2 else 128))
     m = functools.reduce(jnp.maximum, [p[0] for p in partials])
     scales = [jnp.exp(p[0] - m) for p in partials]
     acc = sum(p[2] * r for p, r in zip(partials, scales))
@@ -193,18 +194,24 @@
 
     def conv_rows(cells):
         return lax.conv_general_dilated(
-            cells[None],
+            cells,
             conv_weight,
             (1, 1),
             ((0, 0), (1, 1)),
             dimension_numbers=("NHWC", "HWIO", "NHWC"),
             preferred_element_type=jnp.float32,
-        )[0]
-
-    inner = conv_rows(activated)
-    first_row = conv_rows(jnp.concatenate([top, activated[:2]], axis=0))
-    last_row = conv_rows(jnp.concatenate([activated[rows - 2 :], bottom], axis=0))
-    convolved = jnp.concatenate([first_row, inner, last_row], axis=0)
+        )
+
+    inner = conv_rows(activated[None])[0]
+    edges = conv_rows(
+        jnp.stack(
+            [
+                jnp.concatenate([top, activated[:2]], axis=0),
+                jnp.concatenate([activated[rows - 2 :], bottom], axis=0),
+            ]
+        )
+    )
+    convolved = jnp.concatenate([edges[0], inner, edges[1]], axis=0)
     temb = time_embedding(timestep, w_time)
     conv_out = (convolved + conv_bias + temb).astype(jnp.bfloat16)
     return conv_out.reshape(tok_rows, conv_weight.shape[3])

time: 215 us -> 261 us (1.21)
  waiting for transfers between devices: 85.6 us -> 140 us
    ppermute x2, waiting for transfers between devices: 40.2 us -> 80.3 us  [body(): stale_all = stale_all + lax.ppermute(stale_all, 'patch', pairs)]
    ppermute x2 -> x1, waiting for transfers between devices: 0.01 us -> 11.7 us  [body(): far = lax.ppermute(from_left, 'patch', perm(1, 0))]
    slice x5 -> x1, local copies, waits for them, and re-layouts: 3.34 us -> 0.04 us  [body(): activated[:2]]
    conv_general_dilated x3 -> x2, matrix products: 14.3 us -> 11.7 us  [conv_rows(): lax.conv_general_dilated(cells, conv_weight, (1, 1), ((0, 0), (1, 1)), di...]
    unnamed x37 -> x40, local copies, waits for them, and re-layouts: 3.66 us -> 5.44 us
  transfers between devices with their start and end apart: 14 -> 13, of which waited for: 4 -> 5; matrix products, arithmetic and copies ran while one was open for 13% -> 8% of each run, Pallas kernels for 20% -> 17%
where the time goes in v5:
time: 261 us
  waiting for transfers between devices  140 us (54%)
  Pallas kernels  54.8 us (21%)
  starting transfers between devices  24 us (9%)
  matrix products  17.4 us (7%)
  local copies, waits for them, and re-layouts  13.1 us (5%)
  other arithmetic  10.7 us (4%)
    ppermute x2, waiting for transfers between devices, body(): stale_all = stale_all + lax.ppermute(stale_all, 'patch', pairs)  80.3 us
    pallas_call x3, Pallas kernels, attention_partial(): pl.pallas_call(functools.partial(attn_kernel, n_pieces=len(pieces)), grid...  54.8 us
    ppermute x1, waiting for transfers between devices, body(): partner = lax.ppermute(kv, 'patch', perm(0, 1))  44.8 us
    conv_general_dilated x2, matrix products, conv_rows(): lax.conv_general_dilated(cells, conv_weight, (1, 1), ((0, 0), (1, 1)), di...  11.7 us
    ppermute x1, waiting for transfers between devices, body(): far = lax.ppermute(from_left, 'patch', perm(1, 0))  11.7 us
    ppermute x1, starting transfers between devices, body(): lax.ppermute(activated[:1], 'patch', [(i + 1, i) for i in range(count_p -...  7.76 us
    reduce_sum x4, other arithmetic, group_moments(): jnp.sum(values, axis=(0, 2))  5.53 us
    unnamed x40, local copies, waits for them, and re-layouts  5.44 us
  transfers between devices with their start and end apart: 13, of which 5 were waited for; matrix products, arithmetic and copies ran while one was open for 8% of the time, Pallas kernels for 17%

profile of v5, /device:TPU:64, one launch (start us, length us, event | category | flops | bytes accessed | tf_op | source)
XLA Modules:
  0.0 260.8 jit_solution(9008564229259617698)
XLA Ops:
  0.0 2.4 constant_dynamic-update-slice_fusion.1
  2.4 1.1 constant_dynamic-update-slice_fusion
  3.5 1.6 collective-permute-start.3
  5.1 44.8 %collective-permute-done.5.refs_7_.refs_8_ = bf16[384,2560]{1,0:T(8,128)(2,1)} collective-permute-done((bf16[384,2560]{1,0:T(8,128)(2,1)}, bf16[384,2560]{1,0:T(8,128)(2,1)}, u32[]{:S(2)}, u32[]{:S(2)}) %collective-permute-start.5) | collective-permute-done | bytes 1966112 | tf_op jit(solution)/shard_map/ppermute | solution.py:151
  49.9 3.0 %collective-permute-start.8 = (bf16[384,2560]{1,0:T(8,128)(2,1)}, bf16[384,2560]{1,0:T(8,128)(2,1)}, u32[]{:S(2)}, u32[]{:S(2)}) collective-permute-start(bf16[384,2560]{1,0:T(8,128)(2,1)} %collective-permute-done.5.refs_7_.refs_8_), channel_id=1, source_target_pairs={{0,3},{1,0},{2,1},{3,2},{4,7},{5,4},{6,5},{7,6},{8,11},{9,8},{10,9... | collective-permute-start | bytes 5898248 | tf_op jit(solution)/shard_map/ppermute | solution.py:154
  52.9 0.3 collective-permute-start.7
  53.2 1.5 collective-permute-start.4
  54.7 0.6 collective-permute-start
  56.0 1.5 convert_reduce_fusion
  57.5 78.6 %collective-permute-done = f32[2,2,32]{2,1,0:T(2,128)S(1)} collective-permute-done((f32[2,2,32]{2,1,0:T(2,128)S(1)}, f32[2,2,32]{2,1,0:T(2,128)S(1)}, u32[]{:S(2)}, u32[]{:S(2)}) %collective-permute-start) | collective-permute-done | bytes 544 | tf_op jit(solution)/shard_map/ppermute | solution.py:146
  136.1 3.2 %collective-permute-start.1 = (f32[2,2,32]{2,1,0:T(2,128)S(1)}, f32[2,2,32]{2,1,0:T(2,128)S(1)}, u32[]{:S(2)}, u32[]{:S(2)}) collective-permute-start(f32[2,2,32]{2,1,0:T(2,128)S(1)} %add.74), channel_id=1, source_target_pairs={{0,2},{1,3},{2,0},{3,1},{4,6},{5,7},{6,4},{7,5},{8,10},{9,11},{10,... | collective-permute-start | bytes 1544 | tf_op jit(solution)/shard_map/ppermute | solution.py:146
  139.3 0.1 pad_maximum_fusion.2
  139.4 1.8 collective-permute-done.1
  141.2 0.6 collective-permute-start.2
  141.7 1.3 convolution_reduce_fusion
  143.0 0.1 reduce_sum.59
  143.1 0.1 reduce_sum.60
  143.2 0.1 reduce_sum.62
  143.3 0.1 reduce_sum.66
  143.4 2.8 %collective-permute-done.2 = f32[2,2,32]{2,1,0:T(2,128)S(1)} collective-permute-done((f32[2,2,32]{2,1,0:T(2,128)S(1)}, f32[2,2,32]{2,1,0:T(2,128)S(1)}, u32[]{:S(2)}, u32[]{:S(2)}) %collective-permute-start.2) | collective-permute-done | bytes 544 | tf_op jit(solution)/shard_map/ppermute | solution.py:147
  146.4 0.1 reshape.47
  146.5 0.1 reshape.46
  146.7 1.3 slice.91
  148.0 3.3 %collective-permute-start.10 = (bf16[192,2560]{1,0:T(8,128)(2,1)S(1)}, bf16[192,2560]{1,0:T(8,128)(2,1)S(1)}, u32[]{:S(2)}, u32[]{:S(2)}) collective-permute-start(bf16[192,2560]{1,0:T(8,128)(2,1)S(1)} %slice.91), channel_id=1, source_target_pairs={{0,3},{1,0},{2,1},{3,2},{4,7},{5,4},{6,5},{7,6},{8,11},{9,8},{10,9... | collective-permute-start | bytes 2949128 | tf_op jit(solution)/shard_map/ppermute | solution.py:156
  151.3 1.3 slice.90
  152.6 0.3 collective-permute-start.9
  152.9 1.5 fusion.1.refs_0_
  154.4 0.5 copy-done.11
  154.8 1.4 convolution_convert_fusion.1.refs_1_
  156.3 0.5 copy-done.12
  156.7 1.5 convolution_convert_fusion.refs_2_
  158.2 23.6 %shard_map.145 = (f32[384,1280]{1,0:T(8,128)S(1)}, f32[384,1280]{1,0:T(8,128)}, f32[384,1280]{1,0:T(8,128)}) custom-call(bf16[384,1280]{1,0:T(8,128)(2,1)S(1)} %fusion.1.refs_0_, bf16[384,1280]{1,0:T(8,128)(2,1)S(1)} %convolution_convert_fusion.1.refs_1_, bf16[384,1280]{1,0:T(8,128)(2,1)S(1)} %convolution_convert_fusion.refs_2_, ...), custom_call_target="tpu_custom_call" | custom-call | tf_op jit(solution)/shard_map/pallas_call | solution.py:95
  181.8 11.7 %collective-permute-done.6.refs_1_.refs_2_ = bf16[384,2560]{1,0:T(8,128)(2,1)} collective-permute-done((bf16[384,2560]{1,0:T(8,128)(2,1)}, bf16[384,2560]{1,0:T(8,128)(2,1)}, u32[]{:S(2)}, u32[]{:S(2)}) %collective-permute-start.6) | collective-permute-done | bytes 1966112 | tf_op jit(solution)/shard_map/ppermute | solution.py:152
  193.5 19.6 %shard_map.146 = (f32[384,1280]{1,0:T(8,128)S(1)}, f32[384,1280]{1,0:T(8,128)S(1)}, f32[384,1280]{1,0:T(8,128)}) custom-call(bf16[384,1280]{1,0:T(8,128)(2,1)S(1)} %fusion.1.refs_0_, bf16[384,2560]{1,0:T(8,128)(2,1)} %collective-permute-done.6.refs_1_.refs_2_, bf16[384,2560]{1,0:T(8,128)(2,1)} %collective-permute-done.6.refs_1_.refs_2_, ...), custom_call_target="tpu_custom_call" | custom-call | tf_op jit(solution)/shard_map/pallas_call | solution.py:95
  213.1 1.4 pad_maximum_fusion.refs_1_.refs_2_
  214.5 11.6 %shard_map.147 = (f32[384,1280]{1,0:T(8,128)S(1)}, f32[384,1280]{1,0:T(8,128)S(1)}, f32[384,1280]{1,0:T(8,128)}) custom-call(bf16[384,1280]{1,0:T(8,128)(2,1)S(1)} %fusion.1.refs_0_, bf16[384,2560]{1,0:T(8,128)(2,1)} %pad_maximum_fusion.refs_1_.refs_2_, bf16[384,2560]{1,0:T(8,128)(2,1)} %pad_maximum_fusion.refs_1_.refs_2_), custom_call_target="tpu_custom_call" | custom-call | tf_op jit(solution)/shard_map/pallas_call | solution.py:95
  226.1 3.8 %convert_reduce_fusion.1 = (f32[1280]{0:T(1024)S(1)}, f32[1280]{0:T(1024)S(1)}, bf16[384,1280]{1,0:T(8,128)(2,1)S(1)}) fusion(f32[384,1280]{1,0:T(8,128)S(1)} %get-tuple-element.22, f32[384,1280]{1,0:T(8,128)S(1)} %get-tuple-element.21, f32[384,1280]{1,0:T(8,128)S(1)} %copy-done.3, f32[384,1280]{1,0:T(8,128)} %get-tuple-element.19, ...), kind=kLoop, calls=%fused_computation.7 | loop fusion | flops 11302400 | bytes 19671040 | tf_op jit(solution)/shard_map/reduce_sum | solution.py:25
  229.9 0.1 reduce_sum.81
  230.0 0.1 reduce_sum.82
  230.1 0.1 reduce_sum.84
  230.2 0.1 reduce_sum.85
  230.4 0.1 reshape.49
  230.6 0.1 reshape.48
  230.7 0.6 fusion.9
  231.4 1.9 collective-permute-start.11
  233.3 7.8 %collective-permute-start.12 = (bf16[1,64,1280]{2,1,0:T(8,128)(2,1)S(1)}, bf16[1,64,1280]{2,1,0:T(8,128)(2,1)S(1)}, u32[]{:S(2)}, u32[]{:S(2)}) collective-permute-start(bf16[1,64,1280]{2,1,0:T(8,128)(2,1)S(1)} %get-tuple-element.33), channel_id=1, source_target_pairs={{1,0},{2,1},{3,2},{4,3},{5,4},{6,5},{7,6},{9,8},{10,9},{11,10},{12... | collective-permute-start | bytes 491528 | tf_op jit(solution)/shard_map/ppermute | solution.py:193
  241.1 0.6 copy.35
  241.6 0.2 pad.2
  241.9 0.2 copy.37
  242.1 0.4 copy-done.14
  242.6 8.9 %fusion.25 = f32[4,8,9,640]{3,1,2,0:T(8,128)S(1)} fusion(bf16[3,3,1280,640]{3,2,1,0:T(8,128)(2,1)} %param.26, bf16[6,1,7,2,1280]{4,2,3,0,1:T(8,128)(2,1)S(1)} %slice.100, bf16[6,1,8,9,1280]{4,2,3,0,1:T(8,128)(2,1)S(1)} %copy.37, pred[8,9]{0,1:T(8,128)(4,1)S(1)} %copy-done.14), kind=kOutput, calls=%fused_computation.38 | convolution fusion | flops 4250972160 | bytes 16803912 | tf_op jit(solution)/shard_map/conv_general_dilated | solution.py:196
  251.5 0.2 copy.38
  251.9 0.1 maximum_bitcast_fusion
  252.0 1.0 copy.40
  253.1 0.8 pad.clone
  253.9 0.1 slice.98
  254.0 1.3 fusion.18
  255.4 2.8 %fusion.28 = f32[1,16,9,640]{3,1,2,0:T(8,128)S(1)} fusion(bf16[3,3,1280,640]{3,2,1,0:T(8,128)(2,1)S(1)} %bitcast.102, bf16[3,2,8,11,1280]{4,1,3,2,0:T(2,128)(2,1)S(1)} %fusion.18, pred[16,9]{0,1:T(8,128)(4,1)S(1)} %copy-done.13), kind=kOutput, calls=%fused_computation.39 | convolution fusion | flops 2123458560 | bytes 16466064 | tf_op jit(solution)/shard_map/conv_general_dilated | solution.py:196
  258.2 0.4 copy.34
  258.5 0.1 slice_bitcast_fusion.2
  258.7 0.4 pad_maximum_fusion.1
  259.1 0.2 copy.39
  259.3 0.9 fusion.32
  260.2 0.6 copy-done.1
  (67 shorter events, 0.8 us)
Async XLA Ops:
  0.0 152.9 %copy-start = (bf16[1280,1280]{1,0:T(8,128)(2,1)S(1)}, bf16[1280,1280]{1,0:T(8,128)(2,1)}, u32[]{:S(2)}) copy-start(bf16[1280,1280]{1,0:T(8,128)(2,1)} %param.21) | copy-start | bytes 9830404
  0.0 2.4 copy-start.4
  0.0 54.7 %copy-start.5 = (f32[6,2,2,32]{3,2,1,0:T(2,128)S(1)}, f32[6,2,2,32]{3,2,1,0:T(2,128)}, u32[]{:S(2)}) copy-start(f32[6,2,2,32]{3,2,1,0:T(2,128)} %param.18) | copy-start | bytes 9220
  2.4 144.2 %copy-start.6 = (f32[1280]{0:T(1024)S(1)}, f32[1280]{0:T(1024)}, u32[]{:S(2)}) copy-start(f32[1280]{0:T(1024)} %param.19) | copy-start | bytes 15364
  2.4 144.2 %copy-start.7 = (f32[1280]{0:T(1024)S(1)}, f32[1280]{0:T(1024)}, u32[]{:S(2)}) copy-start(f32[1280]{0:T(1024)} %param.20) | copy-start | bytes 15364
  3.5 46.4 %collective-permute-start.5 = (bf16[384,2560]{1,0:T(8,128)(2,1)}, bf16[384,2560]{1,0:T(8,128)(2,1)}, u32[]{:S(2)}, u32[]{:S(2)}) collective-permute-start(bf16[384,2560]{1,0:T(8,128)(2,1)} %constant_dynamic-update-slice_fusion), channel_id=1, source_target_pairs={{0,4},{1,5},{2,6},{3,7},{4,0},{5,1},{6,2},{7,3},{8,12},{9,13},{10,... | collective-permute-start | bytes 5898248 | tf_op jit(solution)/shard_map/ppermute | solution.py:151
  3.5 49.4 %collective-permute-start.3 = (bf16[384,2560]{1,0:T(8,128)(2,1)}, bf16[384,2560]{1,0:T(8,128)(2,1)}, u32[]{:S(2)}, u32[]{:S(2)}) collective-permute-start(bf16[384,2560]{1,0:T(8,128)(2,1)} %constant_dynamic-update-slice_fusion), channel_id=1, source_target_pairs={{0,1},{1,2},{2,3},{3,0},{4,5},{5,6},{6,7},{7,4},{8,9},{9,10},{10,1... | collective-permute-start | bytes 5898248 | tf_op jit(solution)/shard_map/ppermute | solution.py:149
  49.9 96.8 %collective-permute-start.8 = (bf16[384,2560]{1,0:T(8,128)(2,1)}, bf16[384,2560]{1,0:T(8,128)(2,1)}, u32[]{:S(2)}, u32[]{:S(2)}) collective-permute-start(bf16[384,2560]{1,0:T(8,128)(2,1)} %collective-permute-done.5.refs_7_.refs_8_), channel_id=1, source_target_pairs={{0,3},{1,0},{2,1},{3,2},{4,7},{5,4},{6,5},{7,6},{8,11},{9,8},{10,9... | collective-permute-start | bytes 5898248 | tf_op jit(solution)/shard_map/ppermute | solution.py:154
  52.9 98.4 %collective-permute-start.7 = (bf16[384,2560]{1,0:T(8,128)(2,1)}, bf16[384,2560]{1,0:T(8,128)(2,1)}, u32[]{:S(2)}, u32[]{:S(2)}) collective-permute-start(bf16[384,2560]{1,0:T(8,128)(2,1)} %collective-permute-done.3.refs_3_.refs_4_), channel_id=1, source_target_pairs={{0,4},{1,5},{2,6},{3,7},{4,0},{5,1},{6,2},{7,3},{8,12},{9,13},{10,... | collective-permute-start | bytes 5898248 | tf_op jit(solution)/shard_map/ppermute | solution.py:153
  53.2 105.0 %collective-permute-start.4 = (bf16[384,2560]{1,0:T(8,128)(2,1)}, bf16[384,2560]{1,0:T(8,128)(2,1)}, u32[]{:S(2)}, u32[]{:S(2)}) collective-permute-start(bf16[384,2560]{1,0:T(8,128)(2,1)} %constant_dynamic-update-slice_fusion), channel_id=1, source_target_pairs={{0,3},{1,0},{2,1},{3,2},{4,7},{5,4},{6,5},{7,6},{8,11},{9,8},{10,9... | collective-permute-start | bytes 5898248 | tf_op jit(solution)/shard_map/ppermute | solution.py:150
  54.7 81.4 %collective-permute-start = (f32[2,2,32]{2,1,0:T(2,128)S(1)}, f32[2,2,32]{2,1,0:T(2,128)S(1)}, u32[]{:S(2)}, u32[]{:S(2)}) collective-permute-start(f32[2,2,32]{2,1,0:T(2,128)S(1)} %reduce_sum.54), channel_id=1, source_target_pairs={{0,1},{1,0},{2,3},{3,2},{4,5},{5,4},{6,7},{7,6},{8,9},{9,8},{10,11... | collective-permute-start | bytes 1544 | tf_op jit(solution)/shard_map/ppermute | solution.py:146
  136.1 5.1 %collective-permute-start.1 = (f32[2,2,32]{2,1,0:T(2,128)S(1)}, f32[2,2,32]{2,1,0:T(2,128)S(1)}, u32[]{:S(2)}, u32[]{:S(2)}) collective-permute-start(f32[2,2,32]{2,1,0:T(2,128)S(1)} %add.74), channel_id=1, source_target_pairs={{0,2},{1,3},{2,0},{3,1},{4,6},{5,7},{6,4},{7,5},{8,10},{9,11},{10,... | collective-permute-start | bytes 1544 | tf_op jit(solution)/shard_map/ppermute | solution.py:146
  141.2 5.1 %collective-permute-start.2 = (f32[2,2,32]{2,1,0:T(2,128)S(1)}, f32[2,2,32]{2,1,0:T(2,128)S(1)}, u32[]{:S(2)}, u32[]{:S(2)}) collective-permute-start(f32[2,2,32]{2,1,0:T(2,128)S(1)} %add.75), channel_id=1, source_target_pairs={{0,4},{1,5},{2,6},{3,7},{4,0},{5,1},{6,2},{7,3},{8,12},{9,13},{10,... | collective-permute-start | bytes 1544 | tf_op jit(solution)/shard_map/ppermute | solution.py:147
  146.3 47.2 %collective-permute-start.6 = (bf16[384,2560]{1,0:T(8,128)(2,1)}, bf16[384,2560]{1,0:T(8,128)(2,1)}, u32[]{:S(2)}, u32[]{:S(2)}) collective-permute-start(bf16[384,2560]{1,0:T(8,128)(2,1)} %collective-permute-done.3.refs_3_.refs_4_), channel_id=1, source_target_pairs={{0,1},{1,2},{2,3},{3,0},{4,5},{5,6},{6,7},{7,4},{8,9},{9,10},{10,1... | collective-permute-start | bytes 5898248 | tf_op jit(solution)/shard_map/ppermute | solution.py:152
  146.7 6.2 %copy-start.2 = (bf16[384,1280]{1,0:T(8,128)(2,1)S(1)}, bf16[384,1280]{1,0:T(8,128)(2,1)}, u32[]{:S(2)}) copy-start(bf16[384,1280]{1,0:T(8,128)(2,1)} %param.15) | copy-start | bytes 2949124
  148.0 65.1 %collective-permute-start.10 = (bf16[192,2560]{1,0:T(8,128)(2,1)S(1)}, bf16[192,2560]{1,0:T(8,128)(2,1)S(1)}, u32[]{:S(2)}, u32[]{:S(2)}) collective-permute-start(bf16[192,2560]{1,0:T(8,128)(2,1)S(1)} %slice.91), channel_id=1, source_target_pairs={{0,3},{1,0},{2,1},{3,2},{4,7},{5,4},{6,5},{7,6},{8,11},{9,8},{10,9... | collective-permute-start | bytes 2949128 | tf_op jit(solution)/shard_map/ppermute | solution.py:156
  152.6 60.5 %collective-permute-start.9 = (bf16[192,2560]{1,0:T(8,128)(2,1)S(1)}, bf16[192,2560]{1,0:T(8,128)(2,1)S(1)}, u32[]{:S(2)}, u32[]{:S(2)}) collective-permute-start(bf16[192,2560]{1,0:T(8,128)(2,1)S(1)} %slice.90), channel_id=1, source_target_pairs={{0,1},{1,2},{2,3},{3,0},{4,5},{5,6},{6,7},{7,4},{8,9},{9,10},{10,1... | collective-permute-start | bytes 2949128 | tf_op jit(solution)/shard_map/ppermute | solution.py:155
  152.9 1.9 copy-start.11
  154.8 1.9 copy-start.12
  214.5 11.6 %copy-start.3 = (f32[384,1280]{1,0:T(8,128)S(1)}, f32[384,1280]{1,0:T(8,128)}, u32[]{:S(2)}) copy-start(f32[384,1280]{1,0:T(8,128)} %get-tuple-element.20) | copy-start | bytes 5898244
  226.1 4.6 %copy-start.8 = (f32[1280]{0:T(1024)S(1)}, f32[1280]{0:T(1024)}, u32[]{:S(2)}) copy-start(f32[1280]{0:T(1024)} %param.24) | copy-start | bytes 15364
  226.1 4.6 %copy-start.9 = (f32[1280]{0:T(1024)S(1)}, f32[1280]{0:T(1024)}, u32[]{:S(2)}) copy-start(f32[1280]{0:T(1024)} %param.25) | copy-start | bytes 15364
  231.4 20.4 %collective-permute-start.11 = (bf16[1,64,1280]{2,1,0:T(8,128)(2,1)S(1)}, bf16[1,64,1280]{2,1,0:T(8,128)(2,1)S(1)}, u32[]{:S(2)}, u32[]{:S(2)}) collective-permute-start(bf16[1,64,1280]{2,1,0:T(8,128)(2,1)S(1)} %get-tuple-element.32), channel_id=1, source_target_pairs={{0,1},{1,2},{2,3},{3,4},{4,5},{5,6},{6,7},{8,9},{9,10},{10,11},{11... | collective-permute-start | bytes 491528 | tf_op jit(solution)/shard_map/ppermute | solution.py:190
  233.3 18.6 %collective-permute-start.12 = (bf16[1,64,1280]{2,1,0:T(8,128)(2,1)S(1)}, bf16[1,64,1280]{2,1,0:T(8,128)(2,1)S(1)}, u32[]{:S(2)}, u32[]{:S(2)}) collective-permute-start(bf16[1,64,1280]{2,1,0:T(8,128)(2,1)S(1)} %get-tuple-element.33), channel_id=1, source_target_pairs={{1,0},{2,1},{3,2},{4,3},{5,4},{6,5},{7,6},{9,8},{10,9},{11,10},{12... | collective-permute-start | bytes 491528 | tf_op jit(solution)/shard_map/ppermute | solution.py:193
  241.9 0.7 copy-start.14
  242.6 12.8 %slice-start = ((s8[14745600]{0:T(1024)(128)(4,1)}), s8[4194304]{0:T(1024)(128)(4,1)S(1)}, s32[]{:S(2)}) async-start(s8[14745600]{0:T(1024)(128)(4,1)} %bitcast.101), calls=%async_computation | async-start | bytes 8388608
  242.6 12.8 %slice-start.1 = ((s8[14745600]{0:T(1024)(128)(4,1)}), s8[4194304]{0:T(1024)(128)(4,1)S(1)}, s32[]{:S(2)}) async-start(s8[14745600]{0:T(1024)(128)(4,1)} %bitcast.101), calls=%async_computation.1 | async-start | bytes 8388608
  242.6 12.8 %slice-start.2 = ((s8[14745600]{0:T(1024)(128)(4,1)}), s8[4194304]{0:T(1024)(128)(4,1)S(1)}, s32[]{:S(2)}) async-start(s8[14745600]{0:T(1024)(128)(4,1)} %bitcast.101), calls=%async_computation.2 | async-start | bytes 8388608
  251.7 3.6 %slice-start.3 = ((s8[14745600]{0:T(1024)(128)(4,1)}), s8[2162688]{0:T(1024)(128)(4,1)S(1)}, s32[]{:S(2)}) async-start(s8[14745600]{0:T(1024)(128)(4,1)} %bitcast.101), calls=%async_computation.3 | async-start | bytes 4325376
  253.9 1.5 copy-start.13
  258.6 0.7 copy-start.10
  258.7 2.1 copy-start.1

commit v6 on v5

--- a/solution.py
+++ b/solution.py
@@ -127,6 +127,7 @@
     ring = YRING
     planes = devices // ring
     half = tok_rows // 2
+    tail_cut = 2 * tok_rows // 3
     vblk = channels // 128
 
     def perm(dy, dz):
@@ -149,11 +150,12 @@
     from_left = lax.ppermute(kv, "patch", perm(1, 0))
     from_right = lax.ppermute(kv, "patch", perm(-1, 0))
     partner = lax.ppermute(kv, "patch", perm(0, 1))
-    far = lax.ppermute(from_left, "patch", perm(1, 0))
+    far_a = lax.ppermute(from_left[:half], "patch", perm(1, 0))
+    far_b = lax.ppermute(from_right[half:], "patch", perm(-1, 0))
     partner_left = lax.ppermute(from_left, "patch", perm(0, 1))
     partner_right = lax.ppermute(partner, "patch", perm(-1, 0))
-    partner_far_a = lax.ppermute(partner_left[:half], "patch", perm(1, 0))
-    partner_far_b = lax.ppermute(partner_right[half:], "patch", perm(-1, 0))
+    partner_far_a = lax.ppermute(partner_left[:tail_cut], "patch", perm(1, 0))
+    partner_far_b = lax.ppermute(partner_right[tail_cut:], "patch", perm(-1, 0))
 
     total_attn = stale_all[0]
     totals_attn = total_attn - own_stale[0] + group_moments(hidden_in, GROUPS)
@@ -165,6 +167,7 @@
     value_fresh = jnp.dot(normed, w_value, preferred_element_type=jnp.float32).astype(jnp.bfloat16)
     query = query * jnp.asarray((channels // HEADS) ** -0.5, jnp.bfloat16)
 
+    far = jnp.concatenate([far_a, far_b], axis=0)
     partner_far = jnp.concatenate([partner_far_a, partner_far_b], axis=0)
     sets = [
         [(key_fresh, 0, value_fresh, 0)]

time: 261 us -> 210 us (0.80)
  waiting for transfers between devices: 140 us -> 77.5 us
  starting transfers between devices: 24 us -> 31.1 us
    ppermute x2, waiting for transfers between devices: 80.3 us -> 3.09 us  [body(): stale_all = stale_all + lax.ppermute(stale_all, 'patch', pairs)]
    ppermute x1, waiting for transfers between devices: 44.8 us -> 1.12 us  [body(): partner = lax.ppermute(kv, 'patch', perm(0, 1))]
    ppermute x1, waiting for transfers between devices: 0.01 us -> 42.9 us  [body(): from_left = lax.ppermute(kv, 'patch', perm(1, 0))]
    ppermute x1, waiting for transfers between devices: 2.82 us -> 30.4 us  [body(): stale_all = stale_all + lax.ppermute(stale_all, 'patch', perm(0, 1))]
    ppermute x3 -> x4, waiting for transfers between devices: 11.7 us -> 0.01 us  [the longest x1 0.01 us: body(): far_b = lax.ppermute(from_right[half:], 'patch', perm(-1, 0))]
    ppermute x3 -> x4, starting transfers between devices: 3.56 us -> 11.2 us  [the longest x1 7.56 us: body(): far_b = lax.ppermute(from_right[half:], 'patch', perm(-1, 0))]
  transfers between devices with their start and end apart: 13 -> 14, of which waited for: 5 -> 4; matrix products, arithmetic and copies ran while one was open for 8% -> 12% of each run, Pallas kernels for 17% -> 21%
where the time goes in v6:
time: 210 us; the launch traced here: 209 us
  waiting for transfers between devices  77.5 us (37%)
  Pallas kernels  54.8 us (26%)
  starting transfers between devices  31.1 us (15%)
  matrix products  17.4 us (8%)
  local copies, waits for them, and re-layouts  15.1 us (7%)
  other arithmetic  12.1 us (6%)
    pallas_call x3, Pallas kernels, attention_partial(): pl.pallas_call(functools.partial(attn_kernel, n_pieces=len(pieces)), grid...  54.8 us
    ppermute x1, waiting for transfers between devices, body(): from_left = lax.ppermute(kv, 'patch', perm(1, 0))  42.9 us
    ppermute x1, waiting for transfers between devices, body(): stale_all = stale_all + lax.ppermute(stale_all, 'patch', perm(0, 1))  30.4 us
    conv_general_dilated x2, matrix products, conv_rows(): lax.conv_general_dilated(cells, conv_weight, (1, 1), ((0, 0), (1, 1)), di...  11.7 us
    ppermute x1, starting transfers between devices, body(): far_b = lax.ppermute(from_right[half:], 'patch', perm(-1, 0))  7.56 us
    ppermute x1, starting transfers between devices, body(): lax.ppermute(activated[:1], 'patch', [(i + 1, i) for i in range(count_p -...  7.49 us
    reduce_sum x4, other arithmetic, group_moments(): jnp.sum(values, axis=(0, 2))  5.53 us
    unnamed x40, local copies, waits for them, and re-layouts  4.99 us
  transfers between devices with their start and end apart: 14, of which 4 were waited for; matrix products, arithmetic and copies ran while one was open for 12% of the time, Pallas kernels for 21%

profile of v6, /device:TPU:64, one launch (start us, length us, event | category | flops | bytes accessed | tf_op | source)
XLA Modules:
  0.0 209.3 jit_solution(7073007704871540956)
XLA Ops:
  0.0 2.4 %constant_dynamic-update-slice_fusion.1 = bf16[384,2560]{1,0:T(8,128)(2,1)} fusion(bf16[384,1280]{1,0:T(8,128)(2,1)} %param.16), kind=kLoop, calls=%fused_computation.57 | loop fusion | bytes 1966080
  2.5 1.1 constant_dynamic-update-slice_fusion
  3.5 1.6 collective-permute-start.3
  5.1 1.7 collective-permute-start.4
  6.8 42.9 %collective-permute-done.3.refs_3_.refs_4_ = bf16[384,2560]{1,0:T(8,128)(2,1)} collective-permute-done((bf16[384,2560]{1,0:T(8,128)(2,1)}, bf16[384,2560]{1,0:T(8,128)(2,1)}, u32[]{:S(2)}, u32[]{:S(2)}) %collective-permute-start.3) | collective-permute-done | bytes 1966112 | tf_op jit(solution)/shard_map/ppermute | solution.py:150
  49.7 0.4 collective-permute-start
  50.1 1.1 collective-permute-done.5.refs_7_.refs_8_
  51.2 1.7 collective-permute-start.9
  52.9 1.5 convert_reduce_fusion
  55.1 2.0 collective-permute-start.1
  57.2 3.1 %collective-permute-done.1 = f32[2,2,32]{2,1,0:T(2,128)S(1)} collective-permute-done((f32[2,2,32]{2,1,0:T(2,128)S(1)}, f32[2,2,32]{2,1,0:T(2,128)S(1)}, u32[]{:S(2)}, u32[]{:S(2)}) %collective-permute-start.1) | collective-permute-done | bytes 544 | tf_op jit(solution)/shard_map/ppermute | solution.py:147
  60.3 2.9 %collective-permute-start.2 = (f32[2,2,32]{2,1,0:T(2,128)S(1)}, f32[2,2,32]{2,1,0:T(2,128)S(1)}, u32[]{:S(2)}, u32[]{:S(2)}) collective-permute-start(f32[2,2,32]{2,1,0:T(2,128)S(1)} %add.75), channel_id=1, source_target_pairs={{0,4},{1,5},{2,6},{3,7},{4,0},{5,1},{6,2},{7,3},{8,12},{9,13},{10,... | collective-permute-start | bytes 1544 | tf_op jit(solution)/shard_map/ppermute | solution.py:148
  63.2 1.3 convolution_reduce_fusion
  64.5 0.1 reduce_sum.59
  64.6 0.1 reduce_sum.60
  64.7 0.1 reduce_sum.62
  64.8 0.1 reduce_sum.66
  64.9 30.4 %collective-permute-done.2 = f32[2,2,32]{2,1,0:T(2,128)S(1)} collective-permute-done((f32[2,2,32]{2,1,0:T(2,128)S(1)}, f32[2,2,32]{2,1,0:T(2,128)S(1)}, u32[]{:S(2)}, u32[]{:S(2)}) %collective-permute-start.2) | collective-permute-done | bytes 544 | tf_op jit(solution)/shard_map/ppermute | solution.py:148
  95.4 0.1 reshape.47
  95.6 0.1 reshape.46
  95.7 1.3 slice.99
  97.0 7.6 %collective-permute-start.7 = (bf16[192,2560]{1,0:T(8,128)(2,1)S(1)}, bf16[192,2560]{1,0:T(8,128)(2,1)S(1)}, u32[]{:S(2)}, u32[]{:S(2)}) collective-permute-start(bf16[192,2560]{1,0:T(8,128)(2,1)S(1)} %slice.99), channel_id=1, source_target_pairs={{0,3},{1,0},{2,1},{3,2},{4,7},{5,4},{6,5},{7,6},{8,11},{9,8},{10,9... | collective-permute-start | bytes 2949128 | tf_op jit(solution)/shard_map/ppermute | solution.py:154
  104.5 1.3 slice.98
  105.9 1.4 slice.100
  107.3 1.6 collective-permute-start.10
  108.9 1.5 fusion.1.refs_0_
  110.3 0.5 copy-done.11
  110.8 1.5 convolution_convert_fusion.1.refs_1_
  112.3 1.1 slice.101
  113.4 2.0 collective-permute-start.11
  115.4 1.5 convolution_convert_fusion.refs_2_
  116.9 23.6 %shard_map.145 = (f32[384,1280]{1,0:T(8,128)S(1)}, f32[384,1280]{1,0:T(8,128)}, f32[384,1280]{1,0:T(8,128)}) custom-call(bf16[384,1280]{1,0:T(8,128)(2,1)S(1)} %fusion.1.refs_0_, bf16[384,1280]{1,0:T(8,128)(2,1)S(1)} %convolution_convert_fusion.1.refs_1_, bf16[384,1280]{1,0:T(8,128)(2,1)S(1)} %convolution_convert_fusion.refs_2_, ...), custom_call_target="tpu_custom_call" | custom-call | tf_op jit(solution)/shard_map/pallas_call | solution.py:95
  140.6 1.4 pad_maximum_fusion.refs_1_.refs_2_
  142.0 19.6 %shard_map.146 = (f32[384,1280]{1,0:T(8,128)S(1)}, f32[384,1280]{1,0:T(8,128)S(1)}, f32[384,1280]{1,0:T(8,128)}) custom-call(bf16[384,1280]{1,0:T(8,128)(2,1)S(1)} %fusion.1.refs_0_, bf16[384,2560]{1,0:T(8,128)(2,1)} %pad_maximum_fusion.refs_1_.refs_2_, bf16[384,2560]{1,0:T(8,128)(2,1)} %pad_maximum_fusion.refs_1_.refs_2_, ...), custom_call_target="tpu_custom_call" | custom-call | tf_op jit(solution)/shard_map/pallas_call | solution.py:95
  161.6 1.4 pad_maximum_fusion.1.refs_1_.refs_2_
  163.0 11.6 %shard_map.147 = (f32[384,1280]{1,0:T(8,128)S(1)}, f32[384,1280]{1,0:T(8,128)S(1)}, f32[384,1280]{1,0:T(8,128)}) custom-call(bf16[384,1280]{1,0:T(8,128)(2,1)S(1)} %fusion.1.refs_0_, bf16[384,2560]{1,0:T(8,128)(2,1)} %pad_maximum_fusion.1.refs_1_.refs_2_, bf16[384,2560]{1,0:T(8,128)(2,1)} %pad_maximum_fusion.1.refs_1_.refs_2_), custom_call_target="tpu_custom_call" | custom-call | tf_op jit(solution)/shard_map/pallas_call | solution.py:95
  174.6 3.8 %convert_reduce_fusion.1 = (f32[1280]{0:T(1024)S(1)}, f32[1280]{0:T(1024)S(1)}, bf16[384,1280]{1,0:T(8,128)(2,1)S(1)}) fusion(f32[384,1280]{1,0:T(8,128)S(1)} %get-tuple-element.22, f32[384,1280]{1,0:T(8,128)S(1)} %get-tuple-element.21, f32[384,1280]{1,0:T(8,128)S(1)} %copy-done.3, f32[384,1280]{1,0:T(8,128)} %get-tuple-element.19, ...), kind=kLoop, calls=%fused_computation.7 | loop fusion | flops 11302400 | bytes 19671040 | tf_op jit(solution)/shard_map/reduce_sum | solution.py:25
  178.4 0.1 reduce_sum.81
  178.5 0.1 reduce_sum.82
  178.6 0.1 reduce_sum.84
  178.7 0.1 reduce_sum.85
  178.9 0.1 reshape.49
  179.1 0.1 reshape.48
  179.2 0.6 fusion.9
  179.9 2.2 %collective-permute-start.12 = (bf16[1,64,1280]{2,1,0:T(8,128)(2,1)S(1)}, bf16[1,64,1280]{2,1,0:T(8,128)(2,1)S(1)}, u32[]{:S(2)}, u32[]{:S(2)}) collective-permute-start(bf16[1,64,1280]{2,1,0:T(8,128)(2,1)S(1)} %get-tuple-element.32), channel_id=1, source_target_pairs={{0,1},{1,2},{2,3},{3,4},{4,5},{5,6},{6,7},{8,9},{9,10},{10,11},{11... | collective-permute-start | bytes 491528 | tf_op jit(solution)/shard_map/ppermute | solution.py:193
  182.1 7.5 %collective-permute-start.13 = (bf16[1,64,1280]{2,1,0:T(8,128)(2,1)S(1)}, bf16[1,64,1280]{2,1,0:T(8,128)(2,1)S(1)}, u32[]{:S(2)}, u32[]{:S(2)}) collective-permute-start(bf16[1,64,1280]{2,1,0:T(8,128)(2,1)S(1)} %get-tuple-element.33), channel_id=1, source_target_pairs={{1,0},{2,1},{3,2},{4,3},{5,4},{6,5},{7,6},{9,8},{10,9},{11,10},{12... | collective-permute-start | bytes 491528 | tf_op jit(solution)/shard_map/ppermute | solution.py:196
  189.6 0.6 copy.35
  190.1 0.2 pad.2
  190.4 0.2 copy.37
  190.6 0.4 copy-done.14
  191.1 8.9 %fusion.25 = f32[4,8,9,640]{3,1,2,0:T(8,128)S(1)} fusion(bf16[3,3,1280,640]{3,2,1,0:T(8,128)(2,1)} %param.26, bf16[6,1,7,2,1280]{4,2,3,0,1:T(8,128)(2,1)S(1)} %slice.110, bf16[6,1,8,9,1280]{4,2,3,0,1:T(8,128)(2,1)S(1)} %copy.37, pred[8,9]{0,1:T(8,128)(4,1)S(1)} %copy-done.14), kind=kOutput, calls=%fused_computation.39 | convolution fusion | flops 4250972160 | bytes 16803912 | tf_op jit(solution)/shard_map/conv_general_dilated | solution.py:199
  200.0 0.2 copy.38
  200.4 0.1 maximum_bitcast_fusion
  200.5 1.0 copy.40
  201.5 0.8 pad.clone
  202.4 0.1 slice.108
  202.5 1.3 fusion.18
  203.9 2.8 %fusion.28 = f32[1,16,9,640]{3,1,2,0:T(8,128)S(1)} fusion(bf16[3,3,1280,640]{3,2,1,0:T(8,128)(2,1)S(1)} %bitcast.102, bf16[3,2,8,11,1280]{4,1,3,2,0:T(2,128)(2,1)S(1)} %fusion.18, pred[16,9]{0,1:T(8,128)(4,1)S(1)} %copy-done.13), kind=kOutput, calls=%fused_computation.40 | convolution fusion | flops 2123458560 | bytes 16466064 | tf_op jit(solution)/shard_map/conv_general_dilated | solution.py:199
  206.6 0.4 copy.34
  207.0 0.1 slice_bitcast_fusion.2
  207.2 0.4 pad_maximum_fusion.2
  207.6 0.2 copy.39
  207.8 0.9 fusion.32
  208.7 0.6 copy-done.1
  (72 shorter events, 1.0 us)
Async XLA Ops:
  0.0 108.9 %copy-start = (bf16[1280,1280]{1,0:T(8,128)(2,1)S(1)}, bf16[1280,1280]{1,0:T(8,128)(2,1)}, u32[]{:S(2)}) copy-start(bf16[1280,1280]{1,0:T(8,128)(2,1)} %param.21) | copy-start | bytes 9830404
  0.0 2.4 %copy-start.4 = (bf16[384,1280]{1,0:T(8,128)(2,1)S(1)}, bf16[384,1280]{1,0:T(8,128)(2,1)}, u32[]{:S(2)}) copy-start(bf16[384,1280]{1,0:T(8,128)(2,1)} %param.17) | copy-start | bytes 2949124
  0.0 49.7 %copy-start.5 = (f32[6,2,2,32]{3,2,1,0:T(2,128)S(1)}, f32[6,2,2,32]{3,2,1,0:T(2,128)}, u32[]{:S(2)}) copy-start(f32[6,2,2,32]{3,2,1,0:T(2,128)} %param.18) | copy-start | bytes 9220
  2.4 93.2 %copy-start.6 = (f32[1280]{0:T(1024)S(1)}, f32[1280]{0:T(1024)}, u32[]{:S(2)}) copy-start(f32[1280]{0:T(1024)} %param.19) | copy-start | bytes 15364
  2.4 93.2 %copy-start.7 = (f32[1280]{0:T(1024)S(1)}, f32[1280]{0:T(1024)}, u32[]{:S(2)}) copy-start(f32[1280]{0:T(1024)} %param.20) | copy-start | bytes 15364
  3.5 46.1 %collective-permute-start.3 = (bf16[384,2560]{1,0:T(8,128)(2,1)}, bf16[384,2560]{1,0:T(8,128)(2,1)}, u32[]{:S(2)}, u32[]{:S(2)}) collective-permute-start(bf16[384,2560]{1,0:T(8,128)(2,1)} %constant_dynamic-update-slice_fusion), channel_id=1, source_target_pairs={{0,1},{1,2},{2,3},{3,0},{4,5},{5,6},{6,7},{7,4},{8,9},{9,10},{10,1... | collective-permute-start | bytes 5898248 | tf_op jit(solution)/shard_map/ppermute | solution.py:150
  5.1 46.1 %collective-permute-start.5 = (bf16[384,2560]{1,0:T(8,128)(2,1)}, bf16[384,2560]{1,0:T(8,128)(2,1)}, u32[]{:S(2)}, u32[]{:S(2)}) collective-permute-start(bf16[384,2560]{1,0:T(8,128)(2,1)} %constant_dynamic-update-slice_fusion), channel_id=1, source_target_pairs={{0,4},{1,5},{2,6},{3,7},{4,0},{5,1},{6,2},{7,3},{8,12},{9,13},{10,... | collective-permute-start | bytes 5898248 | tf_op jit(solution)/shard_map/ppermute | solution.py:152
  5.1 90.6 %collective-permute-start.4 = (bf16[384,2560]{1,0:T(8,128)(2,1)}, bf16[384,2560]{1,0:T(8,128)(2,1)}, u32[]{:S(2)}, u32[]{:S(2)}) collective-permute-start(bf16[384,2560]{1,0:T(8,128)(2,1)} %constant_dynamic-update-slice_fusion), channel_id=1, source_target_pairs={{0,3},{1,0},{2,1},{3,2},{4,7},{5,4},{6,5},{7,6},{8,11},{9,8},{10,9... | collective-permute-start | bytes 5898248 | tf_op jit(solution)/shard_map/ppermute | solution.py:151
  49.7 56.2 %collective-permute-start.8 = (bf16[384,2560]{1,0:T(8,128)(2,1)}, bf16[384,2560]{1,0:T(8,128)(2,1)}, u32[]{:S(2)}, u32[]{:S(2)}) collective-permute-start(bf16[384,2560]{1,0:T(8,128)(2,1)} %collective-permute-done.3.refs_3_.refs_4_), channel_id=1, source_target_pairs={{0,4},{1,5},{2,6},{3,7},{4,0},{5,1},{6,2},{7,3},{8,12},{9,13},{10,... | collective-permute-start | bytes 5898248 | tf_op jit(solution)/shard_map/ppermute | solution.py:155
  49.7 5.4 %collective-permute-start = (f32[2,2,32]{2,1,0:T(2,128)S(1)}, f32[2,2,32]{2,1,0:T(2,128)S(1)}, u32[]{:S(2)}, u32[]{:S(2)}) collective-permute-start(f32[2,2,32]{2,1,0:T(2,128)S(1)} %reduce_sum.54), channel_id=1, source_target_pairs={{0,1},{1,0},{2,3},{3,2},{4,5},{5,4},{6,7},{7,6},{8,9},{9,8},{10,11... | collective-permute-start | bytes 1544 | tf_op jit(solution)/shard_map/ppermute | solution.py:147
  51.2 61.1 %collective-permute-start.9 = (bf16[384,2560]{1,0:T(8,128)(2,1)}, bf16[384,2560]{1,0:T(8,128)(2,1)}, u32[]{:S(2)}, u32[]{:S(2)}) collective-permute-start(bf16[384,2560]{1,0:T(8,128)(2,1)} %collective-permute-done.5.refs_7_.refs_8_), channel_id=1, source_target_pairs={{0,3},{1,0},{2,1},{3,2},{4,7},{5,4},{6,5},{7,6},{8,11},{9,8},{10,9... | collective-permute-start | bytes 5898248 | tf_op jit(solution)/shard_map/ppermute | solution.py:156
  55.1 5.2 %collective-permute-start.1 = (f32[2,2,32]{2,1,0:T(2,128)S(1)}, f32[2,2,32]{2,1,0:T(2,128)S(1)}, u32[]{:S(2)}, u32[]{:S(2)}) collective-permute-start(f32[2,2,32]{2,1,0:T(2,128)S(1)} %add.74), channel_id=1, source_target_pairs={{0,2},{1,3},{2,0},{3,1},{4,6},{5,7},{6,4},{7,5},{8,10},{9,11},{10,... | collective-permute-start | bytes 1544 | tf_op jit(solution)/shard_map/ppermute | solution.py:147
  60.3 35.0 %collective-permute-start.2 = (f32[2,2,32]{2,1,0:T(2,128)S(1)}, f32[2,2,32]{2,1,0:T(2,128)S(1)}, u32[]{:S(2)}, u32[]{:S(2)}) collective-permute-start(f32[2,2,32]{2,1,0:T(2,128)S(1)} %add.75), channel_id=1, source_target_pairs={{0,4},{1,5},{2,6},{3,7},{4,0},{5,1},{6,2},{7,3},{8,12},{9,13},{10,... | collective-permute-start | bytes 1544 | tf_op jit(solution)/shard_map/ppermute | solution.py:148
  97.0 11.9 %copy-start.2 = (bf16[384,1280]{1,0:T(8,128)(2,1)S(1)}, bf16[384,1280]{1,0:T(8,128)(2,1)}, u32[]{:S(2)}) copy-start(bf16[384,1280]{1,0:T(8,128)(2,1)} %param.15) | copy-start | bytes 2949124
  97.0 43.6 %collective-permute-start.7 = (bf16[192,2560]{1,0:T(8,128)(2,1)S(1)}, bf16[192,2560]{1,0:T(8,128)(2,1)S(1)}, u32[]{:S(2)}, u32[]{:S(2)}) collective-permute-start(bf16[192,2560]{1,0:T(8,128)(2,1)S(1)} %slice.99), channel_id=1, source_target_pairs={{0,3},{1,0},{2,1},{3,2},{4,7},{5,4},{6,5},{7,6},{8,11},{9,8},{10,9... | collective-permute-start | bytes 2949128 | tf_op jit(solution)/shard_map/ppermute | solution.py:154
  105.8 34.8 %collective-permute-start.6 = (bf16[192,2560]{1,0:T(8,128)(2,1)S(1)}, bf16[192,2560]{1,0:T(8,128)(2,1)S(1)}, u32[]{:S(2)}, u32[]{:S(2)}) collective-permute-start(bf16[192,2560]{1,0:T(8,128)(2,1)S(1)} %slice.98), channel_id=1, source_target_pairs={{0,1},{1,2},{2,3},{3,0},{4,5},{5,6},{6,7},{7,4},{8,9},{9,10},{10,1... | collective-permute-start | bytes 2949128 | tf_op jit(solution)/shard_map/ppermute | solution.py:153
  107.3 54.3 %collective-permute-start.10 = (bf16[256,2560]{1,0:T(8,128)(2,1)S(1)}, bf16[256,2560]{1,0:T(8,128)(2,1)S(1)}, u32[]{:S(2)}, u32[]{:S(2)}) collective-permute-start(bf16[256,2560]{1,0:T(8,128)(2,1)S(1)} %slice.100), channel_id=1, source_target_pairs={{0,1},{1,2},{2,3},{3,0},{4,5},{5,6},{6,7},{7,4},{8,9},{9,10},{10,1... | collective-permute-start | bytes 3932168 | tf_op jit(solution)/shard_map/ppermute | solution.py:157
  108.9 1.9 copy-start.11
  110.8 4.6 %copy-start.12 = (bf16[1280,1280]{1,0:T(8,128)(2,1)S(1)}, bf16[1280,1280]{1,0:T(8,128)(2,1)}, u32[]{:S(2)}) copy-start(bf16[1280,1280]{1,0:T(8,128)(2,1)} %param.23) | copy-start | bytes 9830404
  113.4 48.2 %collective-permute-start.11 = (bf16[128,2560]{1,0:T(8,128)(2,1)S(1)}, bf16[128,2560]{1,0:T(8,128)(2,1)S(1)}, u32[]{:S(2)}, u32[]{:S(2)}) collective-permute-start(bf16[128,2560]{1,0:T(8,128)(2,1)S(1)} %slice.101), channel_id=1, source_target_pairs={{0,3},{1,0},{2,1},{3,2},{4,7},{5,4},{6,5},{7,6},{8,11},{9,8},{10,9... | collective-permute-start | bytes 1966088 | tf_op jit(solution)/shard_map/ppermute | solution.py:158
  163.0 11.6 %copy-start.3 = (f32[384,1280]{1,0:T(8,128)S(1)}, f32[384,1280]{1,0:T(8,128)}, u32[]{:S(2)}) copy-start(f32[384,1280]{1,0:T(8,128)} %get-tuple-element.20) | copy-start | bytes 5898244
  174.6 4.6 %copy-start.8 = (f32[1280]{0:T(1024)S(1)}, f32[1280]{0:T(1024)}, u32[]{:S(2)}) copy-start(f32[1280]{0:T(1024)} %param.24) | copy-start | bytes 15364
  174.6 4.6 %copy-start.9 = (f32[1280]{0:T(1024)S(1)}, f32[1280]{0:T(1024)}, u32[]{:S(2)}) copy-start(f32[1280]{0:T(1024)} %param.25) | copy-start | bytes 15364
  179.9 20.4 %collective-permute-start.12 = (bf16[1,64,1280]{2,1,0:T(8,128)(2,1)S(1)}, bf16[1,64,1280]{2,1,0:T(8,128)(2,1)S(1)}, u32[]{:S(2)}, u32[]{:S(2)}) collective-permute-start(bf16[1,64,1280]{2,1,0:T(8,128)(2,1)S(1)} %get-tuple-element.32), channel_id=1, source_target_pairs={{0,1},{1,2},{2,3},{3,4},{4,5},{5,6},{6,7},{8,9},{9,10},{10,11},{11... | collective-permute-start | bytes 491528 | tf_op jit(solution)/shard_map/ppermute | solution.py:193
  182.1 18.3 %collective-permute-start.13 = (bf16[1,64,1280]{2,1,0:T(8,128)(2,1)S(1)}, bf16[1,64,1280]{2,1,0:T(8,128)(2,1)S(1)}, u32[]{:S(2)}, u32[]{:S(2)}) collective-permute-start(bf16[1,64,1280]{2,1,0:T(8,128)(2,1)S(1)} %get-tuple-element.33), channel_id=1, source_target_pairs={{1,0},{2,1},{3,2},{4,3},{5,4},{6,5},{7,6},{9,8},{10,9},{11,10},{12... | collective-permute-start | bytes 491528 | tf_op jit(solution)/shard_map/ppermute | solution.py:196
  190.4 0.7 copy-start.14
  191.1 12.8 %slice-start = ((s8[14745600]{0:T(1024)(128)(4,1)}), s8[4194304]{0:T(1024)(128)(4,1)S(1)}, s32[]{:S(2)}) async-start(s8[14745600]{0:T(1024)(128)(4,1)} %bitcast.101), calls=%async_computation | async-start | bytes 8388608
  191.1 12.8 %slice-start.1 = ((s8[14745600]{0:T(1024)(128)(4,1)}), s8[4194304]{0:T(1024)(128)(4,1)S(1)}, s32[]{:S(2)}) async-start(s8[14745600]{0:T(1024)(128)(4,1)} %bitcast.101), calls=%async_computation.1 | async-start | bytes 8388608
  191.1 12.8 %slice-start.2 = ((s8[14745600]{0:T(1024)(128)(4,1)}), s8[4194304]{0:T(1024)(128)(4,1)S(1)}, s32[]{:S(2)}) async-start(s8[14745600]{0:T(1024)(128)(4,1)} %bitcast.101), calls=%async_computation.2 | async-start | bytes 8388608
  200.2 3.6 %slice-start.3 = ((s8[14745600]{0:T(1024)(128)(4,1)}), s8[2162688]{0:T(1024)(128)(4,1)S(1)}, s32[]{:S(2)}) async-start(s8[14745600]{0:T(1024)(128)(4,1)} %bitcast.101), calls=%async_computation.3 | async-start | bytes 4325376
  202.4 1.5 copy-start.13
  207.1 0.7 copy-start.10
  207.1 2.1 %copy-start.1 = (bf16[1280,1280]{1,0:T(8,128)(2,1)S(1)}, bf16[1280,1280]{1,0:T(8,128)(2,1)}, u32[]{:S(2)}) copy-start(bf16[1280,1280]{1,0:T(8,128)(2,1)} %param.21) | copy-start | bytes 9830404
